TPU v7x, 256 devices: a whole 4x4x8 slice. The times are simulated.
256 devices in a mesh: dp: 32 (over x, y, core), expert: 8 (over z).
Axes of the slice: x: 4, y: 4, z: 8, core: 2. Of those that a mesh axis runs over, the one named last changes fastest.
Arguments:
- tokens: bfloat16 [16384, 1024], P('dp'), may hold values from -6 to 6
- grad_out: bfloat16 [16384, 1024], P('dp'), may hold values from -3 to 3
- region_ids: int32 [16384], P('dp'), may hold values from 0 to 63, as said below
- slot_ids: int32 [16384], P('dp'), may hold values from 0 to 31, as said below
- weight_in: bfloat16 [64, 1024, 4096], P('dp', None, 'expert'), may hold values from -0.25 to 0.25
- weight_out: bfloat16 [64, 4096, 1024], P('dp', 'expert'), may hold values from -0.09375 to 0.09375
Outputs:
- grad_tokens: bfloat16 [16384, 1024], P('dp', 'expert')
- grad_weight_in: bfloat16 [64, 1024, 4096], P('dp', None, 'expert')
- grad_weight_out: bfloat16 [64, 4096, 1024], P('dp', 'expert')
Inputs may be any that keep to these rules, and one draw needn't show every extreme that they name: `region_ids`: among the rows of one index of dp, no expert is named more than 32 times, and one expert drawn from the seed is named exactly 32 times on every index of dp. `slot_ids`: among the rows of one index of dp, rows that name the same expert have different slots.
All inputs are finite; a program needn't handle non-finite values.
Results may differ from a plain program's by a relative error of at most 0.017.
Values may be sent and summed in bfloat16 or wider, within the bound.
No kernel may reach another device: no remote copies, remote signals or barrier semaphores. Data moves between devices by JAX's collectives and lax.ppermute only.
A program may use at most 128 MiB of HBM per device.

v0:
```python
import jax
import jax.numpy as jnp
from jax import lax
from jax.sharding import PartitionSpec as P


def on_device(tokens, grad_out, region_ids, slot_ids, weight_in, weight_out):
    owners = lax.axis_size("dp")
    local_count = weight_in.shape[0]
    model_width = tokens.shape[1]
    tok_rows = tokens.shape[0]
    experts_all = local_count * owners
    capacity = 4 * tok_rows // experts_all
    where_to = region_ids * capacity + slot_ids
    send_in = (
        jnp.zeros((experts_all * capacity, model_width), jnp.bfloat16).at[where_to].set(tokens)
    )
    send_grad = (
        jnp.zeros((experts_all * capacity, model_width), jnp.bfloat16).at[where_to].set(grad_out)
    )
    send_in = send_in.reshape(owners, local_count, capacity, model_width)
    send_grad = send_grad.reshape(owners, local_count, capacity, model_width)
    got_in, got_grad = (
        lax.all_to_all(send_in, "dp", split_axis=0, concat_axis=2, tiled=True),
        lax.all_to_all(send_grad, "dp", split_axis=0, concat_axis=2, tiled=True),
    )
    routed_in = got_in[0]
    routed_grad = got_grad[0]
    pre_act = jnp.einsum("erd,edf->erf", routed_in, weight_in, preferred_element_type=jnp.float32)
    gate_sig = jax.nn.sigmoid(pre_act)
    hidden_act = (pre_act * gate_sig).astype(jnp.bfloat16)
    back_grad = jnp.einsum(
        "erd,efd->erf", routed_grad, weight_out, preferred_element_type=jnp.float32
    )
    pre_grad = (back_grad * gate_sig * (1.0 + pre_act * (1.0 - gate_sig))).astype(jnp.bfloat16)
    grad_wout = jnp.einsum(
        "erf,erd->efd", hidden_act, routed_grad, preferred_element_type=jnp.float32
    ).astype(jnp.bfloat16)
    grad_win = jnp.einsum(
        "erd,erf->edf", routed_in, pre_grad, preferred_element_type=jnp.float32
    ).astype(jnp.bfloat16)
    partial_value = jnp.einsum(
        "erf,edf->erd", pre_grad, weight_in, preferred_element_type=jnp.float32
    )
    summed = lax.psum_scatter(
        partial_value.astype(jnp.bfloat16), "expert", scatter_dimension=2, tiled=True
    )
    back_rows = lax.all_to_all(summed[None], "dp", split_axis=2, concat_axis=0, tiled=True)
    grad_tokens = back_rows.reshape(experts_all * capacity, summed.shape[2])[where_to]
    return (grad_tokens, grad_win, grad_wout)


def solution(mesh):
    in_specs = (
        P("dp", None),
        P("dp", None),
        P("dp"),
        P("dp"),
        P("dp", None, "expert"),
        P("dp", "expert", None),
    )
    out_specs = (P("dp", "expert"), P("dp", None, "expert"), P("dp", "expert", None))
    return jax.shard_map(
        on_device, mesh=mesh, in_specs=in_specs, out_specs=out_specs, check_vma=False
    )
```

profile of v0, /device:TPU:1, one launch (start us, length us, event | category | flops | bytes accessed | tf_op | source)
XLA Modules:
  0.0 254.9 jit_solution(1786655254711929388)
XLA Ops:
  7.2 0.9 compare_select_fusion
  8.0 5.9 %scatter_custom_fusion.1 = bf16[2048,1024]{1,0:T(8,128)(2,1)} fusion(s32[512]{0:T(512)S(1)} %compare_select_fusion, bf16[512,1024]{1,0:T(8,128)(2,1)} %param.6, bf16[]{:T(256)} %constant.0.clone.1), kind=kCustom, calls=%fused_computation.9 | custom fusion | bytes 4194816 | tf_op jit(solution)/shard_map/scatter | solution.py:16
  13.9 8.6 %all-to-all-start.1 = ((bf16[32,2,32,1024]{3,2,1,0:T(8,128)(2,1)}), bf16[32,2,32,1024]{3,2,1,0:T(8,128)(2,1)}, u32[]{:S(2)}, u32[]{:S(2)}) async-start(bf16[32,2,32,1024]{3,2,1,0:T(8,128)(2,1)} %bitcast.32), calls=%async_computation.1 | async-start | bytes 8388608 | tf_op jit(solution)/shard_map/all_to_all | solution.py:24
  22.6 5.9 %scatter_custom_fusion = bf16[2048,1024]{1,0:T(8,128)(2,1)} fusion(s32[512]{0:T(512)S(1)} %compare_select_fusion, bf16[512,1024]{1,0:T(8,128)(2,1)} %param.7, bf16[]{:T(256)} %constant.0.clone.1), kind=kCustom, calls=%fused_computation.11 | custom fusion | bytes 4194816 | tf_op jit(solution)/shard_map/scatter | solution.py:19
  28.5 46.2 %all-to-all-done.1 = bf16[32,2,32,1024]{3,2,1,0:T(8,128)(2,1)} async-done(((bf16[32,2,32,1024]{3,2,1,0:T(8,128)(2,1)}), bf16[32,2,32,1024]{3,2,1,0:T(8,128)(2,1)}, u32[]{:S(2)}, u32[]{:S(2)}) %all-to-all-start.1) | async-done | bytes 4194336 | tf_op jit(solution)/shard_map/all_to_all | solution.py:24
  74.7 7.1 %all-to-all-start = ((bf16[32,2,32,1024]{3,2,1,0:T(8,128)(2,1)}), bf16[32,2,32,1024]{3,2,1,0:T(8,128)(2,1)}, u32[]{:S(2)}, u32[]{:S(2)}) async-start(bf16[32,2,32,1024]{3,2,1,0:T(8,128)(2,1)} %bitcast.30), calls=%async_computation | async-start | bytes 8388608 | tf_op jit(solution)/shard_map/all_to_all | solution.py:25
  82.0 4.9 %copy.18 = bf16[1,2,32,32,1024]{4,3,2,1,0:T(8,128)(2,1)} copy(bf16[1,2,32,32,1024]{4,3,1,2,0:T(8,128)(2,1)} %bitcast.6) | data formatting | bytes 8388608 | tf_op jit(solution)/shard_map/all_to_all | solution.py:24
  86.9 47.0 %all-to-all-done = bf16[32,2,32,1024]{3,2,1,0:T(8,128)(2,1)} async-done(((bf16[32,2,32,1024]{3,2,1,0:T(8,128)(2,1)}), bf16[32,2,32,1024]{3,2,1,0:T(8,128)(2,1)}, u32[]{:S(2)}, u32[]{:S(2)}) %all-to-all-start) | async-done | bytes 4194336 | tf_op jit(solution)/shard_map/all_to_all | solution.py:25
  133.9 2.8 %copy.17 = bf16[1,2,32,32,1024]{4,3,2,1,0:T(8,128)(2,1)S(1)} copy(bf16[1,2,32,32,1024]{4,3,1,2,0:T(8,128)(2,1)} %bitcast.2) | data formatting | bytes 8388608 | tf_op jit(solution)/shard_map/all_to_all | solution.py:25
  136.7 0.6 copy-done.1
  137.3 2.3 fusion.8
  139.8 3.5 %multiply_convert_fusion.1 = bf16[2,1024,512]{2,1,0:T(8,128)(2,1)S(1)} fusion(f32[2,1024,512]{2,1,0:T(8,128)S(1)} %fusion.8, bf16[2,1024,1024]{2,1,0:T(8,128)(2,1)S(1)} %bitcast.37, bf16[2,512,1024]{2,1,0:T(8,128)(2,1)S(1)} %copy-done.3), kind=kOutput, calls=%fused_computation.4 | convolution fusion | flops 2156920832 | bytes 12582912 | tf_op jit(solution)/shard_map/erd,efd->erf/dot_general | solution.py:32
  143.3 1.3 copy-done.5
  144.6 4.3 %convolution_convert_fusion = bf16[2,1024,1024]{2,1,0:T(8,128)(2,1)} fusion(bf16[2,1024,512]{2,1,0:T(8,128)(2,1)S(1)} %multiply_convert_fusion.1, bf16[2,1024,512]{2,1,0:T(8,128)(2,1)S(1)} %copy-done), kind=kOutput, calls=%fused_computation.6 | convolution fusion | flops 2149580800 | bytes 8388608 | tf_op jit(solution)/shard_map/erf,edf->erd/dot_general | solution.py:42
  149.0 11.3 %copy.25 = bf16[2,1024,1024]{1,0,2:T(2,128)(2,1)} copy(bf16[2,1024,1024]{2,1,0:T(8,128)(2,1)} %convolution_convert_fusion) | data formatting | bytes 8388608
  160.3 5.5 %copy.27 = bf16[128,8,2,1024]{3,1,2,0:T(8,128)(2,1)} copy(bf16[128,8,2,1024]{3,2,1,0:T(2,128)(2,1)} %bitcast.33) | data formatting | bytes 8388608
  165.8 7.2 %fusion.6 = bf16[2,512,1024]{2,1,0:T(8,128)(2,1)} fusion(bf16[2,1024,1024]{2,1,0:T(8,128)(2,1)} %bitcast.38, f32[2,1024,512]{2,1,0:T(8,128)} %copy-done.4), kind=kOutput, calls=%fused_computation.13 | convolution fusion | flops 2153775104 | bytes 10485760 | tf_op jit(solution)/shard_map/erf,erd->efd/dot_general | solution.py:36
  173.0 50.4 %reduce-scatter.4.cloned.1.call-done = bf16[128,2048]{1,0:T(8,128)(2,1)} async-done(((bf16[1024,2048]{1,0:T(8,128)(2,1)}), bf16[128,2048]{1,0:T(8,128)(2,1)}) %reduce-scatter.4.cloned.1.call-update) | async-done | bytes 524304
  223.5 1.4 reshape.49
  225.5 1.4 copy.19
  226.8 7.6 %all-to-all-start.2 = ((bf16[1,2,1024,128]{3,1,0,2:T(2,128)(2,1)}), bf16[1,2,1024,128]{3,1,0,2:T(2,128)(2,1)S(1)}, u32[]{:S(2)}, u32[]{:S(2)}) async-start(bf16[1,2,1024,128]{3,1,0,2:T(2,128)(2,1)} %copy.19), calls=%async_computation.2 | async-start | bytes 1048576 | tf_op jit(solution)/shard_map/all_to_all | solution.py:48
  234.4 6.6 %convolution_convert_fusion.1 = bf16[2,1024,512]{2,1,0:T(8,128)(2,1)} fusion(bf16[2,1024,1024]{2,1,0:T(8,128)(2,1)} %bitcast.35, bf16[2,1024,512]{2,1,0:T(8,128)(2,1)} %copy-done.5), kind=kOutput, calls=%fused_computation.14 | convolution fusion | flops 2148532224 | bytes 8388608 | tf_op jit(solution)/shard_map/erd,erf->edf/dot_general | solution.py:39
  241.0 5.0 %all-to-all-done.2 = bf16[1,2,1024,128]{3,1,0,2:T(2,128)(2,1)S(1)} async-done(((bf16[1,2,1024,128]{3,1,0,2:T(2,128)(2,1)}), bf16[1,2,1024,128]{3,1,0,2:T(2,128)(2,1)S(1)}, u32[]{:S(2)}, u32[]{:S(2)}) %all-to-all-start.2) | async-done | bytes 524320 | tf_op jit(solution)/shard_map/all_to_all | solution.py:48
  246.1 1.9 gather_fusion
  (15 shorter events, 1.0 us)
Async XLA Ops:
  7.2 129.5 %copy-start = (bf16[2,1024,512]{2,1,0:T(8,128)(2,1)S(1)}, bf16[2,1024,512]{2,1,0:T(8,128)(2,1)}, u32[]{:S(2)}) copy-start(bf16[2,1024,512]{2,1,0:T(8,128)(2,1)} %param.10) | copy-start | bytes 6291460
  13.9 60.8 %all-to-all-start.1 = ((bf16[32,2,32,1024]{3,2,1,0:T(8,128)(2,1)}), bf16[32,2,32,1024]{3,2,1,0:T(8,128)(2,1)}, u32[]{:S(2)}, u32[]{:S(2)}) async-start(bf16[32,2,32,1024]{3,2,1,0:T(8,128)(2,1)} %bitcast.32), calls=%async_computation.1 | async-start | bytes 8388608 | tf_op jit(solution)/shard_map/all_to_all | solution.py:24
  74.7 59.2 %all-to-all-start = ((bf16[32,2,32,1024]{3,2,1,0:T(8,128)(2,1)}), bf16[32,2,32,1024]{3,2,1,0:T(8,128)(2,1)}, u32[]{:S(2)}, u32[]{:S(2)}) async-start(bf16[32,2,32,1024]{3,2,1,0:T(8,128)(2,1)} %bitcast.30), calls=%async_computation | async-start | bytes 8388608 | tf_op jit(solution)/shard_map/all_to_all | solution.py:25
  81.8 141.7 %reduce-scatter.4.cloned.1.call-start = ((), (), s32[]{:S(2)}) async-start(), calls=%async_computation.4 | async-start | bytes 4718592
  133.9 3.4 %copy-start.1 = (bf16[1,2,32,32,1024]{4,3,2,1,0:T(8,128)(2,1)S(1)}, bf16[1,2,32,32,1024]{4,3,2,1,0:T(8,128)(2,1)}, u32[]{:S(2)}) copy-start(bf16[1,2,32,32,1024]{4,3,2,1,0:T(8,128)(2,1)} %copy.18) | copy-start | bytes 12582916
  136.7 3.0 %copy-start.2 = (bf16[1,2,32,32,1024]{4,3,2,1,0:T(8,128)(2,1)}, bf16[1,2,32,32,1024]{4,3,2,1,0:T(8,128)(2,1)S(1)}, u32[]{:S(2)}) copy-start(bf16[1,2,32,32,1024]{4,3,2,1,0:T(8,128)(2,1)S(1)} %copy.17) | copy-start | bytes 12582916
  137.3 2.4 copy-start.3
  139.7 3.6 %copy-start.4 = (f32[2,1024,512]{2,1,0:T(8,128)}, f32[2,1024,512]{2,1,0:T(8,128)S(1)}, u32[]{:S(2)}) copy-start(f32[2,1024,512]{2,1,0:T(8,128)S(1)} %fusion.8) | copy-start | bytes 12582916
  143.3 1.3 copy-start.5
  226.8 19.2 %all-to-all-start.2 = ((bf16[1,2,1024,128]{3,1,0,2:T(2,128)(2,1)}), bf16[1,2,1024,128]{3,1,0,2:T(2,128)(2,1)S(1)}, u32[]{:S(2)}, u32[]{:S(2)}) async-start(bf16[1,2,1024,128]{3,1,0,2:T(2,128)(2,1)} %copy.19), calls=%async_computation.2 | async-start | bytes 1048576 | tf_op jit(solution)/shard_map/all_to_all | solution.py:48
Sparse Core Ops, SparseCore 0:
  166.0 57.4 reduce-scatter.3
where the time goes:
time: 256 us; the launch traced here: 255 us
  waiting for transfers between devices  149 us (58%)
  local copies, waits for them, and re-layouts  43.7 us (17%)
  matrix products  23.9 us (9%)
  starting transfers between devices  23.5 us (9%)
  between operations  14.2 us (6%)
    unnamed x2, waiting for transfers between devices  50.5 us
    all_to_all x1, waiting for transfers between devices, on_device(): lax.all_to_all(send_grad, 'dp', split_axis=0, concat_axis=2, tiled=True)  47 us
    all_to_all x1, waiting for transfers between devices, on_device(): lax.all_to_all(send_in, 'dp', split_axis=0, concat_axis=2, tiled=True)  46.2 us
    unnamed x16, local copies, waits for them, and re-layouts  20.9 us
    scatter x2, local copies, waits for them, and re-layouts, on_device(): jnp.zeros((experts_all * capacity, model_width), jnp.bfloat16).at[where_to]  11.8 us
    all_to_all x1, starting transfers between devices, on_device(): lax.all_to_all(send_in, 'dp', split_axis=0, concat_axis=2, tiled=True)  8.63 us
    all_to_all x1, starting transfers between devices, on_device(): lax.all_to_all(summed[None], 'dp', split_axis=2, concat_axis=0, tiled=True)  7.59 us
    dot_general x1, matrix products, on_device(): jnp.einsum('erf,erd->efd', hidden_act, routed_grad, preferred_element_typ...  7.19 us
  transfers between devices with their start and end apart: 4, of which 4 were waited for; matrix products, arithmetic and copies ran while one was open for 10% of the time, Pallas kernels for 0%

commit v1 on v0

v1 whole, which is shorter than its diff:
```python
import jax
import jax.numpy as jnp
from jax import lax
from jax.sharding import PartitionSpec as P

CHUNKS = 4


def on_device(tokens, grad_out, region_ids, slot_ids, weight_in, weight_out):
    owners = lax.axis_size("dp")
    local_count = weight_in.shape[0]
    model_width = tokens.shape[1]
    tok_rows = tokens.shape[0]
    experts_all = local_count * owners
    capacity = 4 * tok_rows // experts_all
    step = capacity // CHUNKS
    where_to = region_ids * capacity + slot_ids
    both = jnp.concatenate([tokens, grad_out], axis=1)

    grad_win = None
    grad_wout = None
    back_parts = []
    for chunk in range(CHUNKS):
        rows = jnp.arange(experts_all * step, dtype=jnp.int32)
        expert_of = rows // step
        slot_of = rows % step + chunk * step
        pick = (
            (region_ids[None, :] == expert_of[:, None]) & (slot_ids[None, :] == slot_of[:, None])
        ).astype(jnp.bfloat16)
        sent = jnp.dot(pick, both, preferred_element_type=jnp.float32).astype(jnp.bfloat16)
        sent = sent.reshape(owners, local_count, step, 2, model_width)
        sent = jnp.moveaxis(sent, 3, 1).reshape(owners, 2 * local_count, step, model_width)
        got = lax.all_to_all(sent, "dp", split_axis=0, concat_axis=2, tiled=True)[0]
        routed_in = got[:local_count]
        routed_grad = got[local_count:]
        pre_act = jnp.einsum(
            "erd,edf->erf", routed_in, weight_in, preferred_element_type=jnp.float32
        )
        gate_sig = jax.nn.sigmoid(pre_act)
        hidden_act = (pre_act * gate_sig).astype(jnp.bfloat16)
        back_grad = jnp.einsum(
            "erd,efd->erf", routed_grad, weight_out, preferred_element_type=jnp.float32
        )
        pre_grad = (back_grad * gate_sig * (1.0 + pre_act * (1.0 - gate_sig))).astype(
            jnp.bfloat16
        )
        part_wout = jnp.einsum(
            "erf,erd->efd", hidden_act, routed_grad, preferred_element_type=jnp.float32
        )
        part_win = jnp.einsum(
            "erd,erf->edf", routed_in, pre_grad, preferred_element_type=jnp.float32
        )
        grad_wout = part_wout if grad_wout is None else grad_wout + part_wout
        grad_win = part_win if grad_win is None else grad_win + part_win
        partial_value = jnp.einsum(
            "erf,edf->erd", pre_grad, weight_in, preferred_element_type=jnp.float32
        )
        summed = lax.psum_scatter(
            partial_value.astype(jnp.bfloat16), "expert", scatter_dimension=2, tiled=True
        )
        back_parts.append(
            lax.all_to_all(summed[None], "dp", split_axis=2, concat_axis=0, tiled=True)
        )
    back_rows = jnp.concatenate(back_parts, axis=2)
    grad_tokens = back_rows.reshape(experts_all * capacity, back_rows.shape[3])[where_to]
    return (grad_tokens, grad_win.astype(jnp.bfloat16), grad_wout.astype(jnp.bfloat16))


def solution(mesh):
    in_specs = (
        P("dp", None),
        P("dp", None),
        P("dp"),
        P("dp"),
        P("dp", None, "expert"),
        P("dp", "expert", None),
    )
    out_specs = (P("dp", "expert"), P("dp", None, "expert"), P("dp", "expert", None))
    return jax.shard_map(
        on_device, mesh=mesh, in_specs=in_specs, out_specs=out_specs, check_vma=False
    )
```

time: 256 us -> 260 us (1.016)
  waiting for transfers between devices: 149 us -> 81.2 us
  starting transfers between devices: 23.5 us -> 52.7 us
  matrix products: 23.9 us -> 51.4 us
  local copies, waits for them, and re-layouts: 43.7 us -> 58.3 us
    unnamed x2 -> x8, waiting for transfers between devices: 50.5 us -> 11.4 us
    all_to_all x2 -> x4, waiting for transfers between devices: 93.2 us -> 65.5 us  [on_device(): got = lax.all_to_all(sent, 'dp', split_axis=0, concat_axis=2, tiled=True)[0]]
    all_to_all x1 -> x4, starting transfers between devices: 7.59 us -> 27.9 us  [on_device(): lax.all_to_all(summed[None], 'dp', split_axis=2, concat_axis=0, tiled=True)]
    unnamed x16 -> x87, local copies, waits for them, and re-layouts: 20.9 us -> 38.4 us
    dot_general x1 -> x4, matrix products: 6.57 us -> 19.3 us  [on_device(): jnp.einsum('erd,erf->edf', routed_in, pre_grad, preferred_element_type=jn...]
    scatter x2 -> x0, local copies, waits for them, and re-layouts: 11.8 us -> none  [on_device(): jnp.zeros((experts_all * capacity, model_width), jnp.bfloat16).at[where_to]]
    dot_general x0 -> x4, matrix products: none -> 10 us  [on_device(): jnp.dot(pick, both, preferred_element_type=jnp.float32).astype(jnp.bfloat16)]
    all_to_all x2 -> x4, starting transfers between devices: 15.7 us -> 24.2 us  [on_device(): got = lax.all_to_all(sent, 'dp', split_axis=0, concat_axis=2, tiled=True)[0]]
  transfers between devices with their start and end apart: 4 -> 12, of which waited for: 4 -> 8; matrix products, arithmetic and copies ran while one was open for 10% -> 35% of each run, Pallas kernels for 0% -> 0%
where the time goes in v1:
time: 260 us; the launch traced here: 258 us
  waiting for transfers between devices  81.2 us (31%)
  local copies, waits for them, and re-layouts  58.3 us (22%)
  starting transfers between devices  52.7 us (20%)
  matrix products  51.4 us (20%)
  between operations  14.4 us (6%)
    all_to_all x4, waiting for transfers between devices, on_device(): got = lax.all_to_all(sent, 'dp', split_axis=0, concat_axis=2, tiled=True)[0]  65.5 us
    unnamed x87, local copies, waits for them, and re-layouts  38.4 us
    all_to_all x4, starting transfers between devices, on_device(): lax.all_to_all(summed[None], 'dp', split_axis=2, concat_axis=0, tiled=True)  27.9 us
    all_to_all x4, starting transfers between devices, on_device(): got = lax.all_to_all(sent, 'dp', split_axis=0, concat_axis=2, tiled=True)[0]  24.2 us
    dot_general x4, matrix products, on_device(): jnp.einsum('erd,erf->edf', routed_in, pre_grad, preferred_element_type=jn...  19.3 us
    dot_general x4, matrix products, on_device(): jnp.einsum('erf,erd->efd', hidden_act, routed_grad, preferred_element_typ...  12.6 us
    unnamed x8, waiting for transfers between devices  11.4 us
    dot_general x4, matrix products, on_device(): jnp.dot(pick, both, preferred_element_type=jnp.float32).astype(jnp.bfloat16)  10 us
  transfers between devices with their start and end apart: 12, of which 8 were waited for; matrix products, arithmetic and copies ran while one was open for 35% of the time, Pallas kernels for 0%

profile of v1, /device:TPU:1, one launch (start us, length us, event | category | flops | bytes accessed | tf_op | source)
XLA Modules:
  0.0 258.1 jit_solution(6683102804561061375)
XLA Ops:
  11.8 8.6 %all-to-all-start.6 = ((bf16[32,4,8,1024]{3,2,1,0:T(8,128)(2,1)}), bf16[32,4,8,1024]{3,2,1,0:T(8,128)(2,1)}, u32[]{:S(2)}, u32[]{:S(2)}) async-start(bf16[32,4,8,1024]{3,2,1,0:T(8,128)(2,1)} %bitcast.140), calls=%async_computation.6 | async-start | bytes 4194304 | tf_op jit(solution)/shard_map/all_to_all | solution.py:33
  20.5 2.9 %convolution_convert_fusion.1 = bf16[512,2048]{1,0:T(8,128)(2,1)S(1)} fusion(bf16[512,2048]{1,0:T(8,128)(2,1)} %copy-done.23, s32[512]{0:T(512)S(1)} %copy-done.24, s32[512]{0:T(512)S(1)} %copy-done.25, s32[512]{0:T(512)S(1)} %broadcast_add_fusion.1, s32[512]{0:T(512)S(1)} %get-tuple-element.11), kind=kOutput, calls=%fused_computation.4 | convolution fusion | flops 1075576832 | bytes 4202496 | tf_op jit(solution)/shard_map/dot_general | solution.py:30
  24.9 24.0 %all-to-all-done.6 = bf16[32,4,8,1024]{3,2,1,0:T(8,128)(2,1)} async-done(((bf16[32,4,8,1024]{3,2,1,0:T(8,128)(2,1)}), bf16[32,4,8,1024]{3,2,1,0:T(8,128)(2,1)}, u32[]{:S(2)}, u32[]{:S(2)}) %all-to-all-start.6) | async-done | bytes 2097184 | tf_op jit(solution)/shard_map/all_to_all | solution.py:33
  48.8 5.2 %all-to-all-start.4 = ((bf16[32,4,8,1024]{3,2,1,0:T(8,128)(2,1)}), bf16[32,4,8,1024]{3,2,1,0:T(8,128)(2,1)}, u32[]{:S(2)}, u32[]{:S(2)}) async-start(bf16[32,4,8,1024]{3,2,1,0:T(8,128)(2,1)} %bitcast.138), calls=%async_computation.4 | async-start | bytes 4194304 | tf_op jit(solution)/shard_map/all_to_all | solution.py:33
  65.5 2.9 %convolution_convert_fusion.2 = bf16[512,2048]{1,0:T(8,128)(2,1)S(1)} fusion(bf16[512,2048]{1,0:T(8,128)(2,1)} %copy-done.23, s32[512]{0:T(512)S(1)} %copy-done.24, s32[512]{0:T(512)S(1)} %copy-done.25, s32[512]{0:T(512)S(1)} %broadcast_add_fusion.2, s32[512]{0:T(512)S(1)} %get-tuple-element.11), kind=kOutput, calls=%fused_computation.5 | convolution fusion | flops 1075576832 | bytes 4202496 | tf_op jit(solution)/shard_map/dot_general | solution.py:30
  69.9 12.6 %all-to-all-done.4 = bf16[32,4,8,1024]{3,2,1,0:T(8,128)(2,1)} async-done(((bf16[32,4,8,1024]{3,2,1,0:T(8,128)(2,1)}), bf16[32,4,8,1024]{3,2,1,0:T(8,128)(2,1)}, u32[]{:S(2)}, u32[]{:S(2)}) %all-to-all-start.4) | async-done | bytes 2097184 | tf_op jit(solution)/shard_map/all_to_all | solution.py:33
  82.5 5.2 %all-to-all-start.2 = ((bf16[32,4,8,1024]{3,2,1,0:T(8,128)(2,1)}), bf16[32,4,8,1024]{3,2,1,0:T(8,128)(2,1)}, u32[]{:S(2)}, u32[]{:S(2)}) async-start(bf16[32,4,8,1024]{3,2,1,0:T(8,128)(2,1)} %bitcast.137), calls=%async_computation.2 | async-start | bytes 4194304 | tf_op jit(solution)/shard_map/all_to_all | solution.py:33
  99.5 2.9 %convolution_convert_fusion.3 = bf16[512,2048]{1,0:T(8,128)(2,1)S(1)} fusion(bf16[512,2048]{1,0:T(8,128)(2,1)} %copy-done.23, s32[512]{0:T(512)S(1)} %copy-done.24, s32[512]{0:T(512)S(1)} %copy-done.25, s32[512]{0:T(512)S(1)} %fusion.74, s32[512]{0:T(512)S(1)} %get-tuple-element.11), kind=kOutput, calls=%fused_computation.6 | convolution fusion | flops 1075576832 | bytes 4202496 | tf_op jit(solution)/shard_map/dot_general | solution.py:30
  103.9 12.3 %all-to-all-done.2 = bf16[32,4,8,1024]{3,2,1,0:T(8,128)(2,1)} async-done(((bf16[32,4,8,1024]{3,2,1,0:T(8,128)(2,1)}), bf16[32,4,8,1024]{3,2,1,0:T(8,128)(2,1)}, u32[]{:S(2)}, u32[]{:S(2)}) %all-to-all-start.2) | async-done | bytes 2097184 | tf_op jit(solution)/shard_map/all_to_all | solution.py:33
  116.2 5.2 %all-to-all-start = ((bf16[32,4,8,1024]{3,2,1,0:T(8,128)(2,1)}), bf16[32,4,8,1024]{3,2,1,0:T(8,128)(2,1)}, u32[]{:S(2)}, u32[]{:S(2)}) async-start(bf16[32,4,8,1024]{3,2,1,0:T(8,128)(2,1)} %bitcast.139), calls=%async_computation | async-start | bytes 4194304 | tf_op jit(solution)/shard_map/all_to_all | solution.py:33
  133.2 16.6 %all-to-all-done = bf16[32,4,8,1024]{3,2,1,0:T(8,128)(2,1)} async-done(((bf16[32,4,8,1024]{3,2,1,0:T(8,128)(2,1)}), bf16[32,4,8,1024]{3,2,1,0:T(8,128)(2,1)}, u32[]{:S(2)}, u32[]{:S(2)}) %all-to-all-start) | async-done | bytes 2097184 | tf_op jit(solution)/shard_map/all_to_all | solution.py:33
  158.9 2.6 copy.83
  161.4 2.8 %fusion.24 = f32[2,512,1024]{2,1,0:T(8,128)} fusion(bf16[1,2,32,8,1024]{4,3,1,2,0:T(8,128)(2,1)S(1)} %copy-done.20, f32[2,256,512]{2,1,0:T(8,128)S(1)} %copy-done.32), kind=kOutput, calls=%fused_computation.43 | convolution fusion | flops 538181632 | bytes 6291456 | tf_op jit(solution)/shard_map/erf,erd->efd/dot_general | solution.py:47
  164.2 2.8 %fusion.31 = f32[2,512,1024]{2,1,0:T(8,128)} fusion(bf16[1,2,32,8,1024]{4,3,1,2,0:T(8,128)(2,1)S(1)} %copy-done.22, f32[2,256,512]{2,1,0:T(8,128)S(1)} %copy-done.34), kind=kOutput, calls=%fused_computation.50 | convolution fusion | flops 538181632 | bytes 6291456 | tf_op jit(solution)/shard_map/erf,erd->efd/dot_general | solution.py:47
  170.2 4.8 %add_convert_fusion = bf16[2,512,1024]{2,1,0:T(8,128)(2,1)} fusion(f32[2,512,1024]{2,1,0:T(8,128)S(1)} %fusion.17, f32[2,512,1024]{2,1,0:T(8,128)} %fusion.31, f32[2,512,1024]{2,1,0:T(8,128)S(1)} %copy-done.5, bf16[1,2,32,8,1024]{4,3,1,2,0:T(8,128)(2,1)S(1)} %copy-done.4, f32[2,256,512]{2,1,0:T(8,128)S(1)} %copy-done.15), kind=kOutput, calls=%fused_computation.1 | convolution fusion | flops 542375936 | bytes 16777216 | tf_op jit(solution)/shard_map/erf,erd->efd/dot_general | solution.py:47
  176.9 4.3 %all-to-all-start.7 = ((bf16[1,2,256,128]{3,1,0,2:T(2,128)(2,1)}), bf16[1,2,256,128]{3,1,0,2:T(2,128)(2,1)S(1)}, u32[]{:S(2)}, u32[]{:S(2)}) async-start(bf16[1,2,256,128]{3,1,0,2:T(2,128)(2,1)} %copy.57), calls=%async_computation.7 | async-start | bytes 262144 | tf_op jit(solution)/shard_map/all_to_all | solution.py:62
  181.2 4.2 %fusion.27 = f32[2,1024,512]{2,1,0:T(8,128)} fusion(bf16[2,256,512]{2,1,0:T(8,128)(2,1)} %copy-done.13, bf16[1,2,32,8,1024]{4,3,1,2,0:T(8,128)(2,1)} %copy-done.9), kind=kOutput, calls=%fused_computation.46 | convolution fusion | flops 536870912 | bytes 5767168 | tf_op jit(solution)/shard_map/erd,erf->edf/dot_general | solution.py:50
  189.0 5.8 %all-to-all-start.5 = ((bf16[1,2,256,128]{3,1,0,2:T(2,128)(2,1)}), bf16[1,2,256,128]{3,1,0,2:T(2,128)(2,1)S(1)}, u32[]{:S(2)}, u32[]{:S(2)}) async-start(bf16[1,2,256,128]{3,1,0,2:T(2,128)(2,1)} %copy.52), calls=%async_computation.5 | async-start | bytes 262144 | tf_op jit(solution)/shard_map/all_to_all | solution.py:62
  194.8 3.8 %fusion.20 = f32[2,1024,512]{2,1,0:T(8,128)} fusion(bf16[2,256,512]{2,1,0:T(8,128)(2,1)} %copy-done.12, bf16[1,2,32,8,1024]{4,3,1,2,0:T(8,128)(2,1)S(1)} %copy-done.8), kind=kOutput, calls=%fused_computation.39 | convolution fusion | flops 536870912 | bytes 5767168 | tf_op jit(solution)/shard_map/erd,erf->edf/dot_general | solution.py:50
  202.5 5.4 %all-to-all-start.3 = ((bf16[1,2,256,128]{3,1,0,2:T(2,128)(2,1)}), bf16[1,2,256,128]{3,1,0,2:T(2,128)(2,1)S(1)}, u32[]{:S(2)}, u32[]{:S(2)}) async-start(bf16[1,2,256,128]{3,1,0,2:T(2,128)(2,1)} %copy.47), calls=%async_computation.3 | async-start | bytes 262144 | tf_op jit(solution)/shard_map/all_to_all | solution.py:62
  207.9 4.3 %fusion.13 = f32[2,1024,512]{2,1,0:T(8,128)} fusion(bf16[2,256,512]{2,1,0:T(8,128)(2,1)} %copy-done.11, bf16[1,2,32,8,1024]{4,3,1,2,0:T(8,128)(2,1)} %copy-done.6), kind=kOutput, calls=%fused_computation.32 | convolution fusion | flops 536870912 | bytes 5767168 | tf_op jit(solution)/shard_map/erd,erf->edf/dot_general | solution.py:50
  212.2 11.3 %reduce-scatter.13.cloned.1.call-done = bf16[128,512]{1,0:T(8,128)(2,1)} async-done(((bf16[1024,512]{1,0:T(8,128)(2,1)}), bf16[128,512]{1,0:T(8,128)(2,1)}) %reduce-scatter.13.cloned.1.call-update) | async-done | bytes 131088
  228.5 12.5 %all-to-all-start.1 = ((bf16[1,2,256,128]{3,1,0,2:T(2,128)(2,1)}), bf16[1,2,256,128]{3,1,0,2:T(2,128)(2,1)}, u32[]{:S(2)}, u32[]{:S(2)}) async-start(bf16[1,2,256,128]{3,1,0,2:T(2,128)(2,1)} %copy.42), calls=%async_computation.1 | async-start | bytes 262144 | tf_op jit(solution)/shard_map/all_to_all | solution.py:62
  240.9 7.0 %add_convert_fusion.1 = bf16[2,1024,512]{2,1,0:T(8,128)(2,1)} fusion(f32[2,1024,512]{2,1,0:T(8,128)} %fusion.13, f32[2,1024,512]{2,1,0:T(8,128)} %fusion.27, f32[2,1024,512]{2,1,0:T(8,128)} %fusion.20, bf16[2,256,512]{2,1,0:T(8,128)(2,1)} %copy-done.10, bf16[1,2,32,8,1024]{4,3,1,2,0:T(8,128)(2,1)S(1)} %copy-done.2), kind=kOutput, calls=%fused_computation.2 | convolution fusion | flops 541065216 | bytes 16252928 | tf_op jit(solution)/shard_map/erd,erf->edf/dot_general | solution.py:50
  (140 shorter events, 73.9 us)
Async XLA Ops:
  7.2 48.7 %copy-start = (bf16[2,1024,512]{2,1,0:T(8,128)(2,1)S(1)}, bf16[2,1024,512]{2,1,0:T(8,128)(2,1)}, u32[]{:S(2)}) copy-start(bf16[2,1024,512]{2,1,0:T(8,128)(2,1)} %param.10) | copy-start | bytes 6291460
  11.8 37.0 %all-to-all-start.6 = ((bf16[32,4,8,1024]{3,2,1,0:T(8,128)(2,1)}), bf16[32,4,8,1024]{3,2,1,0:T(8,128)(2,1)}, u32[]{:S(2)}, u32[]{:S(2)}) async-start(bf16[32,4,8,1024]{3,2,1,0:T(8,128)(2,1)} %bitcast.140), calls=%async_computation.6 | async-start | bytes 4194304 | tf_op jit(solution)/shard_map/all_to_all | solution.py:33
  48.8 33.7 %all-to-all-start.4 = ((bf16[32,4,8,1024]{3,2,1,0:T(8,128)(2,1)}), bf16[32,4,8,1024]{3,2,1,0:T(8,128)(2,1)}, u32[]{:S(2)}, u32[]{:S(2)}) async-start(bf16[32,4,8,1024]{3,2,1,0:T(8,128)(2,1)} %bitcast.138), calls=%async_computation.4 | async-start | bytes 4194304 | tf_op jit(solution)/shard_map/all_to_all | solution.py:33
  54.0 121.0 %reduce-scatter.19.cloned.1.call-start = ((), (), s32[]{:S(2)}) async-start(), calls=%async_computation.15 | async-start | bytes 1179648
  56.8 2.7 %copy-start.14 = (f32[2,256,512]{2,1,0:T(8,128)}, f32[2,256,512]{2,1,0:T(8,128)S(1)}, u32[]{:S(2)}) copy-start(f32[2,256,512]{2,1,0:T(8,128)S(1)} %fusion.9) | copy-start | bytes 3145732
  82.5 33.7 %all-to-all-start.2 = ((bf16[32,4,8,1024]{3,2,1,0:T(8,128)(2,1)}), bf16[32,4,8,1024]{3,2,1,0:T(8,128)(2,1)}, u32[]{:S(2)}, u32[]{:S(2)}) async-start(bf16[32,4,8,1024]{3,2,1,0:T(8,128)(2,1)} %bitcast.137), calls=%async_computation.2 | async-start | bytes 4194304 | tf_op jit(solution)/shard_map/all_to_all | solution.py:33
  87.7 97.7 %reduce-scatter.17.cloned.1.call-start = ((), (), s32[]{:S(2)}) async-start(), calls=%async_computation.14 | async-start | bytes 1179648
  89.7 2.7 %copy-start.27 = (bf16[2,512,1024]{2,1,0:T(8,128)(2,1)S(1)}, bf16[2,512,1024]{2,1,0:T(8,128)(2,1)}, u32[]{:S(2)}) copy-start(bf16[2,512,1024]{2,1,0:T(8,128)(2,1)} %param.11) | copy-start | bytes 6291460
  90.6 2.7 %copy-start.30 = (f32[2,256,512]{2,1,0:T(8,128)}, f32[2,256,512]{2,1,0:T(8,128)S(1)}, u32[]{:S(2)}) copy-start(f32[2,256,512]{2,1,0:T(8,128)S(1)} %fusion.15) | copy-start | bytes 3145732
  116.2 33.7 %all-to-all-start = ((bf16[32,4,8,1024]{3,2,1,0:T(8,128)(2,1)}), bf16[32,4,8,1024]{3,2,1,0:T(8,128)(2,1)}, u32[]{:S(2)}, u32[]{:S(2)}) async-start(bf16[32,4,8,1024]{3,2,1,0:T(8,128)(2,1)} %bitcast.139), calls=%async_computation | async-start | bytes 4194304 | tf_op jit(solution)/shard_map/all_to_all | solution.py:33
  121.4 77.3 %reduce-scatter.15.cloned.1.call-start = ((), (), s32[]{:S(2)}) async-start(), calls=%async_computation.13 | async-start | bytes 1179648
  123.2 2.7 %copy-start.28 = (bf16[2,512,1024]{2,1,0:T(8,128)(2,1)S(1)}, bf16[2,512,1024]{2,1,0:T(8,128)(2,1)}, u32[]{:S(2)}) copy-start(bf16[2,512,1024]{2,1,0:T(8,128)(2,1)} %param.11) | copy-start | bytes 6291460
  132.9 90.6 %reduce-scatter.13.cloned.1.call-start = ((), (), s32[]{:S(2)}) async-start(), calls=%async_computation.12 | async-start | bytes 1179648
  161.4 2.8 %copy-start.22 = (bf16[1,2,32,8,1024]{4,3,1,2,0:T(8,128)(2,1)S(1)}, bf16[1,2,32,8,1024]{4,3,1,2,0:T(8,128)(2,1)}, u32[]{:S(2)}) copy-start(bf16[1,2,32,8,1024]{4,3,1,2,0:T(8,128)(2,1)} %copy-done.21) | copy-start | bytes 3145732
  161.4 2.8 %copy-start.34 = (f32[2,256,512]{2,1,0:T(8,128)S(1)}, f32[2,256,512]{2,1,0:T(8,128)}, u32[]{:S(2)}) copy-start(f32[2,256,512]{2,1,0:T(8,128)} %copy-done.33) | copy-start | bytes 3145732
  164.2 2.8 %copy-start.18 = (bf16[1,2,32,8,1024]{4,3,1,2,0:T(8,128)(2,1)S(1)}, bf16[1,2,32,8,1024]{4,3,1,2,0:T(8,128)(2,1)}, u32[]{:S(2)}) copy-start(bf16[1,2,32,8,1024]{4,3,1,2,0:T(8,128)(2,1)} %copy-done.17) | copy-start | bytes 3145732
  167.1 2.9 %copy-start.5 = (f32[2,512,1024]{2,1,0:T(8,128)S(1)}, f32[2,512,1024]{2,1,0:T(8,128)}, u32[]{:S(2)}) copy-start(f32[2,512,1024]{2,1,0:T(8,128)} %fusion.24) | copy-start | bytes 12582916
  167.1 3.1 %copy-start.15 = (f32[2,256,512]{2,1,0:T(8,128)S(1)}, f32[2,256,512]{2,1,0:T(8,128)}, u32[]{:S(2)}) copy-start(f32[2,256,512]{2,1,0:T(8,128)} %copy-done.14) | copy-start | bytes 3145732
  176.9 12.1 %all-to-all-start.7 = ((bf16[1,2,256,128]{3,1,0,2:T(2,128)(2,1)}), bf16[1,2,256,128]{3,1,0,2:T(2,128)(2,1)S(1)}, u32[]{:S(2)}, u32[]{:S(2)}) async-start(bf16[1,2,256,128]{3,1,0,2:T(2,128)(2,1)} %copy.57), calls=%async_computation.7 | async-start | bytes 262144 | tf_op jit(solution)/shard_map/all_to_all | solution.py:62
  181.2 13.6 %copy-start.8 = (bf16[1,2,32,8,1024]{4,3,1,2,0:T(8,128)(2,1)S(1)}, bf16[1,2,32,8,1024]{4,3,1,2,0:T(8,128)(2,1)}, u32[]{:S(2)}) copy-start(bf16[1,2,32,8,1024]{4,3,1,2,0:T(8,128)(2,1)} %copy-done.7) | copy-start | bytes 3145732
  189.0 13.5 %all-to-all-start.5 = ((bf16[1,2,256,128]{3,1,0,2:T(2,128)(2,1)}), bf16[1,2,256,128]{3,1,0,2:T(2,128)(2,1)S(1)}, u32[]{:S(2)}, u32[]{:S(2)}) async-start(bf16[1,2,256,128]{3,1,0,2:T(2,128)(2,1)} %copy.52), calls=%async_computation.5 | async-start | bytes 262144 | tf_op jit(solution)/shard_map/all_to_all | solution.py:62
  202.5 26.0 %all-to-all-start.3 = ((bf16[1,2,256,128]{3,1,0,2:T(2,128)(2,1)}), bf16[1,2,256,128]{3,1,0,2:T(2,128)(2,1)S(1)}, u32[]{:S(2)}, u32[]{:S(2)}) async-start(bf16[1,2,256,128]{3,1,0,2:T(2,128)(2,1)} %copy.47), calls=%async_computation.3 | async-start | bytes 262144 | tf_op jit(solution)/shard_map/all_to_all | solution.py:62
  207.9 33.1 %copy-start.2 = (bf16[1,2,32,8,1024]{4,3,1,2,0:T(8,128)(2,1)S(1)}, bf16[1,2,32,8,1024]{4,3,1,2,0:T(8,128)(2,1)}, u32[]{:S(2)}) copy-start(bf16[1,2,32,8,1024]{4,3,1,2,0:T(8,128)(2,1)} %copy-done.1) | copy-start | bytes 3145732
  228.5 20.2 %all-to-all-start.1 = ((bf16[1,2,256,128]{3,1,0,2:T(2,128)(2,1)}), bf16[1,2,256,128]{3,1,0,2:T(2,128)(2,1)}, u32[]{:S(2)}, u32[]{:S(2)}) async-start(bf16[1,2,256,128]{3,1,0,2:T(2,128)(2,1)} %copy.42), calls=%async_computation.1 | async-start | bytes 262144 | tf_op jit(solution)/shard_map/all_to_all | solution.py:62
  (23 other events, 37.2 us)
Sparse Core Ops, SparseCore 0:
  65.6 37.0 reduce-scatter.18
  105.3 38.1 reduce-scatter.16
  146.0 36.8 reduce-scatter.14
  185.9 37.6 reduce-scatter.12

commit v2 on v1

v2 whole, which is shorter than its diff:
```python
import jax
import jax.numpy as jnp
from jax import lax
from jax.sharding import PartitionSpec as P


def on_device(tokens, grad_out, region_ids, slot_ids, weight_in, weight_out):
    owners = lax.axis_size("dp")
    local_count = weight_in.shape[0]
    model_width = tokens.shape[1]
    tok_rows = tokens.shape[0]
    experts_all = local_count * owners
    capacity = 4 * tok_rows // experts_all
    where_to = region_ids * capacity + slot_ids
    both = jnp.concatenate([tokens, grad_out], axis=1)

    rows = jnp.arange(owners * capacity, dtype=jnp.int32)
    owner_of = rows // capacity
    slot_of = rows % capacity
    win_parts, wout_parts, back_parts = [], [], []
    for local in range(local_count):
        expert_of = owner_of * local_count + local
        pick = (
            (region_ids[None, :] == expert_of[:, None]) & (slot_ids[None, :] == slot_of[:, None])
        ).astype(jnp.bfloat16)
        sent = jnp.dot(pick, both, preferred_element_type=jnp.float32).astype(jnp.bfloat16)
        sent = sent.reshape(owners, capacity, 2, model_width)
        got = lax.all_to_all(sent, "dp", split_axis=0, concat_axis=1, tiled=True)[0]
        routed_in = got[:, 0, :]
        routed_grad = got[:, 1, :]
        w_in = weight_in[local]
        w_out = weight_out[local]
        pre_act = jnp.dot(routed_in, w_in, preferred_element_type=jnp.float32)
        gate_sig = jax.nn.sigmoid(pre_act)
        back_grad = lax.dot_general(
            routed_grad, w_out, (((1,), (1,)), ((), ())), preferred_element_type=jnp.float32
        )
        pre_grad = (back_grad * gate_sig * (1.0 + pre_act * (1.0 - gate_sig))).astype(
            jnp.bfloat16
        )
        partial_value = lax.dot_general(
            pre_grad, w_in, (((1,), (1,)), ((), ())), preferred_element_type=jnp.float32
        )
        summed = lax.psum_scatter(
            partial_value.astype(jnp.bfloat16), "expert", scatter_dimension=1, tiled=True
        )
        back_parts.append(
            lax.all_to_all(
                summed.reshape(1, owners, capacity, summed.shape[1]),
                "dp",
                split_axis=1,
                concat_axis=0,
                tiled=True,
            )
        )
        hidden_act = (pre_act * gate_sig).astype(jnp.bfloat16)
        wout_parts.append(
            lax.dot_general(
                hidden_act, routed_grad, (((0,), (0,)), ((), ())),
                preferred_element_type=jnp.float32,
            ).astype(jnp.bfloat16)
        )
        win_parts.append(
            lax.dot_general(
                routed_in, pre_grad, (((0,), (0,)), ((), ())),
                preferred_element_type=jnp.float32,
            ).astype(jnp.bfloat16)
        )
    back_rows = jnp.concatenate(back_parts, axis=1)
    grad_tokens = back_rows.reshape(experts_all * capacity, back_rows.shape[3])[where_to]
    return (grad_tokens, jnp.stack(win_parts), jnp.stack(wout_parts))


def solution(mesh):
    in_specs = (
        P("dp", None),
        P("dp", None),
        P("dp"),
        P("dp"),
        P("dp", None, "expert"),
        P("dp", "expert", None),
    )
    out_specs = (P("dp", "expert"), P("dp", None, "expert"), P("dp", "expert", None))
    return jax.shard_map(
        on_device, mesh=mesh, in_specs=in_specs, out_specs=out_specs, check_vma=False
    )
```

time: 260 us -> 228 us (0.88)
  matrix products: 51.4 us -> 27.7 us
  waiting for transfers between devices: 81.2 us -> 101 us
  starting transfers between devices: 52.7 us -> 34.9 us
  local copies, waits for them, and re-layouts: 58.3 us -> 44.2 us
  other arithmetic: 0.12 us -> 4.4 us
    dot_general x20 -> x10, matrix products: 41.4 us -> 19.4 us  [the longest x2 7.17 us: on_device(): lax.dot_general(routed_in, pre_grad, (((0,), (0,)), ((), ())), preferred_...]
    unnamed x87 -> x47, local copies, waits for them, and re-layouts: 38.4 us -> 19.1 us
    all_to_all x8 -> x4, starting transfers between devices: 52.1 us -> 34.7 us  [the longest x2 18.9 us: on_device(): lax.all_to_all(summed.reshape(1, owners, capacity, summed.shape[1]), 'dp'...]
    all_to_all x8 -> x4, waiting for transfers between devices: 69.8 us -> 83.1 us  [the longest x2 78.4 us: on_device(): got = lax.all_to_all(sent, 'dp', split_axis=0, concat_axis=1, tiled=True)[0]]
    reshape x4 -> x2, local copies, waits for them, and re-layouts: 5.99 us -> 15.8 us  [on_device(): sent = sent.reshape(owners, capacity, 2, model_width)]
    slice x4 -> x0, local copies, waits for them, and re-layouts: 6.89 us -> none  [on_device(): routed_grad = got[local_count:]]
    unnamed x8 -> x4, waiting for transfers between devices: 11.4 us -> 18 us
    all_to_all x4 -> x2, local copies, waits for them, and re-layouts: 0.98 us -> 7.28 us  [on_device(): got = lax.all_to_all(sent, 'dp', split_axis=0, concat_axis=1, tiled=True)[0]]
  transfers between devices with their start and end apart: 12 -> 6, of which waited for: 8 -> 4; matrix products, arithmetic and copies ran while one was open for 35% -> 23% of each run, Pallas kernels for 0% -> 0%
where the time goes in v2:
time: 228 us; the launch traced here: 227 us
  waiting for transfers between devices  101 us (44%)
  local copies, waits for them, and re-layouts  44.2 us (19%)
  starting transfers between devices  34.9 us (15%)
  matrix products  27.7 us (12%)
  between operations  14.4 us (6%)
  other arithmetic  4.4 us (2%)
    all_to_all x2, waiting for transfers between devices, on_device(): got = lax.all_to_all(sent, 'dp', split_axis=0, concat_axis=1, tiled=True)[0]  78.4 us
    unnamed x47, local copies, waits for them, and re-layouts  19.1 us
    all_to_all x2, starting transfers between devices, on_device(): lax.all_to_all(summed.reshape(1, owners, capacity, summed.shape[1]), 'dp'...  18.9 us
    unnamed x4, waiting for transfers between devices  18 us
    reshape x2, local copies, waits for them, and re-layouts, on_device(): sent = sent.reshape(owners, capacity, 2, model_width)  15.8 us
    all_to_all x2, starting transfers between devices, on_device(): got = lax.all_to_all(sent, 'dp', split_axis=0, concat_axis=1, tiled=True)[0]  15.7 us
    dot_general x2, matrix products, on_device(): jnp.dot(pick, both, preferred_element_type=jnp.float32).astype(jnp.bfloat16)  8.24 us
    all_to_all x2, local copies, waits for them, and re-layouts, on_device(): got = lax.all_to_all(sent, 'dp', split_axis=0, concat_axis=1, tiled=True)[0]  7.28 us
  transfers between devices with their start and end apart: 6, of which 4 were waited for; matrix products, arithmetic and copies ran while one was open for 23% of the time, Pallas kernels for 0%

profile of v2, /device:TPU:1, one launch (start us, length us, event | category | flops | bytes accessed | tf_op | source)
XLA Modules:
  0.0 226.6 jit_solution(6557683872605920073)
XLA Ops:
  8.8 4.1 %convolution_convert_fusion.1 = bf16[1024,2048]{1,0:T(8,128)(2,1)} fusion(bf16[512,2048]{1,0:T(8,128)(2,1)S(1)} %constant_dynamic-update-slice_fusion, s32[512]{0:T(512)S(1)} %copy-done.6, s32[512]{0:T(512)S(1)} %copy-done.7, s32[1024]{0:T(1024)S(1)} %get-tuple-element.3, s32[1024]{0:T(1024)S(1)} %fusion.50), kind=kOutput, calls=%fused_computation.2 | convolution fusion | flops 2151153664 | bytes 6303744 | tf_op jit(solution)/shard_map/dot_general | solution.py:26
  12.9 7.9 %reshape.63 = bf16[32,32,2,1024]{3,2,1,0:T(2,128)(2,1)} reshape(bf16[1024,2048]{1,0:T(8,128)(2,1)} %convolution_convert_fusion.1) | data formatting | bytes 8388608 | tf_op jit(solution)/shard_map/reshape | solution.py:27
  20.9 8.6 %all-to-all-start = ((bf16[32,32,2,1024]{3,2,1,0:T(2,128)(2,1)}), bf16[32,32,2,1024]{3,2,1,0:T(2,128)(2,1)}, u32[]{:S(2)}, u32[]{:S(2)}) async-start(bf16[32,32,2,1024]{3,2,1,0:T(2,128)(2,1)} %reshape.63), calls=%async_computation | async-start | bytes 8388608 | tf_op jit(solution)/shard_map/all_to_all | solution.py:28
  29.5 4.1 %convolution_convert_fusion = bf16[1024,2048]{1,0:T(8,128)(2,1)} fusion(bf16[512,2048]{1,0:T(8,128)(2,1)S(1)} %constant_dynamic-update-slice_fusion, s32[512]{0:T(512)S(1)} %copy-done.6, s32[512]{0:T(512)S(1)} %copy-done.7, s32[1024]{0:T(1024)S(1)} %get-tuple-element.4, s32[1024]{0:T(1024)S(1)} %get-tuple-element.3), kind=kOutput, calls=%fused_computation.1 | convolution fusion | flops 2151153664 | bytes 6303744 | tf_op jit(solution)/shard_map/dot_general | solution.py:26
  33.6 7.8 %reshape.65 = bf16[32,32,2,1024]{3,2,1,0:T(2,128)(2,1)} reshape(bf16[1024,2048]{1,0:T(8,128)(2,1)} %convolution_convert_fusion) | data formatting | bytes 8388608 | tf_op jit(solution)/shard_map/reshape | solution.py:27
  41.5 40.2 %all-to-all-done = bf16[32,32,2,1024]{3,2,1,0:T(2,128)(2,1)} async-done(((bf16[32,32,2,1024]{3,2,1,0:T(2,128)(2,1)}), bf16[32,32,2,1024]{3,2,1,0:T(2,128)(2,1)}, u32[]{:S(2)}, u32[]{:S(2)}) %all-to-all-start) | async-done | bytes 4194336 | tf_op jit(solution)/shard_map/all_to_all | solution.py:28
  81.6 7.1 %all-to-all-start.2 = ((bf16[32,32,2,1024]{3,2,1,0:T(2,128)(2,1)}), bf16[32,32,2,1024]{3,2,1,0:T(2,128)(2,1)}, u32[]{:S(2)}, u32[]{:S(2)}) async-start(bf16[32,32,2,1024]{3,2,1,0:T(2,128)(2,1)} %reshape.65), calls=%async_computation.2 | async-start | bytes 8388608 | tf_op jit(solution)/shard_map/all_to_all | solution.py:28
  88.8 3.7 %copy.13 = bf16[32,32,2,1024]{3,1,0,2:T(8,128)(2,1)S(1)} copy(bf16[32,32,2,1024]{3,2,1,0:T(2,128)(2,1)} %all-to-all-done) | data formatting | bytes 8388608 | tf_op jit(solution)/shard_map/all_to_all | solution.py:28
  95.6 1.8 multiply_convert_fusion.3
  99.7 2.6 %copy.18 = bf16[1024,1024]{0,1:T(8,128)(2,1)} copy(bf16[1024,1024]{1,0:T(8,128)(2,1)S(1)} %convolution_convert_fusion.3) | data formatting | bytes 4194304
  102.5 38.3 %all-to-all-done.2 = bf16[32,32,2,1024]{3,2,1,0:T(2,128)(2,1)} async-done(((bf16[32,32,2,1024]{3,2,1,0:T(2,128)(2,1)}), bf16[32,32,2,1024]{3,2,1,0:T(2,128)(2,1)}, u32[]{:S(2)}, u32[]{:S(2)}) %all-to-all-start.2) | async-done | bytes 4194336 | tf_op jit(solution)/shard_map/all_to_all | solution.py:28
  140.8 3.6 %copy.15 = bf16[32,32,2,1024]{3,1,0,2:T(8,128)(2,1)S(1)} copy(bf16[32,32,2,1024]{3,2,1,0:T(2,128)(2,1)} %all-to-all-done.2) | data formatting | bytes 8388608 | tf_op jit(solution)/shard_map/all_to_all | solution.py:28
  147.6 1.8 multiply_convert_fusion.2
  151.6 2.6 %copy.20 = bf16[1024,1024]{0,1:T(8,128)(2,1)} copy(bf16[1024,1024]{1,0:T(8,128)(2,1)S(1)} %convolution_convert_fusion.2) | data formatting | bytes 4194304
  155.4 3.0 %fusion.15 = bf16[1,1024,512]{2,1,0:T(8,128)(2,1)S(1)} fusion(bf16[1024,512]{1,0:T(8,128)(2,1)S(1)} %copy-done.19, bf16[1024,2,1024]{2,0,1:T(8,128)(2,1)} %bitcast.90), kind=kOutput, calls=%fused_computation.34 | convolution fusion | flops 1074266112 | bytes 4194304 | tf_op jit(solution)/shard_map/dot_general | solution.py:64
  161.8 2.3 %fusion.16 = bf16[1,512,1024]{2,1,0:T(8,128)(2,1)} fusion(bf16[1024,2,1024]{2,0,1:T(8,128)(2,1)S(1)} %bitcast.95, f32[1024,512]{1,0:T(8,128)S(1)} %copy-done.17), kind=kOutput, calls=%fused_computation.35 | convolution fusion | flops 1076887552 | bytes 5242880 | tf_op jit(solution)/shard_map/dot_general | solution.py:58
  165.9 7.0 %all-to-all-start.1 = ((bf16[1,32,32,128]{3,2,0,1:T(8,128)(2,1)}), bf16[1,32,32,128]{3,2,0,1:T(8,128)(2,1)S(1)}, u32[]{:S(2)}, u32[]{:S(2)}) async-start(bf16[1,32,32,128]{3,2,0,1:T(8,128)(2,1)} %bitcast.6), calls=%async_computation.1 | async-start | bytes 524288 | tf_op jit(solution)/shard_map/all_to_all | solution.py:48
  172.9 4.2 %fusion.17 = bf16[1,1024,512]{2,1,0:T(8,128)(2,1)} fusion(bf16[1024,512]{1,0:T(8,128)(2,1)} %copy-done.20, bf16[1024,2,1024]{2,0,1:T(8,128)(2,1)} %bitcast.94), kind=kOutput, calls=%fused_computation.36 | convolution fusion | flops 1074266112 | bytes 4194304 | tf_op jit(solution)/shard_map/dot_general | solution.py:64
  177.1 18.0 %reduce-scatter.9.cloned.1.call-done = bf16[128,1024]{1,0:T(8,128)(2,1)} async-done(((bf16[1024,1024]{1,0:T(8,128)(2,1)}), bf16[128,1024]{1,0:T(8,128)(2,1)}) %reduce-scatter.9.cloned.1.call-update) | async-done | bytes 262160
  195.1 1.8 copy.21
  196.9 11.9 %all-to-all-start.3 = ((bf16[1,32,32,128]{3,2,0,1:T(8,128)(2,1)}), bf16[1,32,32,128]{3,2,0,1:T(8,128)(2,1)S(1)}, u32[]{:S(2)}, u32[]{:S(2)}) async-start(bf16[1,32,32,128]{3,2,0,1:T(8,128)(2,1)} %bitcast.14), calls=%async_computation.3 | async-start | bytes 524288 | tf_op jit(solution)/shard_map/all_to_all | solution.py:48
  208.8 2.8 %pad_maximum_fusion = bf16[2,1024,512]{2,1,0:T(8,128)(2,1)} fusion(bf16[1,1024,512]{2,1,0:T(8,128)(2,1)} %fusion.17, bf16[1,1024,512]{2,1,0:T(8,128)(2,1)S(1)} %fusion.15), kind=kLoop, calls=%fused_computation.9 | loop fusion | flops 1048576 | bytes 4194304 | tf_op jit(solution)/shard_map/stack | solution.py:71
  213.1 4.6 %all-to-all-done.3 = bf16[1,32,32,128]{3,2,0,1:T(8,128)(2,1)S(1)} async-done(((bf16[1,32,32,128]{3,2,0,1:T(8,128)(2,1)}), bf16[1,32,32,128]{3,2,0,1:T(8,128)(2,1)S(1)}, u32[]{:S(2)}, u32[]{:S(2)}) %all-to-all-start.3) | async-done | bytes 262176 | tf_op jit(solution)/shard_map/all_to_all | solution.py:48
  217.9 1.9 gather_fusion
  (63 shorter events, 20.6 us)
Async XLA Ops:
  7.2 1.5 copy-start.4
  7.2 1.6 copy-start.6
  7.2 1.6 copy-start.7
  20.9 60.8 %all-to-all-start = ((bf16[32,32,2,1024]{3,2,1,0:T(2,128)(2,1)}), bf16[32,32,2,1024]{3,2,1,0:T(2,128)(2,1)}, u32[]{:S(2)}, u32[]{:S(2)}) async-start(bf16[32,32,2,1024]{3,2,1,0:T(2,128)(2,1)} %reshape.63), calls=%async_computation | async-start | bytes 8388608 | tf_op jit(solution)/shard_map/all_to_all | solution.py:28
  81.6 59.2 %all-to-all-start.2 = ((bf16[32,32,2,1024]{3,2,1,0:T(2,128)(2,1)}), bf16[32,32,2,1024]{3,2,1,0:T(2,128)(2,1)}, u32[]{:S(2)}, u32[]{:S(2)}) async-start(bf16[32,32,2,1024]{3,2,1,0:T(2,128)(2,1)} %reshape.65), calls=%async_computation.2 | async-start | bytes 8388608 | tf_op jit(solution)/shard_map/all_to_all | solution.py:28
  88.7 3.8 %copy-start.10 = (bf16[2,1024,512]{2,1,0:T(8,128)(2,1)S(1)}, bf16[2,1024,512]{2,1,0:T(8,128)(2,1)}, u32[]{:S(2)}) copy-start(bf16[2,1024,512]{2,1,0:T(8,128)(2,1)} %param.10) | copy-start | bytes 6291460
  88.7 75.4 %reduce-scatter.7.cloned.1.call-start = ((), (), s32[]{:S(2)}) async-start(), calls=%async_computation.6 | async-start | bytes 2359296
  92.4 2.1 copy-start
  92.5 3.1 %copy-start.8 = (bf16[2,512,1024]{2,1,0:T(8,128)(2,1)S(1)}, bf16[2,512,1024]{2,1,0:T(8,128)(2,1)}, u32[]{:S(2)}) copy-start(bf16[2,512,1024]{2,1,0:T(8,128)(2,1)} %param.11) | copy-start | bytes 6291460
  95.6 1.8 copy-start.14
  95.6 2.8 %copy-start.11 = (bf16[2,1024,512]{2,1,0:T(8,128)(2,1)S(1)}, bf16[2,1024,512]{2,1,0:T(8,128)(2,1)}, u32[]{:S(2)}) copy-start(bf16[2,1024,512]{2,1,0:T(8,128)(2,1)} %param.10) | copy-start | bytes 6291460
  102.3 42.2 %copy-start.12 = (bf16[2,1024,512]{2,1,0:T(8,128)(2,1)S(1)}, bf16[2,1024,512]{2,1,0:T(8,128)(2,1)}, u32[]{:S(2)}) copy-start(bf16[2,1024,512]{2,1,0:T(8,128)(2,1)} %param.10) | copy-start | bytes 6291460
  102.3 92.8 %reduce-scatter.9.cloned.1.call-start = ((), (), s32[]{:S(2)}) async-start(), calls=%async_computation.7 | async-start | bytes 2359296
  144.4 2.1 copy-start.2
  144.4 3.1 %copy-start.9 = (bf16[2,512,1024]{2,1,0:T(8,128)(2,1)S(1)}, bf16[2,512,1024]{2,1,0:T(8,128)(2,1)}, u32[]{:S(2)}) copy-start(bf16[2,512,1024]{2,1,0:T(8,128)(2,1)} %param.11) | copy-start | bytes 6291460
  147.6 1.8 copy-start.16
  147.6 2.8 %copy-start.13 = (bf16[2,1024,512]{2,1,0:T(8,128)(2,1)S(1)}, bf16[2,1024,512]{2,1,0:T(8,128)(2,1)}, u32[]{:S(2)}) copy-start(bf16[2,1024,512]{2,1,0:T(8,128)(2,1)} %param.10) | copy-start | bytes 6291460
  155.4 3.0 %copy-start.1 = (bf16[32,32,2,1024]{3,1,0,2:T(8,128)(2,1)S(1)}, bf16[32,32,2,1024]{3,1,0,2:T(8,128)(2,1)}, u32[]{:S(2)}) copy-start(bf16[32,32,2,1024]{3,1,0,2:T(8,128)(2,1)} %copy-done) | copy-start | bytes 12582916
  155.4 3.5 %copy-start.15 = (f32[1024,512]{1,0:T(8,128)S(1)}, f32[1024,512]{1,0:T(8,128)}, u32[]{:S(2)}) copy-start(f32[1024,512]{1,0:T(8,128)} %copy-done.14) | copy-start | bytes 6291460
  158.9 2.2 copy-start.3
  158.9 2.9 %copy-start.17 = (f32[1024,512]{1,0:T(8,128)S(1)}, f32[1024,512]{1,0:T(8,128)}, u32[]{:S(2)}) copy-start(f32[1024,512]{1,0:T(8,128)} %copy-done.16) | copy-start | bytes 6291460
  165.9 30.9 %all-to-all-start.1 = ((bf16[1,32,32,128]{3,2,0,1:T(8,128)(2,1)}), bf16[1,32,32,128]{3,2,0,1:T(8,128)(2,1)S(1)}, u32[]{:S(2)}, u32[]{:S(2)}) async-start(bf16[1,32,32,128]{3,2,0,1:T(8,128)(2,1)} %bitcast.6), calls=%async_computation.1 | async-start | bytes 524288 | tf_op jit(solution)/shard_map/all_to_all | solution.py:48
  196.9 20.9 %all-to-all-start.3 = ((bf16[1,32,32,128]{3,2,0,1:T(8,128)(2,1)}), bf16[1,32,32,128]{3,2,0,1:T(8,128)(2,1)S(1)}, u32[]{:S(2)}, u32[]{:S(2)}) async-start(bf16[1,32,32,128]{3,2,0,1:T(8,128)(2,1)} %bitcast.14), calls=%async_computation.3 | async-start | bytes 524288 | tf_op jit(solution)/shard_map/all_to_all | solution.py:48
  208.8 2.8 %copy-start.5 = (bf16[1,512,1024]{2,1,0:T(8,128)(2,1)S(1)}, bf16[1,512,1024]{2,1,0:T(8,128)(2,1)}, u32[]{:S(2)}) copy-start(bf16[1,512,1024]{2,1,0:T(8,128)(2,1)} %fusion.16) | copy-start | bytes 3145732
  (3 other events, 3.2 us)
Sparse Core Ops, SparseCore 0:
  102.4 41.0 reduce-scatter.6
  154.4 40.6 reduce-scatter.8

commit v3 on v0

v3 whole, which is shorter than its diff:
```python
import jax
import jax.numpy as jnp
from jax import lax
from jax.sharding import PartitionSpec as P


def expert_math(routed_in, routed_grad, w_in, w_out):
    pre_act = jnp.dot(routed_in, w_in, preferred_element_type=jnp.float32)
    gate_sig = jax.nn.sigmoid(pre_act)
    back_grad = lax.dot_general(
        routed_grad, w_out, (((1,), (1,)), ((), ())), preferred_element_type=jnp.float32
    )
    pre_grad = (back_grad * gate_sig * (1.0 + pre_act * (1.0 - gate_sig))).astype(jnp.bfloat16)
    partial_value = lax.dot_general(
        pre_grad, w_in, (((1,), (1,)), ((), ())), preferred_element_type=jnp.float32
    ).astype(jnp.bfloat16)
    hidden_act = (pre_act * gate_sig).astype(jnp.bfloat16)
    grad_wout = lax.dot_general(
        hidden_act, routed_grad, (((0,), (0,)), ((), ())), preferred_element_type=jnp.float32
    ).astype(jnp.bfloat16)
    grad_win = lax.dot_general(
        routed_in, pre_grad, (((0,), (0,)), ((), ())), preferred_element_type=jnp.float32
    ).astype(jnp.bfloat16)
    return partial_value, grad_win, grad_wout


def on_device(tokens, grad_out, region_ids, slot_ids, weight_in, weight_out):
    owners = lax.axis_size("dp")
    splits = lax.axis_size("expert")
    local_count = weight_in.shape[0]
    model_width = tokens.shape[1]
    tok_rows = tokens.shape[0]
    experts_all = local_count * owners
    capacity = 4 * tok_rows // experts_all
    where_to = region_ids * capacity + slot_ids
    both = jnp.concatenate([tokens, grad_out], axis=1)
    band = 2 * model_width // splits
    my_band = lax.dynamic_slice_in_dim(both, lax.axis_index("expert") * band, band, axis=1)

    rows = jnp.arange(owners * capacity, dtype=jnp.int32)
    owner_of = rows // capacity
    slot_of = rows % capacity

    def pick_for(local):
        expert_of = owner_of * local_count + local
        return (
            (region_ids[None, :] == expert_of[:, None]) & (slot_ids[None, :] == slot_of[:, None])
        ).astype(jnp.bfloat16)

    sent_b = jnp.dot(pick_for(1), my_band, preferred_element_type=jnp.float32).astype(
        jnp.bfloat16
    )
    got_b = lax.all_to_all(
        sent_b.reshape(owners, capacity, band), "dp", split_axis=0, concat_axis=1, tiled=True
    )[0]
    full_b = lax.all_gather(got_b, "expert", axis=1, tiled=True)
    sent_a = jnp.dot(pick_for(0), both, preferred_element_type=jnp.float32).astype(jnp.bfloat16)
    got_a = lax.all_to_all(
        sent_a.reshape(owners, capacity, 2 * model_width),
        "dp",
        split_axis=0,
        concat_axis=1,
        tiled=True,
    )[0]

    outs = []
    for local, got in ((0, got_a), (1, full_b)):
        outs.append(
            expert_math(
                got[:, :model_width], got[:, model_width:], weight_in[local], weight_out[local]
            )
        )
    partial_value = jnp.stack([o[0] for o in outs])
    summed = lax.psum_scatter(partial_value, "expert", scatter_dimension=2, tiled=True)
    back_rows = lax.all_to_all(
        summed.reshape(1, local_count, owners, capacity, summed.shape[2]),
        "dp",
        split_axis=2,
        concat_axis=0,
        tiled=True,
    )
    grad_tokens = back_rows.reshape(experts_all * capacity, summed.shape[2])[where_to]
    grad_win = jnp.stack([o[1] for o in outs])
    grad_wout = jnp.stack([o[2] for o in outs])
    return (grad_tokens, grad_win, grad_wout)


def solution(mesh):
    in_specs = (
        P("dp", None),
        P("dp", None),
        P("dp"),
        P("dp"),
        P("dp", None, "expert"),
        P("dp", "expert", None),
    )
    out_specs = (P("dp", "expert"), P("dp", None, "expert"), P("dp", "expert", None))
    return jax.shard_map(
        on_device, mesh=mesh, in_specs=in_specs, out_specs=out_specs, check_vma=False
    )
```

time: 256 us -> 206 us (0.80)
  waiting for transfers between devices: 149 us -> 50.2 us
  blocking collectives: 0 us -> 74.2 us
  starting transfers between devices: 23.5 us -> 7.67 us
  local copies, waits for them, and re-layouts: 43.7 us -> 29.4 us
  other arithmetic: 0.86 us -> 5.37 us
    all_to_all x3 -> x1, waiting for transfers between devices: 98.2 us -> 5.43 us  [on_device(): lax.all_to_all(summed.reshape(1, local_count, owners, capacity, summed.sh...]
    all_to_all x0 -> x2, blocking collectives: none -> 74.2 us  [the longest x1 54.2 us: on_device(): lax.all_to_all(sent_a.reshape(owners, capacity, 2 * model_width), 'dp', s...]
    all_to_all x3 -> x1, starting transfers between devices: 23.3 us -> 7.58 us  [on_device(): lax.all_to_all(summed.reshape(1, local_count, owners, capacity, summed.sh...]
    scatter x2 -> x0, local copies, waits for them, and re-layouts: 11.8 us -> none  [on_device(): jnp.zeros((experts_all * capacity, model_width), jnp.bfloat16).at[where_to]]
    all_to_all x3 -> x0, local copies, waits for them, and re-layouts: 7.83 us -> none  [the longest x1 4.93 us: on_device(): lax.all_to_all(send_in, 'dp', split_axis=0, concat_axis=2, tiled=True)]
    unnamed x2 -> x3, waiting for transfers between devices: 50.5 us -> 44.7 us
    unnamed x16 -> x43, local copies, waits for them, and re-layouts: 20.9 us -> 26.5 us
    another operation x0 -> x3, other arithmetic: none -> 5.35 us  [the longest x1 2.35 us: on_device(): partial_value = jnp.stack([o[0] for o in outs])]
  transfers between devices with their start and end apart: 4 -> 3, of which waited for: 4 -> 2; matrix products, arithmetic and copies ran while one was open for 10% -> 10% of each run, Pallas kernels for 0% -> 0%
where the time goes in v3:
time: 206 us; the launch traced here: 205 us
  blocking collectives  74.2 us (36%)
  waiting for transfers between devices  50.2 us (24%)
  local copies, waits for them, and re-layouts  29.4 us (14%)
  matrix products  24.2 us (12%)
  between operations  14.3 us (7%)
  starting transfers between devices  7.67 us (4%)
  other arithmetic  5.37 us (3%)
    all_to_all x1, blocking collectives, on_device(): lax.all_to_all(sent_a.reshape(owners, capacity, 2 * model_width), 'dp', s...  54.2 us
    unnamed x3, waiting for transfers between devices  44.7 us
    unnamed x43, local copies, waits for them, and re-layouts  26.5 us
    all_to_all x1, blocking collectives, on_device(): lax.all_to_all(sent_b.reshape(owners, capacity, band), 'dp', split_axis=0...  20.1 us
    all_to_all x1, starting transfers between devices, on_device(): lax.all_to_all(summed.reshape(1, local_count, owners, capacity, summed.sh...  7.58 us
    dot_general x2, matrix products, expert_math(): lax.dot_general(routed_in, pre_grad, (((0,), (0,)), ((), ())), preferred_...  6.16 us
    all_to_all x1, waiting for transfers between devices, on_device(): lax.all_to_all(summed.reshape(1, local_count, owners, capacity, summed.sh...  5.43 us
    dot_general x2, matrix products, expert_math(): pre_act = jnp.dot(routed_in, w_in, preferred_element_type=jnp.float32)  4.51 us
  transfers between devices with their start and end apart: 3, of which 2 were waited for; matrix products, arithmetic and copies ran while one was open for 10% of the time, Pallas kernels for 0%

profile of v3, /device:TPU:1, one launch (start us, length us, event | category | flops | bytes accessed | tf_op | source)
XLA Modules:
  0.0 205.4 jit_solution(8638458743335659562)
XLA Ops:
  7.3 1.4 constant_dynamic-update-slice_fusion.1
  9.8 20.1 %all_to_all.33 = bf16[32,32,256]{2,1,0:T(8,128)(2,1)} all-to-all(bf16[32,32,256]{2,1,0:T(8,128)(2,1)S(1)} %bitcast.62), channel_id=1, replica_groups=mesh['dp'=32,'expert'=8] {'dp'}, dimensions={0} | all-to-all | bytes 1048576 | tf_op jit(solution)/shard_map/all_to_all | solution.py:53
  29.9 2.8 %convolution_convert_fusion = bf16[1024,2048]{1,0:T(8,128)(2,1)S(1)} fusion(bf16[512,2048]{1,0:T(8,128)(2,1)S(1)} %constant_dynamic-update-slice_fusion, s32[512]{0:T(512)S(1)} %copy-done.4, s32[512]{0:T(512)S(1)} %copy-done.5, s32[1024]{0:T(1024)S(1)} %get-tuple-element.3, s32[1024]{0:T(1024)S(1)} %fusion.81), kind=kOutput, calls=%fused_computation.2 | convolution fusion | flops 2151153664 | bytes 6303744 | tf_op jit(solution)/shard_map/dot_general | solution.py:57
  32.8 54.2 %all_to_all.34 = bf16[32,32,2048]{2,1,0:T(8,128)(2,1)S(1)} all-to-all(bf16[32,32,2048]{2,1,0:T(8,128)(2,1)S(1)} %bitcast.58), channel_id=1, replica_groups=mesh['dp'=32,'expert'=8] {'dp'}, dimensions={0} | all-to-all | bytes 8388608 | tf_op jit(solution)/shard_map/all_to_all | solution.py:58
  86.9 1.2 fusion.13
  90.1 1.8 multiply_convert_fusion.3
  91.9 1.3 convert_bitcast_fusion.1
  93.2 3.3 %fusion.5 = f32[1024,512]{1,0:T(8,128)S(1)} fusion(bf16[1024,2048]{1,0:T(8,128)(2,1)} %all-gather.2.cloned.1.call-done, bf16[2,1024,512]{2,1,0:T(8,128)(2,1)} %param.10), kind=kOutput, calls=%fused_computation.20 | convolution fusion | flops 1073741824 | bytes 5242880 | tf_op jit(solution)/shard_map/dot_general | solution.py:8
  97.0 1.8 multiply_convert_fusion.2
  99.4 1.3 convert_bitcast_fusion
  100.7 2.3 %pad_maximum_fusion = bf16[2,1024,1024]{2,1,0:T(8,128)(2,1)} fusion(bf16[1,1024,1024]{2,1,0:T(8,128)(2,1)S(1)} %convert_bitcast_fusion, bf16[1,1024,1024]{2,1,0:T(8,128)(2,1)S(1)} %convert_bitcast_fusion.1), kind=kLoop, calls=%fused_computation.1 | loop fusion | flops 2097152 | bytes 8388608 | tf_op jit(solution)/shard_map/stack | solution.py:73
  103.0 11.4 %copy.11 = bf16[2,1024,1024]{1,0,2:T(2,128)(2,1)} copy(bf16[2,1024,1024]{2,1,0:T(8,128)(2,1)} %pad_maximum_fusion) | data formatting | bytes 8388608
  114.4 5.6 %copy.13 = bf16[128,8,2,1024]{3,1,2,0:T(8,128)(2,1)} copy(bf16[128,8,2,1024]{3,2,1,0:T(2,128)(2,1)} %bitcast.52) | data formatting | bytes 8388608
  121.2 3.0 %fusion.37 = bf16[1,1024,512]{2,1,0:T(8,128)(2,1)S(1)} fusion(bf16[1024,512]{1,0:T(8,128)(2,1)S(1)} %copy-done.18, bf16[1024,2048]{1,0:T(8,128)(2,1)} %bitcast.56), kind=kOutput, calls=%fused_computation.40 | convolution fusion | flops 1074266112 | bytes 4194304 | tf_op jit(solution)/shard_map/dot_general | solution.py:21
  124.7 1.3 fusion.40
  127.6 2.3 %fusion.34 = bf16[1,512,1024]{2,1,0:T(8,128)(2,1)} fusion(bf16[1024,2048]{1,0:T(8,128)(2,1)S(1)} %copy-done.7, f32[1024,512]{1,0:T(8,128)S(1)} %copy-done.15), kind=kOutput, calls=%fused_computation.39 | convolution fusion | flops 1076887552 | bytes 5242880 | tf_op jit(solution)/shard_map/dot_general | solution.py:18
  129.9 44.7 %reduce-scatter.4.cloned.1.call-done = bf16[128,2048]{1,0:T(8,128)(2,1)} async-done(((bf16[1024,2048]{1,0:T(8,128)(2,1)}), bf16[128,2048]{1,0:T(8,128)(2,1)}) %reduce-scatter.4.cloned.1.call-update) | async-done | bytes 524304
  174.6 1.4 reshape.69
  177.4 7.6 %all-to-all-start.2 = ((bf16[1,2,32,32,128]{4,3,1,0,2:T(8,128)(2,1)}), bf16[1,2,32,32,128]{4,3,1,0,2:T(8,128)(2,1)S(1)}, u32[]{:S(2)}, u32[]{:S(2)}) async-start(bf16[1,2,32,32,128]{4,3,1,0,2:T(8,128)(2,1)} %copy.10), calls=%async_computation.2 | async-start | bytes 1048576 | tf_op jit(solution)/shard_map/all_to_all | solution.py:75
  185.0 3.1 %fusion.31 = bf16[1,1024,512]{2,1,0:T(8,128)(2,1)S(1)} fusion(bf16[1024,512]{1,0:T(8,128)(2,1)} %copy-done.16, bf16[1024,2048]{1,0:T(8,128)(2,1)} %all-gather.2.cloned.1.call-done), kind=kOutput, calls=%fused_computation.38 | convolution fusion | flops 1074266112 | bytes 4194304 | tf_op jit(solution)/shard_map/dot_general | solution.py:21
  188.2 1.5 pad_maximum_fusion.1
  189.7 1.5 pad_maximum_fusion.2
  191.2 5.4 %all-to-all-done.2 = bf16[1,2,32,32,128]{4,3,1,0,2:T(8,128)(2,1)S(1)} async-done(((bf16[1,2,32,32,128]{4,3,1,0,2:T(8,128)(2,1)}), bf16[1,2,32,32,128]{4,3,1,0,2:T(8,128)(2,1)S(1)}, u32[]{:S(2)}, u32[]{:S(2)}) %all-to-all-start.2) | async-done | bytes 524320 | tf_op jit(solution)/shard_map/all_to_all | solution.py:75
  196.6 1.9 gather_fusion
  (51 shorter events, 8.8 us)
Async XLA Ops:
  7.2 1.5 copy-start.2
  7.2 86.0 %all-gather.2.cloned.1.call-start = ((), (), s32[]{:S(2)}) async-start(), calls=%async_computation.4 | async-start | bytes 4718592 | tf_op jit(solution)/shard_map/all_gather | solution.py:56
  7.2 1.6 copy-start.4
  7.3 1.6 copy-start.5
  29.9 144.7 %reduce-scatter.4.cloned.1.call-start = ((), (), s32[]{:S(2)}) async-start(), calls=%async_computation.5 | async-start | bytes 4718592
  32.8 54.2 %copy-start.10 = (bf16[2,1024,512]{2,1,0:T(8,128)(2,1)S(1)}, bf16[2,1024,512]{2,1,0:T(8,128)(2,1)}, u32[]{:S(2)}) copy-start(bf16[2,1024,512]{2,1,0:T(8,128)(2,1)} %param.10) | copy-start | bytes 6291460
  86.9 2.1 %copy-start = (bf16[32,32,2048]{2,1,0:T(8,128)(2,1)}, bf16[32,32,2048]{2,1,0:T(8,128)(2,1)S(1)}, u32[]{:S(2)}) copy-start(bf16[32,32,2048]{2,1,0:T(8,128)(2,1)S(1)} %all_to_all.34) | copy-start | bytes 12582916
  86.9 3.1 %copy-start.8 = (bf16[2,512,1024]{2,1,0:T(8,128)(2,1)S(1)}, bf16[2,512,1024]{2,1,0:T(8,128)(2,1)}, u32[]{:S(2)}) copy-start(bf16[2,512,1024]{2,1,0:T(8,128)(2,1)} %param.11) | copy-start | bytes 6291460
  90.1 1.8 copy-start.12
  91.9 1.3 copy-start.17
  93.2 3.3 %copy-start.6 = (bf16[1024,2048]{1,0:T(8,128)(2,1)S(1)}, bf16[1024,2048]{1,0:T(8,128)(2,1)}, u32[]{:S(2)}) copy-start(bf16[1024,2048]{1,0:T(8,128)(2,1)} %all-gather.2.cloned.1.call-done) | copy-start | bytes 12582916
  93.2 3.8 %copy-start.9 = (bf16[2,512,1024]{2,1,0:T(8,128)(2,1)S(1)}, bf16[2,512,1024]{2,1,0:T(8,128)(2,1)}, u32[]{:S(2)}) copy-start(bf16[2,512,1024]{2,1,0:T(8,128)(2,1)} %param.11) | copy-start | bytes 6291460
  97.0 1.8 copy-start.14
  97.0 2.3 %copy-start.11 = (bf16[2,1024,512]{2,1,0:T(8,128)(2,1)S(1)}, bf16[2,1024,512]{2,1,0:T(8,128)(2,1)}, u32[]{:S(2)}) copy-start(bf16[2,1024,512]{2,1,0:T(8,128)(2,1)} %param.10) | copy-start | bytes 6291460
  99.4 1.3 copy-start.16
  120.0 1.2 copy-start.18
  121.2 3.0 %copy-start.1 = (bf16[32,32,2048]{2,1,0:T(8,128)(2,1)S(1)}, bf16[32,32,2048]{2,1,0:T(8,128)(2,1)}, u32[]{:S(2)}) copy-start(bf16[32,32,2048]{2,1,0:T(8,128)(2,1)} %copy-done) | copy-start | bytes 12582916
  121.2 3.5 %copy-start.13 = (f32[1024,512]{1,0:T(8,128)S(1)}, f32[1024,512]{1,0:T(8,128)}, u32[]{:S(2)}) copy-start(f32[1024,512]{1,0:T(8,128)} %copy-done.12) | copy-start | bytes 6291460
  124.7 2.2 %copy-start.7 = (bf16[1024,2048]{1,0:T(8,128)(2,1)S(1)}, bf16[1024,2048]{1,0:T(8,128)(2,1)}, u32[]{:S(2)}) copy-start(bf16[1024,2048]{1,0:T(8,128)(2,1)} %all-gather.2.cloned.1.call-done) | copy-start | bytes 12582916
  124.7 2.9 %copy-start.15 = (f32[1024,512]{1,0:T(8,128)S(1)}, f32[1024,512]{1,0:T(8,128)}, u32[]{:S(2)}) copy-start(f32[1024,512]{1,0:T(8,128)} %copy-done.14) | copy-start | bytes 6291460
  177.4 19.2 %all-to-all-start.2 = ((bf16[1,2,32,32,128]{4,3,1,0,2:T(8,128)(2,1)}), bf16[1,2,32,32,128]{4,3,1,0,2:T(8,128)(2,1)S(1)}, u32[]{:S(2)}, u32[]{:S(2)}) async-start(bf16[1,2,32,32,128]{4,3,1,0,2:T(8,128)(2,1)} %copy.10), calls=%async_computation.2 | async-start | bytes 1048576 | tf_op jit(solution)/shard_map/all_to_all | solution.py:75
  188.2 1.5 copy-start.3
Sparse Core Ops, SparseCore 0:
  30.0 57.1 all-gather.1
  120.2 54.4 reduce-scatter.3

commit v4 on v3

--- a/solution.py
+++ b/solution.py
@@ -1,6 +1,7 @@
 import jax
 import jax.numpy as jnp
 from jax import lax
+from jax.experimental.layout import Layout, with_layout_constraint
 from jax.sharding import PartitionSpec as P
 
 
@@ -12,7 +13,7 @@
     )
     pre_grad = (back_grad * gate_sig * (1.0 + pre_act * (1.0 - gate_sig))).astype(jnp.bfloat16)
     partial_value = lax.dot_general(
-        pre_grad, w_in, (((1,), (1,)), ((), ())), preferred_element_type=jnp.float32
+        w_in, pre_grad, (((1,), (1,)), ((), ())), preferred_element_type=jnp.float32
     ).astype(jnp.bfloat16)
     hidden_act = (pre_act * gate_sig).astype(jnp.bfloat16)
     grad_wout = lax.dot_general(
@@ -70,16 +71,19 @@
                 got[:, :model_width], got[:, model_width:], weight_in[local], weight_out[local]
             )
         )
-    partial_value = jnp.stack([o[0] for o in outs])
-    summed = lax.psum_scatter(partial_value, "expert", scatter_dimension=2, tiled=True)
+    partial_value = jnp.concatenate([o[0] for o in outs], axis=1)
+    partial_value = with_layout_constraint(partial_value, Layout(major_to_minor=(0, 1)))
+    summed = lax.psum_scatter(partial_value, "expert", scatter_dimension=0, tiled=True)
+    cols = summed.shape[0]
     back_rows = lax.all_to_all(
-        summed.reshape(1, local_count, owners, capacity, summed.shape[2]),
+        summed.reshape(1, cols, local_count, owners, capacity),
         "dp",
-        split_axis=2,
+        split_axis=3,
         concat_axis=0,
         tiled=True,
     )
-    grad_tokens = back_rows.reshape(experts_all * capacity, summed.shape[2])[where_to]
+    back_rows = jnp.transpose(back_rows[:, :, :, 0, :], (0, 2, 3, 1))
+    grad_tokens = back_rows.reshape(experts_all * capacity, cols)[where_to]
     grad_win = jnp.stack([o[1] for o in outs])
     grad_wout = jnp.stack([o[2] for o in outs])
     return (grad_tokens, grad_win, grad_wout)

time: 206 us -> 189 us (0.917)
  local copies, waits for them, and re-layouts: 29.4 us -> 11.1 us
    reduce_scatter x0 -> x1, waiting for transfers between devices: none -> 45.9 us  [on_device(): lax.psum_scatter(partial_value, 'expert', scatter_dimension=0, tiled=True)]
    unnamed x3 -> x2, waiting for transfers between devices: 44.7 us -> 0.03 us
    unnamed x43 -> x35, local copies, waits for them, and re-layouts: 26.5 us -> 6.88 us
    concatenate x0 -> x1, other arithmetic: none -> 2.36 us  [on_device(): partial_value = jnp.concatenate([o[0] for o in outs], axis=1)]
    another operation x1 -> x0, other arithmetic: 2.35 us -> none  [on_device(): partial_value = jnp.stack([o[0] for o in outs])]
  transfers between devices with their start and end apart: 3 -> 3, of which waited for: 2 -> 2; matrix products, arithmetic and copies ran while one was open for 10% -> 11% of each run, Pallas kernels for 0% -> 0%
where the time goes in v4:
time: 189 us; the launch traced here: 188 us
  blocking collectives  74.2 us (39%)
  waiting for transfers between devices  51.4 us (27%)
  matrix products  24.2 us (13%)
  between operations  14.3 us (8%)
  local copies, waits for them, and re-layouts  11.1 us (6%)
  starting transfers between devices  7.66 us (4%)
  other arithmetic  5.38 us (3%)
    all_to_all x1, blocking collectives, on_device(): lax.all_to_all(sent_a.reshape(owners, capacity, 2 * model_width), 'dp', s...  54.2 us
    reduce_scatter x1, waiting for transfers between devices, on_device(): lax.psum_scatter(partial_value, 'expert', scatter_dimension=0, tiled=True)  45.9 us
    all_to_all x1, blocking collectives, on_device(): lax.all_to_all(sent_b.reshape(owners, capacity, band), 'dp', split_axis=0...  20.1 us
    all_to_all x1, starting transfers between devices, on_device(): lax.all_to_all(summed.reshape(1, cols, local_count, owners, capacity), 'd...  7.58 us
    unnamed x35, local copies, waits for them, and re-layouts  6.88 us
    dot_general x2, matrix products, expert_math(): lax.dot_general(routed_in, pre_grad, (((0,), (0,)), ((), ())), preferred_...  6.16 us
    all_to_all x1, waiting for transfers between devices, on_device(): lax.all_to_all(summed.reshape(1, cols, local_count, owners, capacity), 'd...  5.44 us
    dot_general x2, matrix products, expert_math(): pre_act = jnp.dot(routed_in, w_in, preferred_element_type=jnp.float32)  4.5 us
  transfers between devices with their start and end apart: 3, of which 2 were waited for; matrix products, arithmetic and copies ran while one was open for 11% of the time, Pallas kernels for 0%

profile of v4, /device:TPU:1, one launch (start us, length us, event | category | flops | bytes accessed | tf_op | source)
XLA Modules:
  0.0 188.3 jit_solution(3780821241042965144)
XLA Ops:
  7.3 1.4 constant_dynamic-update-slice_fusion.1
  9.8 20.1 %all_to_all.33 = bf16[32,32,256]{2,1,0:T(8,128)(2,1)} all-to-all(bf16[32,32,256]{2,1,0:T(8,128)(2,1)S(1)} %bitcast.59), channel_id=1, replica_groups=mesh['dp'=32,'expert'=8] {'dp'}, dimensions={0} | all-to-all | bytes 1048576 | tf_op jit(solution)/shard_map/all_to_all | solution.py:54
  29.9 2.9 %convolution_convert_fusion = bf16[1024,2048]{1,0:T(8,128)(2,1)S(1)} fusion(bf16[512,2048]{1,0:T(8,128)(2,1)S(1)} %constant_dynamic-update-slice_fusion, s32[512]{0:T(512)S(1)} %copy-done.4, s32[512]{0:T(512)S(1)} %copy-done.5, s32[1024]{0:T(1024)S(1)} %get-tuple-element.3, s32[1024]{0:T(1024)S(1)} %fusion.81), kind=kOutput, calls=%fused_computation.2 | convolution fusion | flops 2151153664 | bytes 6303744 | tf_op jit(solution)/shard_map/dot_general | solution.py:58
  32.8 54.2 %all_to_all.34 = bf16[32,32,2048]{2,1,0:T(8,128)(2,1)S(1)} all-to-all(bf16[32,32,2048]{2,1,0:T(8,128)(2,1)S(1)} %bitcast.56), channel_id=1, replica_groups=mesh['dp'=32,'expert'=8] {'dp'}, dimensions={0} | all-to-all | bytes 8388608 | tf_op jit(solution)/shard_map/all_to_all | solution.py:59
  87.0 1.2 fusion.13
  89.1 1.0 copy-done.8
  90.1 1.8 multiply_convert_fusion.3
  91.9 1.3 convert_bitcast_fusion.1
  93.3 3.3 %fusion.5 = f32[1024,512]{1,0:T(8,128)S(1)} fusion(bf16[1024,2048]{1,0:T(8,128)(2,1)} %all-gather.2.cloned.1.call-done, bf16[2,1024,512]{2,1,0:T(8,128)(2,1)} %param.10), kind=kOutput, calls=%fused_computation.20 | convolution fusion | flops 1073741824 | bytes 5242880 | tf_op jit(solution)/shard_map/dot_general | solution.py:9
  97.1 1.8 multiply_convert_fusion.2
  98.9 1.0 copy-done.16
  99.9 1.3 convert_bitcast_fusion
  101.2 2.4 %pad_maximum_fusion = bf16[1024,2048]{1,0:T(8,128)(2,1)} fusion(bf16[1024,1024]{1,0:T(8,128)(2,1)S(1)} %convert_bitcast_fusion, bf16[1024,1024]{1,0:T(8,128)(2,1)S(1)} %convert_bitcast_fusion.1), kind=kLoop, calls=%fused_computation.1 | loop fusion | flops 8388608 | bytes 8388608 | tf_op jit(solution)/shard_map/concatenate | solution.py:74
  103.6 3.0 %fusion.37 = bf16[1,1024,512]{2,1,0:T(8,128)(2,1)S(1)} fusion(bf16[1024,512]{1,0:T(8,128)(2,1)S(1)} %multiply_convert_fusion.3, bf16[1024,2048]{1,0:T(8,128)(2,1)} %bitcast.54), kind=kOutput, calls=%fused_computation.40 | convolution fusion | flops 1074266112 | bytes 4194304 | tf_op jit(solution)/shard_map/dot_general | solution.py:22
  107.1 1.3 fusion.40
  110.0 2.3 %fusion.34 = bf16[1,512,1024]{2,1,0:T(8,128)(2,1)} fusion(bf16[1024,2048]{1,0:T(8,128)(2,1)S(1)} %copy-done.7, f32[1024,512]{1,0:T(8,128)S(1)} %copy-done.15), kind=kOutput, calls=%fused_computation.39 | convolution fusion | flops 1076887552 | bytes 5242880 | tf_op jit(solution)/shard_map/dot_general | solution.py:19
  112.3 45.9 %reduce-scatter.2.cloned.1.call-done = bf16[128,2048]{1,0:T(8,128)(2,1)} async-done(((bf16[1024,2048]{1,0:T(8,128)(2,1)}), bf16[128,2048]{1,0:T(8,128)(2,1)}) %reduce-scatter.2.cloned.1.call-update) | async-done | bytes 524304 | tf_op jit(solution)/shard_map/reduce_scatter | solution.py:76
  158.1 1.3 copy.18
  160.3 7.6 %all-to-all-start.2 = ((bf16[1,128,2,32,32]{1,4,2,0,3:T(8,128)(2,1)}), bf16[1,128,2,32,32]{1,4,2,0,3:T(8,128)(2,1)S(1)}, u32[]{:S(2)}, u32[]{:S(2)}) async-start(bf16[1,128,2,32,32]{1,4,2,0,3:T(8,128)(2,1)} %copy.19), calls=%async_computation.3 | async-start | bytes 1048576 | tf_op jit(solution)/shard_map/all_to_all | solution.py:78
  167.9 3.1 %fusion.31 = bf16[1,1024,512]{2,1,0:T(8,128)(2,1)S(1)} fusion(bf16[1024,512]{1,0:T(8,128)(2,1)} %copy-done.16, bf16[1024,2048]{1,0:T(8,128)(2,1)} %all-gather.2.cloned.1.call-done), kind=kOutput, calls=%fused_computation.38 | convolution fusion | flops 1074266112 | bytes 4194304 | tf_op jit(solution)/shard_map/dot_general | solution.py:22
  171.1 1.5 pad_maximum_fusion.1
  172.6 1.5 pad_maximum_fusion.2
  174.1 5.4 %all-to-all-done.2 = bf16[1,128,2,32,32]{1,4,2,0,3:T(8,128)(2,1)S(1)} async-done(((bf16[1,128,2,32,32]{1,4,2,0,3:T(8,128)(2,1)}), bf16[1,128,2,32,32]{1,4,2,0,3:T(8,128)(2,1)S(1)}, u32[]{:S(2)}, u32[]{:S(2)}) %all-to-all-start.2) | async-done | bytes 524320 | tf_op jit(solution)/shard_map/all_to_all | solution.py:78
  179.5 1.9 %gather_fusion = bf16[512,128]{1,0:T(8,128)(2,1)} fusion(bf16[2048,128]{1,0:T(8,128)(2,1)S(1)} %bitcast.51, s32[1024]{0:T(1024)S(1)} %pad_clamp_fusion), kind=kCustom, calls=%fused_computation | custom fusion | bytes 264192 | tf_op jit(solution)/shard_map/gather | solution.py:86
  (44 shorter events, 5.6 us)
Async XLA Ops:
  7.2 1.5 copy-start.2
  7.2 86.0 %all-gather.2.cloned.1.call-start = ((), (), s32[]{:S(2)}) async-start(), calls=%async_computation.4 | async-start | bytes 4718592 | tf_op jit(solution)/shard_map/all_gather | solution.py:57
  7.2 1.6 copy-start.4
  7.3 1.6 copy-start.5
  29.9 128.3 %reduce-scatter.2.cloned.1.call-start = ((), (), s32[]{:S(2)}) async-start(), calls=%async_computation.5 | async-start | bytes 4718592 | tf_op jit(solution)/shard_map/reduce_scatter | solution.py:76
  32.8 54.2 %copy-start.10 = (bf16[2,1024,512]{2,1,0:T(8,128)(2,1)S(1)}, bf16[2,1024,512]{2,1,0:T(8,128)(2,1)}, u32[]{:S(2)}) copy-start(bf16[2,1024,512]{2,1,0:T(8,128)(2,1)} %param.10) | copy-start | bytes 6291460
  87.0 2.1 %copy-start = (bf16[32,32,2048]{2,1,0:T(8,128)(2,1)}, bf16[32,32,2048]{2,1,0:T(8,128)(2,1)S(1)}, u32[]{:S(2)}) copy-start(bf16[32,32,2048]{2,1,0:T(8,128)(2,1)S(1)} %all_to_all.34) | copy-start | bytes 12582916
  87.0 3.1 %copy-start.8 = (bf16[2,512,1024]{2,1,0:T(8,128)(2,1)S(1)}, bf16[2,512,1024]{2,1,0:T(8,128)(2,1)}, u32[]{:S(2)}) copy-start(bf16[2,512,1024]{2,1,0:T(8,128)(2,1)} %param.11) | copy-start | bytes 6291460
  90.1 1.8 copy-start.12
  93.2 3.3 %copy-start.6 = (bf16[1024,2048]{1,0:T(8,128)(2,1)S(1)}, bf16[1024,2048]{1,0:T(8,128)(2,1)}, u32[]{:S(2)}) copy-start(bf16[1024,2048]{1,0:T(8,128)(2,1)} %all-gather.2.cloned.1.call-done) | copy-start | bytes 12582916
  93.2 3.8 %copy-start.9 = (bf16[2,512,1024]{2,1,0:T(8,128)(2,1)S(1)}, bf16[2,512,1024]{2,1,0:T(8,128)(2,1)}, u32[]{:S(2)}) copy-start(bf16[2,512,1024]{2,1,0:T(8,128)(2,1)} %param.11) | copy-start | bytes 6291460
  97.0 1.8 copy-start.14
  97.0 2.8 %copy-start.11 = (bf16[2,1024,512]{2,1,0:T(8,128)(2,1)S(1)}, bf16[2,1024,512]{2,1,0:T(8,128)(2,1)}, u32[]{:S(2)}) copy-start(bf16[2,1024,512]{2,1,0:T(8,128)(2,1)} %param.10) | copy-start | bytes 6291460
  98.9 1.0 copy-start.16
  103.6 3.1 %copy-start.1 = (bf16[32,32,2048]{2,1,0:T(8,128)(2,1)S(1)}, bf16[32,32,2048]{2,1,0:T(8,128)(2,1)}, u32[]{:S(2)}) copy-start(bf16[32,32,2048]{2,1,0:T(8,128)(2,1)} %copy-done) | copy-start | bytes 12582916
  103.6 3.5 %copy-start.13 = (f32[1024,512]{1,0:T(8,128)S(1)}, f32[1024,512]{1,0:T(8,128)}, u32[]{:S(2)}) copy-start(f32[1024,512]{1,0:T(8,128)} %copy-done.12) | copy-start | bytes 6291460
  107.1 2.2 %copy-start.7 = (bf16[1024,2048]{1,0:T(8,128)(2,1)S(1)}, bf16[1024,2048]{1,0:T(8,128)(2,1)}, u32[]{:S(2)}) copy-start(bf16[1024,2048]{1,0:T(8,128)(2,1)} %all-gather.2.cloned.1.call-done) | copy-start | bytes 12582916
  107.1 2.9 %copy-start.15 = (f32[1024,512]{1,0:T(8,128)S(1)}, f32[1024,512]{1,0:T(8,128)}, u32[]{:S(2)}) copy-start(f32[1024,512]{1,0:T(8,128)} %copy-done.14) | copy-start | bytes 6291460
  160.3 19.2 %all-to-all-start.2 = ((bf16[1,128,2,32,32]{1,4,2,0,3:T(8,128)(2,1)}), bf16[1,128,2,32,32]{1,4,2,0,3:T(8,128)(2,1)S(1)}, u32[]{:S(2)}, u32[]{:S(2)}) async-start(bf16[1,128,2,32,32]{1,4,2,0,3:T(8,128)(2,1)} %copy.19), calls=%async_computation.3 | async-start | bytes 1048576 | tf_op jit(solution)/shard_map/all_to_all | solution.py:78
  171.1 1.5 copy-start.3
Sparse Core Ops, SparseCore 0:
  30.0 57.1 all-gather.1
  103.7 54.3 reduce-scatter.1

commit v5 on v4

--- a/solution.py
+++ b/solution.py
@@ -23,6 +23,27 @@
         routed_in, pre_grad, (((0,), (0,)), ((), ())), preferred_element_type=jnp.float32
     ).astype(jnp.bfloat16)
     return partial_value, grad_win, grad_wout
+
+
+def ring_reduce_scatter(x, axis):
+    n = lax.axis_size(axis)
+    me = lax.axis_index(axis)
+    blocks = x.reshape(n, x.shape[0] // n, x.shape[1])
+    half = x.shape[1] // 2
+    fwd = blocks[:, :, :half]
+    bwd = blocks[:, :, half:]
+    to_next = [(j, (j + 1) % n) for j in range(n)]
+    to_prev = [(j, (j - 1) % n) for j in range(n)]
+
+    def block(arr, idx):
+        return lax.dynamic_index_in_dim(arr, idx % n, axis=0, keepdims=False)
+
+    acc_f = block(fwd, me - 1)
+    acc_b = block(bwd, me + 1)
+    for k in range(1, n):
+        acc_f = lax.ppermute(acc_f, axis, to_next) + block(fwd, me - 1 - k)
+        acc_b = lax.ppermute(acc_b, axis, to_prev) + block(bwd, me + 1 + k)
+    return jnp.concatenate([acc_f, acc_b], axis=1)
 
 
 def on_device(tokens, grad_out, region_ids, slot_ids, weight_in, weight_out):
@@ -71,9 +92,12 @@
                 got[:, :model_width], got[:, model_width:], weight_in[local], weight_out[local]
             )
         )
-    partial_value = jnp.concatenate([o[0] for o in outs], axis=1)
-    partial_value = with_layout_constraint(partial_value, Layout(major_to_minor=(0, 1)))
-    summed = lax.psum_scatter(partial_value, "expert", scatter_dimension=0, tiled=True)
+    rows_major = Layout(major_to_minor=(0, 1))
+    part_a = with_layout_constraint(outs[0][0], rows_major)
+    part_b = with_layout_constraint(outs[1][0], rows_major)
+    summed_a = lax.psum_scatter(part_a, "expert", scatter_dimension=0, tiled=True)
+    summed_b = ring_reduce_scatter(part_b, "expert")
+    summed = jnp.concatenate([summed_a, summed_b], axis=1)
     cols = summed.shape[0]
     back_rows = lax.all_to_all(
         summed.reshape(1, cols, local_count, owners, capacity),

time: 189 us -> 205 us (1.085)
  blocking collectives: 74.2 us -> 20.1 us
  starting transfers between devices: 7.66 us -> 45.5 us
  waiting for transfers between devices: 51.4 us -> 82.6 us
  matrix products: 24.2 us -> 32.6 us
  local copies, waits for them, and re-layouts: 11.1 us -> 5.41 us
    all_to_all x1 -> x0, blocking collectives: 54.2 us -> none  [on_device(): lax.all_to_all(sent_a.reshape(owners, capacity, 2 * model_width), 'dp', s...]
    all_to_all x0 -> x1, waiting for transfers between devices: none -> 51.2 us  [on_device(): lax.all_to_all(sent_a.reshape(owners, capacity, 2 * model_width), 'dp', s...]
    reduce_scatter x1, waiting for transfers between devices: 45.9 us -> 0.02 us  [on_device(): lax.psum_scatter(part_a, 'expert', scatter_dimension=0, tiled=True)]
    ppermute x0 -> x14, starting transfers between devices: none -> 27.2 us  [the longest x7 26.4 us: ring_reduce_scatter(): acc_b = lax.ppermute(acc_b, axis, to_prev) + block(bwd, me + 1 + k)]
    ppermute x0 -> x14, waiting for transfers between devices: none -> 25.9 us  [the longest x7 21.3 us: ring_reduce_scatter(): acc_b = lax.ppermute(acc_b, axis, to_prev) + block(bwd, me + 1 + k)]
    all_to_all x1, starting transfers between devices: 7.58 us -> 13.2 us  [on_device(): lax.all_to_all(summed.reshape(1, cols, local_count, owners, capacity), 'd...]
    unnamed x35 -> x25, local copies, waits for them, and re-layouts: 6.88 us -> 2.02 us
    all_to_all x0 -> x1, starting transfers between devices: none -> 4.78 us  [on_device(): lax.all_to_all(sent_a.reshape(owners, capacity, 2 * model_width), 'dp', s...]
  transfers between devices with their start and end apart: 3 -> 18, of which waited for: 2 -> 13; matrix products, arithmetic and copies ran while one was open for 11% -> 17% of each run, Pallas kernels for 0% -> 0%
where the time goes in v5:
time: 205 us
  waiting for transfers between devices  82.6 us (40%)
  starting transfers between devices  45.5 us (22%)
  matrix products  32.6 us (16%)
  blocking collectives  20.1 us (10%)
  between operations  14.7 us (7%)
  local copies, waits for them, and re-layouts  5.41 us (3%)
  other arithmetic  4.24 us (2%)
    all_to_all x1, waiting for transfers between devices, on_device(): lax.all_to_all(sent_a.reshape(owners, capacity, 2 * model_width), 'dp', s...  51.2 us
    ppermute x7, starting transfers between devices, ring_reduce_scatter(): acc_b = lax.ppermute(acc_b, axis, to_prev) + block(bwd, me + 1 + k)  26.4 us
    ppermute x7, waiting for transfers between devices, ring_reduce_scatter(): acc_b = lax.ppermute(acc_b, axis, to_prev) + block(bwd, me + 1 + k)  21.3 us
    all_to_all x1, blocking collectives, on_device(): lax.all_to_all(sent_b.reshape(owners, capacity, band), 'dp', split_axis=0...  20.1 us
    all_to_all x1, starting transfers between devices, on_device(): lax.all_to_all(summed.reshape(1, cols, local_count, owners, capacity), 'd...  13.2 us
    dot_general x2, matrix products, expert_math(): pre_act = jnp.dot(routed_in, w_in, preferred_element_type=jnp.float32)  6.25 us
    dot_general x2, matrix products, expert_math(): lax.dot_general(routed_in, pre_grad, (((0,), (0,)), ((), ())), preferred_...  6.15 us
    dot_general x2, matrix products, expert_math(): lax.dot_general(routed_grad, w_out, (((1,), (1,)), ((), ())), preferred_e...  5.9 us
  transfers between devices with their start and end apart: 18, of which 13 were waited for; matrix products, arithmetic and copies ran while one was open for 17% of the time, Pallas kernels for 0%

profile of v5, /device:TPU:1, one launch (start us, length us, event | category | flops | bytes accessed | tf_op | source)
XLA Modules:
  0.0 205.0 jit_solution(8160034943950123551)
XLA Ops:
  9.8 20.1 %all_to_all.33 = bf16[32,32,256]{2,1,0:T(8,128)(2,1)} all-to-all(bf16[32,32,256]{2,1,0:T(8,128)(2,1)S(1)} %bitcast.89), channel_id=1, replica_groups=mesh['dp'=32,'expert'=8] {'dp'}, dimensions={0} | all-to-all | bytes 1048576 | tf_op jit(solution)/shard_map/all_to_all | solution.py:75
  29.9 4.2 %convolution_convert_fusion = bf16[1024,2048]{1,0:T(8,128)(2,1)} fusion(bf16[512,2048]{1,0:T(8,128)(2,1)S(1)} %constant_dynamic-update-slice_fusion, s32[512]{0:T(512)S(1)} %copy-done.2, s32[512]{0:T(512)S(1)} %copy-done.3, s32[1024]{0:T(1024)S(1)} %get-tuple-element.5, s32[1024]{0:T(1024)S(1)} %get-tuple-element.6), kind=kOutput, calls=%fused_computation.1 | convolution fusion | flops 2151153664 | bytes 6303744 | tf_op jit(solution)/shard_map/dot_general | solution.py:79
  34.1 4.8 %all-to-all-start = ((bf16[32,32,2048]{2,1,0:T(8,128)(2,1)}), bf16[32,32,2048]{2,1,0:T(8,128)(2,1)}, u32[]{:S(2)}, u32[]{:S(2)}) async-start(bf16[32,32,2048]{2,1,0:T(8,128)(2,1)} %bitcast.85), calls=%async_computation | async-start | bytes 8388608 | tf_op jit(solution)/shard_map/all_to_all | solution.py:80
  39.4 51.2 %all-to-all-done = bf16[32,32,2048]{2,1,0:T(8,128)(2,1)} async-done(((bf16[32,32,2048]{2,1,0:T(8,128)(2,1)}), bf16[32,32,2048]{2,1,0:T(8,128)(2,1)}, u32[]{:S(2)}, u32[]{:S(2)}) %all-to-all-start) | async-done | bytes 4194336 | tf_op jit(solution)/shard_map/all_to_all | solution.py:80
  90.6 3.0 %fusion.13 = f32[1024,512]{1,0:T(8,128)S(1)} fusion(bf16[1024,2048]{1,0:T(8,128)(2,1)} %bitcast.1, bf16[2,1024,512]{2,1,0:T(8,128)(2,1)S(1)} %copy-done.7), kind=kOutput, calls=%fused_computation.27 | convolution fusion | flops 1073741824 | bytes 5242880 | tf_op jit(solution)/shard_map/dot_general | solution.py:9
  93.6 4.1 %multiply_convert_fusion.3 = bf16[1024,512]{1,0:T(8,128)(2,1)S(1)} fusion(f32[1024,512]{1,0:T(8,128)S(1)} %fusion.13, bf16[2,512,1024]{2,1,0:T(8,128)(2,1)S(1)} %copy-done.5, bf16[1024,2048]{1,0:T(8,128)(2,1)} %bitcast.1), kind=kOutput, calls=%fused_computation.11 | convolution fusion | flops 1078460416 | bytes 6291456 | tf_op jit(solution)/shard_map/dot_general | solution.py:11
  100.3 3.0 %fusion.37 = bf16[1,1024,512]{2,1,0:T(8,128)(2,1)S(1)} fusion(bf16[1024,512]{1,0:T(8,128)(2,1)S(1)} %multiply_convert_fusion.3, bf16[1024,2048]{1,0:T(8,128)(2,1)} %bitcast.1), kind=kOutput, calls=%fused_computation.39 | convolution fusion | flops 1074266112 | bytes 4194304 | tf_op jit(solution)/shard_map/dot_general | solution.py:22
  103.4 2.9 %fusion.40 = bf16[1,512,1024]{2,1,0:T(8,128)(2,1)S(1)} fusion(bf16[1024,2048]{1,0:T(8,128)(2,1)} %bitcast.1, f32[1024,512]{1,0:T(8,128)S(1)} %copy-done.10), kind=kOutput, calls=%fused_computation.40 | convolution fusion | flops 1076887552 | bytes 5242880 | tf_op jit(solution)/shard_map/dot_general | solution.py:19
  106.4 3.2 %fusion.5 = f32[1024,512]{1,0:T(8,128)S(1)} fusion(bf16[1024,2048]{1,0:T(8,128)(2,1)} %all-gather.2.cloned.1.call-done, bf16[2,1024,512]{2,1,0:T(8,128)(2,1)} %param.10), kind=kOutput, calls=%fused_computation.19 | convolution fusion | flops 1073741824 | bytes 5242880 | tf_op jit(solution)/shard_map/dot_general | solution.py:9
  113.5 5.6 %collective-permute-start.7 = (bf16[128,512]{1,0:T(8,128)(2,1)S(1)}, bf16[128,512]{1,0:T(8,128)(2,1)S(1)}, u32[]{:S(2)}, u32[]{:S(2)}) collective-permute-start(bf16[128,512]{1,0:T(8,128)(2,1)S(1)} %dynamic-slice_bitcast_fusion), channel_id=1, source_target_pairs={{0,7},{1,0},{2,1},{3,2},{4,3},{5,4},{6,5},{7,6},{8,15},{9,8},{10,9... | collective-permute-start | bytes 393224 | tf_op jit(solution)/shard_map/ppermute | solution.py:45
  123.8 3.6 %collective-permute-start.8 = (bf16[128,512]{1,0:T(8,128)(2,1)S(1)}, bf16[128,512]{1,0:T(8,128)(2,1)S(1)}, u32[]{:S(2)}, u32[]{:S(2)}) collective-permute-start(bf16[128,512]{1,0:T(8,128)(2,1)S(1)} %bitcast_add_fusion.6), channel_id=1, source_target_pairs={{0,7},{1,0},{2,1},{3,2},{4,3},{5,4},{6,5},{7,6},{8,15},{9,8},{10,9... | collective-permute-start | bytes 393224 | tf_op jit(solution)/shard_map/ppermute | solution.py:45
  127.6 4.8 %collective-permute-done.8 = bf16[128,512]{1,0:T(8,128)(2,1)S(1)} collective-permute-done((bf16[128,512]{1,0:T(8,128)(2,1)S(1)}, bf16[128,512]{1,0:T(8,128)(2,1)S(1)}, u32[]{:S(2)}, u32[]{:S(2)}) %collective-permute-start.8) | collective-permute-done | bytes 131104 | tf_op jit(solution)/shard_map/ppermute | solution.py:45
  132.4 3.6 %collective-permute-start.9 = (bf16[128,512]{1,0:T(8,128)(2,1)S(1)}, bf16[128,512]{1,0:T(8,128)(2,1)S(1)}, u32[]{:S(2)}, u32[]{:S(2)}) collective-permute-start(bf16[128,512]{1,0:T(8,128)(2,1)S(1)} %bitcast_add_fusion.5), channel_id=1, source_target_pairs={{0,7},{1,0},{2,1},{3,2},{4,3},{5,4},{6,5},{7,6},{8,15},{9,8},{10,9... | collective-permute-start | bytes 393224 | tf_op jit(solution)/shard_map/ppermute | solution.py:45
  136.1 4.7 %collective-permute-done.9 = bf16[128,512]{1,0:T(8,128)(2,1)S(1)} collective-permute-done((bf16[128,512]{1,0:T(8,128)(2,1)S(1)}, bf16[128,512]{1,0:T(8,128)(2,1)S(1)}, u32[]{:S(2)}, u32[]{:S(2)}) %collective-permute-start.9) | collective-permute-done | bytes 131104 | tf_op jit(solution)/shard_map/ppermute | solution.py:45
  140.8 3.6 %collective-permute-start.10 = (bf16[128,512]{1,0:T(8,128)(2,1)S(1)}, bf16[128,512]{1,0:T(8,128)(2,1)S(1)}, u32[]{:S(2)}, u32[]{:S(2)}) collective-permute-start(bf16[128,512]{1,0:T(8,128)(2,1)S(1)} %bitcast_add_fusion.4), channel_id=1, source_target_pairs={{0,7},{1,0},{2,1},{3,2},{4,3},{5,4},{6,5},{7,6},{8,15},{9,8},{10,9... | collective-permute-start | bytes 393224 | tf_op jit(solution)/shard_map/ppermute | solution.py:45
  144.5 3.9 %collective-permute-done.10 = bf16[128,512]{1,0:T(8,128)(2,1)S(1)} collective-permute-done((bf16[128,512]{1,0:T(8,128)(2,1)S(1)}, bf16[128,512]{1,0:T(8,128)(2,1)S(1)}, u32[]{:S(2)}, u32[]{:S(2)}) %collective-permute-start.10) | collective-permute-done | bytes 131104 | tf_op jit(solution)/shard_map/ppermute | solution.py:45
  148.5 3.6 %collective-permute-start.11 = (bf16[128,512]{1,0:T(8,128)(2,1)S(1)}, bf16[128,512]{1,0:T(8,128)(2,1)S(1)}, u32[]{:S(2)}, u32[]{:S(2)}) collective-permute-start(bf16[128,512]{1,0:T(8,128)(2,1)S(1)} %bitcast_add_fusion.3), channel_id=1, source_target_pairs={{0,7},{1,0},{2,1},{3,2},{4,3},{5,4},{6,5},{7,6},{8,15},{9,8},{10,9... | collective-permute-start | bytes 393224 | tf_op jit(solution)/shard_map/ppermute | solution.py:45
  154.3 3.2 %collective-permute-start.12 = (bf16[128,512]{1,0:T(8,128)(2,1)S(1)}, bf16[128,512]{1,0:T(8,128)(2,1)S(1)}, u32[]{:S(2)}, u32[]{:S(2)}) collective-permute-start(bf16[128,512]{1,0:T(8,128)(2,1)S(1)} %bitcast_add_fusion.2), channel_id=1, source_target_pairs={{0,7},{1,0},{2,1},{3,2},{4,3},{5,4},{6,5},{7,6},{8,15},{9,8},{10,9... | collective-permute-start | bytes 393224 | tf_op jit(solution)/shard_map/ppermute | solution.py:45
  159.4 3.2 %collective-permute-start.13 = (bf16[128,512]{1,0:T(8,128)(2,1)S(1)}, bf16[128,512]{1,0:T(8,128)(2,1)S(1)}, u32[]{:S(2)}, u32[]{:S(2)}) collective-permute-start(bf16[128,512]{1,0:T(8,128)(2,1)S(1)} %bitcast_add_fusion.1), channel_id=1, source_target_pairs={{0,7},{1,0},{2,1},{3,2},{4,3},{5,4},{6,5},{7,6},{8,15},{9,8},{10,9... | collective-permute-start | bytes 393224 | tf_op jit(solution)/shard_map/ppermute | solution.py:45
  163.0 2.7 %collective-permute-done.13 = bf16[128,512]{1,0:T(8,128)(2,1)S(1)} collective-permute-done((bf16[128,512]{1,0:T(8,128)(2,1)S(1)}, bf16[128,512]{1,0:T(8,128)(2,1)S(1)}, u32[]{:S(2)}, u32[]{:S(2)}) %collective-permute-start.13) | collective-permute-done | bytes 131104 | tf_op jit(solution)/shard_map/ppermute | solution.py:45
  165.7 3.6 %collective-permute-done.6 = bf16[128,512]{1,0:T(8,128)(2,1)S(1)} collective-permute-done((bf16[128,512]{1,0:T(8,128)(2,1)S(1)}, bf16[128,512]{1,0:T(8,128)(2,1)S(1)}, u32[]{:S(2)}, u32[]{:S(2)}) %collective-permute-start.6) | collective-permute-done | bytes 131104 | tf_op jit(solution)/shard_map/ppermute | solution.py:44
  171.4 13.2 %all-to-all-start.2 = ((bf16[1,128,2,32,32]{1,4,2,0,3:T(8,128)(2,1)}), bf16[1,128,2,32,32]{1,4,2,0,3:T(8,128)(2,1)S(1)}, u32[]{:S(2)}, u32[]{:S(2)}) async-start(bf16[1,128,2,32,32]{1,4,2,0,3:T(8,128)(2,1)} %copy.13), calls=%async_computation.3 | async-start | bytes 1048576 | tf_op jit(solution)/shard_map/all_to_all | solution.py:102
  184.7 3.1 %fusion.31 = bf16[1,1024,512]{2,1,0:T(8,128)(2,1)S(1)} fusion(bf16[1024,512]{1,0:T(8,128)(2,1)} %copy-done.11, bf16[1024,2048]{1,0:T(8,128)(2,1)} %all-gather.2.cloned.1.call-done), kind=kOutput, calls=%fused_computation.37 | convolution fusion | flops 1074266112 | bytes 4194304 | tf_op jit(solution)/shard_map/dot_general | solution.py:22
  190.9 5.4 %all-to-all-done.2 = bf16[1,128,2,32,32]{1,4,2,0,3:T(8,128)(2,1)S(1)} async-done(((bf16[1,128,2,32,32]{1,4,2,0,3:T(8,128)(2,1)}), bf16[1,128,2,32,32]{1,4,2,0,3:T(8,128)(2,1)S(1)}, u32[]{:S(2)}, u32[]{:S(2)}) %all-to-all-start.2) | async-done | bytes 524320 | tf_op jit(solution)/shard_map/all_to_all | solution.py:102
  (80 shorter events, 25.9 us)
Async XLA Ops:
  7.2 99.1 %all-gather.2.cloned.1.call-start = ((), (), s32[]{:S(2)}) async-start(), calls=%async_computation.5 | async-start | bytes 4718592 | tf_op jit(solution)/shard_map/all_gather | solution.py:78
  34.1 56.5 %copy-start.7 = (bf16[2,1024,512]{2,1,0:T(8,128)(2,1)S(1)}, bf16[2,1024,512]{2,1,0:T(8,128)(2,1)}, u32[]{:S(2)}) copy-start(bf16[2,1024,512]{2,1,0:T(8,128)(2,1)} %param.10) | copy-start | bytes 6291460
  34.1 56.5 %all-to-all-start = ((bf16[32,32,2048]{2,1,0:T(8,128)(2,1)}), bf16[32,32,2048]{2,1,0:T(8,128)(2,1)}, u32[]{:S(2)}, u32[]{:S(2)}) async-start(bf16[32,32,2048]{2,1,0:T(8,128)(2,1)} %bitcast.85), calls=%async_computation | async-start | bytes 8388608 | tf_op jit(solution)/shard_map/all_to_all | solution.py:80
  38.8 130.5 %reduce-scatter.2.cloned.1.call-start = ((), (), s32[]{:S(2)}) async-start(), calls=%async_computation.4 | async-start | bytes 2359296 | tf_op jit(solution)/shard_map/reduce_scatter | solution.py:98
  90.6 3.0 %copy-start.5 = (bf16[2,512,1024]{2,1,0:T(8,128)(2,1)S(1)}, bf16[2,512,1024]{2,1,0:T(8,128)(2,1)}, u32[]{:S(2)}) copy-start(bf16[2,512,1024]{2,1,0:T(8,128)(2,1)} %param.11) | copy-start | bytes 6291460
  93.6 4.1 %copy-start.9 = (f32[1024,512]{1,0:T(8,128)}, f32[1024,512]{1,0:T(8,128)S(1)}, u32[]{:S(2)}) copy-start(f32[1024,512]{1,0:T(8,128)S(1)} %fusion.13) | copy-start | bytes 6291460
  100.3 3.0 %copy-start.10 = (f32[1024,512]{1,0:T(8,128)S(1)}, f32[1024,512]{1,0:T(8,128)}, u32[]{:S(2)}) copy-start(f32[1024,512]{1,0:T(8,128)} %copy-done.9) | copy-start | bytes 6291460
  106.3 3.3 %copy-start.4 = (bf16[1024,2048]{1,0:T(8,128)(2,1)S(1)}, bf16[1024,2048]{1,0:T(8,128)(2,1)}, u32[]{:S(2)}) copy-start(bf16[1024,2048]{1,0:T(8,128)(2,1)} %all-gather.2.cloned.1.call-done) | copy-start | bytes 12582916
  106.3 3.8 %copy-start.6 = (bf16[2,512,1024]{2,1,0:T(8,128)(2,1)S(1)}, bf16[2,512,1024]{2,1,0:T(8,128)(2,1)}, u32[]{:S(2)}) copy-start(bf16[2,512,1024]{2,1,0:T(8,128)(2,1)} %param.11) | copy-start | bytes 6291460
  113.5 10.3 %collective-permute-start.7 = (bf16[128,512]{1,0:T(8,128)(2,1)S(1)}, bf16[128,512]{1,0:T(8,128)(2,1)S(1)}, u32[]{:S(2)}, u32[]{:S(2)}) collective-permute-start(bf16[128,512]{1,0:T(8,128)(2,1)S(1)} %dynamic-slice_bitcast_fusion), channel_id=1, source_target_pairs={{0,7},{1,0},{2,1},{3,2},{4,3},{5,4},{6,5},{7,6},{8,15},{9,8},{10,9... | collective-permute-start | bytes 393224 | tf_op jit(solution)/shard_map/ppermute | solution.py:45
  119.2 8.3 %collective-permute-start = (bf16[128,512]{1,0:T(8,128)(2,1)S(1)}, bf16[128,512]{1,0:T(8,128)(2,1)S(1)}, u32[]{:S(2)}, u32[]{:S(2)}) collective-permute-start(bf16[128,512]{1,0:T(8,128)(2,1)S(1)} %dynamic-slice_bitcast_fusion.1), channel_id=1, source_target_pairs={{0,1},{1,2},{2,3},{3,4},{4,5},{5,6},{6,7},{7,0},{8,9},{9,10},{10,1... | collective-permute-start | bytes 393224 | tf_op jit(solution)/shard_map/ppermute | solution.py:44
  123.8 8.6 %collective-permute-start.8 = (bf16[128,512]{1,0:T(8,128)(2,1)S(1)}, bf16[128,512]{1,0:T(8,128)(2,1)S(1)}, u32[]{:S(2)}, u32[]{:S(2)}) collective-permute-start(bf16[128,512]{1,0:T(8,128)(2,1)S(1)} %bitcast_add_fusion.6), channel_id=1, source_target_pairs={{0,7},{1,0},{2,1},{3,2},{4,3},{5,4},{6,5},{7,6},{8,15},{9,8},{10,9... | collective-permute-start | bytes 393224 | tf_op jit(solution)/shard_map/ppermute | solution.py:45
  127.5 8.6 %collective-permute-start.1 = (bf16[128,512]{1,0:T(8,128)(2,1)S(1)}, bf16[128,512]{1,0:T(8,128)(2,1)S(1)}, u32[]{:S(2)}, u32[]{:S(2)}) collective-permute-start(bf16[128,512]{1,0:T(8,128)(2,1)S(1)} %bitcast_add_fusion.13), channel_id=1, source_target_pairs={{0,1},{1,2},{2,3},{3,4},{4,5},{5,6},{6,7},{7,0},{8,9},{9,10},{10,1... | collective-permute-start | bytes 393224 | tf_op jit(solution)/shard_map/ppermute | solution.py:44
  132.4 8.4 %collective-permute-start.9 = (bf16[128,512]{1,0:T(8,128)(2,1)S(1)}, bf16[128,512]{1,0:T(8,128)(2,1)S(1)}, u32[]{:S(2)}, u32[]{:S(2)}) collective-permute-start(bf16[128,512]{1,0:T(8,128)(2,1)S(1)} %bitcast_add_fusion.5), channel_id=1, source_target_pairs={{0,7},{1,0},{2,1},{3,2},{4,3},{5,4},{6,5},{7,6},{8,15},{9,8},{10,9... | collective-permute-start | bytes 393224 | tf_op jit(solution)/shard_map/ppermute | solution.py:45
  136.0 8.4 %collective-permute-start.2 = (bf16[128,512]{1,0:T(8,128)(2,1)S(1)}, bf16[128,512]{1,0:T(8,128)(2,1)S(1)}, u32[]{:S(2)}, u32[]{:S(2)}) collective-permute-start(bf16[128,512]{1,0:T(8,128)(2,1)S(1)} %bitcast_add_fusion.12), channel_id=1, source_target_pairs={{0,1},{1,2},{2,3},{3,4},{4,5},{5,6},{6,7},{7,0},{8,9},{9,10},{10,1... | collective-permute-start | bytes 393224 | tf_op jit(solution)/shard_map/ppermute | solution.py:44
  140.8 7.7 %collective-permute-start.10 = (bf16[128,512]{1,0:T(8,128)(2,1)S(1)}, bf16[128,512]{1,0:T(8,128)(2,1)S(1)}, u32[]{:S(2)}, u32[]{:S(2)}) collective-permute-start(bf16[128,512]{1,0:T(8,128)(2,1)S(1)} %bitcast_add_fusion.4), channel_id=1, source_target_pairs={{0,7},{1,0},{2,1},{3,2},{4,3},{5,4},{6,5},{7,6},{8,15},{9,8},{10,9... | collective-permute-start | bytes 393224 | tf_op jit(solution)/shard_map/ppermute | solution.py:45
  144.4 8.1 %collective-permute-start.3 = (bf16[128,512]{1,0:T(8,128)(2,1)S(1)}, bf16[128,512]{1,0:T(8,128)(2,1)S(1)}, u32[]{:S(2)}, u32[]{:S(2)}) collective-permute-start(bf16[128,512]{1,0:T(8,128)(2,1)S(1)} %bitcast_add_fusion.11), channel_id=1, source_target_pairs={{0,1},{1,2},{2,3},{3,4},{4,5},{5,6},{6,7},{7,0},{8,9},{9,10},{10,1... | collective-permute-start | bytes 393224 | tf_op jit(solution)/shard_map/ppermute | solution.py:44
  148.5 5.7 %collective-permute-start.11 = (bf16[128,512]{1,0:T(8,128)(2,1)S(1)}, bf16[128,512]{1,0:T(8,128)(2,1)S(1)}, u32[]{:S(2)}, u32[]{:S(2)}) collective-permute-start(bf16[128,512]{1,0:T(8,128)(2,1)S(1)} %bitcast_add_fusion.3), channel_id=1, source_target_pairs={{0,7},{1,0},{2,1},{3,2},{4,3},{5,4},{6,5},{7,6},{8,15},{9,8},{10,9... | collective-permute-start | bytes 393224 | tf_op jit(solution)/shard_map/ppermute | solution.py:45
  152.6 5.1 %collective-permute-start.4 = (bf16[128,512]{1,0:T(8,128)(2,1)S(1)}, bf16[128,512]{1,0:T(8,128)(2,1)S(1)}, u32[]{:S(2)}, u32[]{:S(2)}) collective-permute-start(bf16[128,512]{1,0:T(8,128)(2,1)S(1)} %bitcast_add_fusion.10), channel_id=1, source_target_pairs={{0,1},{1,2},{2,3},{3,4},{4,5},{5,6},{6,7},{7,0},{8,9},{9,10},{10,1... | collective-permute-start | bytes 393224 | tf_op jit(solution)/shard_map/ppermute | solution.py:44
  154.3 5.1 %collective-permute-start.12 = (bf16[128,512]{1,0:T(8,128)(2,1)S(1)}, bf16[128,512]{1,0:T(8,128)(2,1)S(1)}, u32[]{:S(2)}, u32[]{:S(2)}) collective-permute-start(bf16[128,512]{1,0:T(8,128)(2,1)S(1)} %bitcast_add_fusion.2), channel_id=1, source_target_pairs={{0,7},{1,0},{2,1},{3,2},{4,3},{5,4},{6,5},{7,6},{8,15},{9,8},{10,9... | collective-permute-start | bytes 393224 | tf_op jit(solution)/shard_map/ppermute | solution.py:45
  157.7 5.1 %collective-permute-start.5 = (bf16[128,512]{1,0:T(8,128)(2,1)S(1)}, bf16[128,512]{1,0:T(8,128)(2,1)S(1)}, u32[]{:S(2)}, u32[]{:S(2)}) collective-permute-start(bf16[128,512]{1,0:T(8,128)(2,1)S(1)} %bitcast_add_fusion.9), channel_id=1, source_target_pairs={{0,1},{1,2},{2,3},{3,4},{4,5},{5,6},{6,7},{7,0},{8,9},{9,10},{10,1... | collective-permute-start | bytes 393224 | tf_op jit(solution)/shard_map/ppermute | solution.py:44
  159.4 6.2 %collective-permute-start.13 = (bf16[128,512]{1,0:T(8,128)(2,1)S(1)}, bf16[128,512]{1,0:T(8,128)(2,1)S(1)}, u32[]{:S(2)}, u32[]{:S(2)}) collective-permute-start(bf16[128,512]{1,0:T(8,128)(2,1)S(1)} %bitcast_add_fusion.1), channel_id=1, source_target_pairs={{0,7},{1,0},{2,1},{3,2},{4,3},{5,4},{6,5},{7,6},{8,15},{9,8},{10,9... | collective-permute-start | bytes 393224 | tf_op jit(solution)/shard_map/ppermute | solution.py:45
  162.9 6.4 %collective-permute-start.6 = (bf16[128,512]{1,0:T(8,128)(2,1)S(1)}, bf16[128,512]{1,0:T(8,128)(2,1)S(1)}, u32[]{:S(2)}, u32[]{:S(2)}) collective-permute-start(bf16[128,512]{1,0:T(8,128)(2,1)S(1)} %bitcast_add_fusion.8), channel_id=1, source_target_pairs={{0,1},{1,2},{2,3},{3,4},{4,5},{5,6},{6,7},{7,0},{8,9},{9,10},{10,1... | collective-permute-start | bytes 393224 | tf_op jit(solution)/shard_map/ppermute | solution.py:44
  171.4 24.9 %all-to-all-start.2 = ((bf16[1,128,2,32,32]{1,4,2,0,3:T(8,128)(2,1)}), bf16[1,128,2,32,32]{1,4,2,0,3:T(8,128)(2,1)S(1)}, u32[]{:S(2)}, u32[]{:S(2)}) async-start(bf16[1,128,2,32,32]{1,4,2,0,3:T(8,128)(2,1)} %copy.13), calls=%async_computation.3 | async-start | bytes 1048576 | tf_op jit(solution)/shard_map/all_to_all | solution.py:102
  (6 other events, 9.2 us)
Sparse Core Ops, SparseCore 0:
  30.0 57.0 all-gather.1
  106.4 47.2 reduce-scatter.1

commit v6 on v4

--- a/solution.py
+++ b/solution.py
@@ -36,7 +36,12 @@
     where_to = region_ids * capacity + slot_ids
     both = jnp.concatenate([tokens, grad_out], axis=1)
     band = 2 * model_width // splits
-    my_band = lax.dynamic_slice_in_dim(both, lax.axis_index("expert") * band, band, axis=1)
+    band_at = lax.axis_index("expert") * band
+    my_band = jnp.where(
+        band_at < model_width,
+        lax.dynamic_slice_in_dim(tokens, band_at % model_width, band, axis=1),
+        lax.dynamic_slice_in_dim(grad_out, band_at % model_width, band, axis=1),
+    )
 
     rows = jnp.arange(owners * capacity, dtype=jnp.int32)
     owner_of = rows // capacity

time: 189 us -> 188 us (level)
    unnamed x35 -> x36, local copies, waits for them, and re-layouts: 6.88 us -> 5.48 us
where the time goes in v6:
time: 188 us
  blocking collectives  74.2 us (39%)
  waiting for transfers between devices  51.3 us (27%)
  matrix products  25.4 us (14%)
  between operations  14.3 us (8%)
  local copies, waits for them, and re-layouts  9.58 us (5%)
  starting transfers between devices  7.67 us (4%)
  other arithmetic  5.4 us (3%)
    all_to_all x1, blocking collectives, on_device(): lax.all_to_all(sent_a.reshape(owners, capacity, 2 * model_width), 'dp', s...  54.2 us
    reduce_scatter x1, waiting for transfers between devices, on_device(): lax.psum_scatter(partial_value, 'expert', scatter_dimension=0, tiled=True)  45.8 us
    all_to_all x1, blocking collectives, on_device(): lax.all_to_all(sent_b.reshape(owners, capacity, band), 'dp', split_axis=0...  20.1 us
    all_to_all x1, starting transfers between devices, on_device(): lax.all_to_all(summed.reshape(1, cols, local_count, owners, capacity), 'd...  7.59 us
    dot_general x2, matrix products, expert_math(): lax.dot_general(routed_in, pre_grad, (((0,), (0,)), ((), ())), preferred_...  6.16 us
    unnamed x36, local copies, waits for them, and re-layouts  5.48 us
    all_to_all x1, waiting for transfers between devices, on_device(): lax.all_to_all(summed.reshape(1, cols, local_count, owners, capacity), 'd...  5.44 us
    dot_general x2, matrix products, expert_math(): pre_act = jnp.dot(routed_in, w_in, preferred_element_type=jnp.float32)  4.49 us
  transfers between devices with their start and end apart: 3, of which 2 were waited for; matrix products, arithmetic and copies ran while one was open for 11% of the time, Pallas kernels for 0%

profile of v6, /device:TPU:1, one launch (start us, length us, event | category | flops | bytes accessed | tf_op | source)
XLA Modules:
  0.0 187.9 jit_solution(15654896000219939251)
XLA Ops:
  7.3 2.1 %fusion.46 = bf16[1024,256]{1,0:T(8,128)(2,1)S(1)} fusion(s32[512]{0:T(512)} %param.9, s32[512]{0:T(512)} %param.8, s32[1024]{0:T(1024)S(1)} %get-tuple-element.4, s32[1024]{0:T(1024)S(1)} %get-tuple-element.3, bf16[512,1024]{1,0:T(8,128)(2,1)} %param.7, s32[]{:T(128)S(6)} %select_n.52, bf16[512,1024]{1,0:T(8,128)(2,1)} %param.6, pred[]{:T(512)S(6)} %lt.28), kind=kOutput, calls=%fused_computation.45 | convolution fusion | flops 270401536 | bytes 1060869 | tf_op jit(solution)/shard_map/dot_general | solution.py:56
  9.4 20.1 %all_to_all.33 = bf16[32,32,256]{2,1,0:T(8,128)(2,1)} all-to-all(bf16[32,32,256]{2,1,0:T(8,128)(2,1)S(1)} %bitcast.58), channel_id=1, replica_groups=mesh['dp'=32,'expert'=8] {'dp'}, dimensions={0} | all-to-all | bytes 1048576 | tf_op jit(solution)/shard_map/all_to_all | solution.py:59
  29.6 2.8 %convolution_convert_fusion = bf16[1024,2048]{1,0:T(8,128)(2,1)S(1)} fusion(bf16[512,1024]{1,0:T(8,128)(2,1)S(1)} %copy-done.11, bf16[512,1024]{1,0:T(8,128)(2,1)S(1)} %copy-done.12, s32[512]{0:T(512)S(1)} %copy-done.3, s32[512]{0:T(512)S(1)} %copy-done.4, s32[1024]{0:T(1024)S(1)} %get-tuple-element.3, s32[1024]{0:T(1024)S(1)} %fusion.87), kind=kOutput, calls=%fused_computation.2 | convolution fusion | flops 2155347968 | bytes 6303744 | tf_op jit(solution)/shard_map/dot_general | solution.py:63
  32.5 54.2 %all_to_all.34 = bf16[32,32,2048]{2,1,0:T(8,128)(2,1)S(1)} all-to-all(bf16[32,32,2048]{2,1,0:T(8,128)(2,1)S(1)} %bitcast.55), channel_id=1, replica_groups=mesh['dp'=32,'expert'=8] {'dp'}, dimensions={0} | all-to-all | bytes 8388608 | tf_op jit(solution)/shard_map/all_to_all | solution.py:64
  86.6 1.2 fusion.16
  88.8 1.0 copy-done.7
  89.8 1.8 multiply_convert_fusion.3
  91.6 1.3 convert_bitcast_fusion.1
  92.9 3.2 %fusion.8 = f32[1024,512]{1,0:T(8,128)S(1)} fusion(bf16[1024,2048]{1,0:T(8,128)(2,1)} %all-gather.2.cloned.1.call-done, bf16[2,1024,512]{2,1,0:T(8,128)(2,1)} %param.10), kind=kOutput, calls=%fused_computation.23 | convolution fusion | flops 1073741824 | bytes 5242880 | tf_op jit(solution)/shard_map/dot_general | solution.py:9
  96.7 1.8 multiply_convert_fusion.2
  98.5 1.0 copy-done.17
  99.6 1.3 convert_bitcast_fusion
  100.9 2.4 %pad_maximum_fusion = bf16[1024,2048]{1,0:T(8,128)(2,1)} fusion(bf16[1024,1024]{1,0:T(8,128)(2,1)S(1)} %convert_bitcast_fusion, bf16[1024,1024]{1,0:T(8,128)(2,1)S(1)} %convert_bitcast_fusion.1), kind=kLoop, calls=%fused_computation.1 | loop fusion | flops 8388608 | bytes 8388608 | tf_op jit(solution)/shard_map/concatenate | solution.py:79
  103.3 3.0 %fusion.40 = bf16[1,1024,512]{2,1,0:T(8,128)(2,1)S(1)} fusion(bf16[1024,512]{1,0:T(8,128)(2,1)S(1)} %multiply_convert_fusion.3, bf16[1024,2048]{1,0:T(8,128)(2,1)} %bitcast.53), kind=kOutput, calls=%fused_computation.43 | convolution fusion | flops 1074266112 | bytes 4194304 | tf_op jit(solution)/shard_map/dot_general | solution.py:22
  106.8 1.3 fusion.43
  109.6 2.3 %fusion.37 = bf16[1,512,1024]{2,1,0:T(8,128)(2,1)} fusion(bf16[1024,2048]{1,0:T(8,128)(2,1)S(1)} %copy-done.6, f32[1024,512]{1,0:T(8,128)S(1)} %copy-done.16), kind=kOutput, calls=%fused_computation.42 | convolution fusion | flops 1076887552 | bytes 5242880 | tf_op jit(solution)/shard_map/dot_general | solution.py:19
  111.9 45.8 %reduce-scatter.2.cloned.1.call-done = bf16[128,2048]{1,0:T(8,128)(2,1)} async-done(((bf16[1024,2048]{1,0:T(8,128)(2,1)}), bf16[128,2048]{1,0:T(8,128)(2,1)}) %reduce-scatter.2.cloned.1.call-update) | async-done | bytes 524304 | tf_op jit(solution)/shard_map/reduce_scatter | solution.py:81
  157.8 1.3 copy.18
  160.0 7.6 %all-to-all-start.2 = ((bf16[1,128,2,32,32]{1,4,2,0,3:T(8,128)(2,1)}), bf16[1,128,2,32,32]{1,4,2,0,3:T(8,128)(2,1)S(1)}, u32[]{:S(2)}, u32[]{:S(2)}) async-start(bf16[1,128,2,32,32]{1,4,2,0,3:T(8,128)(2,1)} %copy.19), calls=%async_computation.3 | async-start | bytes 1048576 | tf_op jit(solution)/shard_map/all_to_all | solution.py:83
  167.6 3.1 %fusion.34 = bf16[1,1024,512]{2,1,0:T(8,128)(2,1)S(1)} fusion(bf16[1024,512]{1,0:T(8,128)(2,1)} %copy-done.17, bf16[1024,2048]{1,0:T(8,128)(2,1)} %all-gather.2.cloned.1.call-done), kind=kOutput, calls=%fused_computation.41 | convolution fusion | flops 1074266112 | bytes 4194304 | tf_op jit(solution)/shard_map/dot_general | solution.py:22
  170.7 1.5 pad_maximum_fusion.1
  172.2 1.5 pad_maximum_fusion.2
  173.7 5.4 %all-to-all-done.2 = bf16[1,128,2,32,32]{1,4,2,0,3:T(8,128)(2,1)S(1)} async-done(((bf16[1,128,2,32,32]{1,4,2,0,3:T(8,128)(2,1)}), bf16[1,128,2,32,32]{1,4,2,0,3:T(8,128)(2,1)S(1)}, u32[]{:S(2)}, u32[]{:S(2)}) %all-to-all-start.2) | async-done | bytes 524320 | tf_op jit(solution)/shard_map/all_to_all | solution.py:83
  179.2 1.9 %gather_fusion = bf16[512,128]{1,0:T(8,128)(2,1)} fusion(bf16[2048,128]{1,0:T(8,128)(2,1)S(1)} %bitcast.50, s32[1024]{0:T(1024)S(1)} %pad_clamp_fusion), kind=kCustom, calls=%fused_computation | custom fusion | bytes 264192 | tf_op jit(solution)/shard_map/gather | solution.py:91
  (44 shorter events, 4.5 us)
Async XLA Ops:
  7.2 85.7 %all-gather.2.cloned.1.call-start = ((), (), s32[]{:S(2)}) async-start(), calls=%async_computation.4 | async-start | bytes 4718592 | tf_op jit(solution)/shard_map/all_gather | solution.py:62
  7.2 22.4 %copy-start.3 = (s32[512]{0:T(512)S(1)}, s32[512]{0:T(512)}, u32[]{:S(2)}) copy-start(s32[512]{0:T(512)} %param.9) | copy-start | bytes 6148
  7.3 22.4 %copy-start.4 = (s32[512]{0:T(512)S(1)}, s32[512]{0:T(512)}, u32[]{:S(2)}) copy-start(s32[512]{0:T(512)} %param.8) | copy-start | bytes 6148
  7.3 22.3 %copy-start.11 = (bf16[512,1024]{1,0:T(8,128)(2,1)S(1)}, bf16[512,1024]{1,0:T(8,128)(2,1)}, u32[]{:S(2)}) copy-start(bf16[512,1024]{1,0:T(8,128)(2,1)} %param.7) | copy-start | bytes 3145732
  7.3 22.3 %copy-start.12 = (bf16[512,1024]{1,0:T(8,128)(2,1)S(1)}, bf16[512,1024]{1,0:T(8,128)(2,1)}, u32[]{:S(2)}) copy-start(bf16[512,1024]{1,0:T(8,128)(2,1)} %param.6) | copy-start | bytes 3145732
  29.5 128.3 %reduce-scatter.2.cloned.1.call-start = ((), (), s32[]{:S(2)}) async-start(), calls=%async_computation.5 | async-start | bytes 4718592 | tf_op jit(solution)/shard_map/reduce_scatter | solution.py:81
  32.5 54.2 %copy-start.9 = (bf16[2,1024,512]{2,1,0:T(8,128)(2,1)S(1)}, bf16[2,1024,512]{2,1,0:T(8,128)(2,1)}, u32[]{:S(2)}) copy-start(bf16[2,1024,512]{2,1,0:T(8,128)(2,1)} %param.10) | copy-start | bytes 6291460
  86.6 2.1 %copy-start = (bf16[32,32,2048]{2,1,0:T(8,128)(2,1)}, bf16[32,32,2048]{2,1,0:T(8,128)(2,1)S(1)}, u32[]{:S(2)}) copy-start(bf16[32,32,2048]{2,1,0:T(8,128)(2,1)S(1)} %all_to_all.34) | copy-start | bytes 12582916
  86.6 3.1 %copy-start.7 = (bf16[2,512,1024]{2,1,0:T(8,128)(2,1)S(1)}, bf16[2,512,1024]{2,1,0:T(8,128)(2,1)}, u32[]{:S(2)}) copy-start(bf16[2,512,1024]{2,1,0:T(8,128)(2,1)} %param.11) | copy-start | bytes 6291460
  89.8 1.8 copy-start.13
  92.9 3.3 %copy-start.5 = (bf16[1024,2048]{1,0:T(8,128)(2,1)S(1)}, bf16[1024,2048]{1,0:T(8,128)(2,1)}, u32[]{:S(2)}) copy-start(bf16[1024,2048]{1,0:T(8,128)(2,1)} %all-gather.2.cloned.1.call-done) | copy-start | bytes 12582916
  92.9 3.8 %copy-start.8 = (bf16[2,512,1024]{2,1,0:T(8,128)(2,1)S(1)}, bf16[2,512,1024]{2,1,0:T(8,128)(2,1)}, u32[]{:S(2)}) copy-start(bf16[2,512,1024]{2,1,0:T(8,128)(2,1)} %param.11) | copy-start | bytes 6291460
  96.7 1.8 copy-start.15
  96.7 2.9 %copy-start.10 = (bf16[2,1024,512]{2,1,0:T(8,128)(2,1)S(1)}, bf16[2,1024,512]{2,1,0:T(8,128)(2,1)}, u32[]{:S(2)}) copy-start(bf16[2,1024,512]{2,1,0:T(8,128)(2,1)} %param.10) | copy-start | bytes 6291460
  98.5 1.0 copy-start.17
  103.3 3.1 %copy-start.1 = (bf16[32,32,2048]{2,1,0:T(8,128)(2,1)S(1)}, bf16[32,32,2048]{2,1,0:T(8,128)(2,1)}, u32[]{:S(2)}) copy-start(bf16[32,32,2048]{2,1,0:T(8,128)(2,1)} %copy-done) | copy-start | bytes 12582916
  103.3 3.5 %copy-start.14 = (f32[1024,512]{1,0:T(8,128)S(1)}, f32[1024,512]{1,0:T(8,128)}, u32[]{:S(2)}) copy-start(f32[1024,512]{1,0:T(8,128)} %copy-done.13) | copy-start | bytes 6291460
  106.8 2.2 %copy-start.6 = (bf16[1024,2048]{1,0:T(8,128)(2,1)S(1)}, bf16[1024,2048]{1,0:T(8,128)(2,1)}, u32[]{:S(2)}) copy-start(bf16[1024,2048]{1,0:T(8,128)(2,1)} %all-gather.2.cloned.1.call-done) | copy-start | bytes 12582916
  106.8 2.9 %copy-start.16 = (f32[1024,512]{1,0:T(8,128)S(1)}, f32[1024,512]{1,0:T(8,128)}, u32[]{:S(2)}) copy-start(f32[1024,512]{1,0:T(8,128)} %copy-done.15) | copy-start | bytes 6291460
  160.0 19.2 %all-to-all-start.2 = ((bf16[1,128,2,32,32]{1,4,2,0,3:T(8,128)(2,1)}), bf16[1,128,2,32,32]{1,4,2,0,3:T(8,128)(2,1)S(1)}, u32[]{:S(2)}, u32[]{:S(2)}) async-start(bf16[1,128,2,32,32]{1,4,2,0,3:T(8,128)(2,1)} %copy.19), calls=%async_computation.3 | async-start | bytes 1048576 | tf_op jit(solution)/shard_map/all_to_all | solution.py:83
  170.7 1.5 copy-start.2
Sparse Core Ops, SparseCore 0:
  29.7 57.1 all-gather.1
  103.4 54.3 reduce-scatter.1

commit v7 on v6

--- a/solution.py
+++ b/solution.py
@@ -76,8 +76,12 @@
                 got[:, :model_width], got[:, model_width:], weight_in[local], weight_out[local]
             )
         )
-    partial_value = jnp.concatenate([o[0] for o in outs], axis=1)
-    partial_value = with_layout_constraint(partial_value, Layout(major_to_minor=(0, 1)))
+    rows_major = Layout(major_to_minor=(0, 1))
+    rows_each = outs[0][0].shape[1]
+    partial_value = jnp.concatenate([outs[0][0], jnp.zeros_like(outs[1][0])], axis=1)
+    partial_value = lax.optimization_barrier(with_layout_constraint(partial_value, rows_major))
+    partial_value = lax.dynamic_update_slice_in_dim(partial_value, outs[1][0], rows_each, axis=1)
+    partial_value = with_layout_constraint(partial_value, rows_major)
     summed = lax.psum_scatter(partial_value, "expert", scatter_dimension=0, tiled=True)
     cols = summed.shape[0]
     back_rows = lax.all_to_all(

time: 188 us -> 189 us (level)
  other arithmetic: 5.4 us -> 3.03 us
  local copies, waits for them, and re-layouts: 9.58 us -> 11.5 us
    concatenate x0 -> x1, local copies, waits for them, and re-layouts: none -> 2.45 us  [on_device(): jnp.concatenate([outs[0][0], jnp.zeros_like(outs[1][0])], axis=1)]
    concatenate x1 -> x0, other arithmetic: 2.37 us -> none  [on_device(): partial_value = jnp.concatenate([o[0] for o in outs], axis=1)]
    unnamed x36 -> x34, local copies, waits for them, and re-layouts: 5.48 us -> 4.93 us
  transfers between devices with their start and end apart: 3 -> 3, of which waited for: 2 -> 2; matrix products, arithmetic and copies ran while one was open for 11% -> 12% of each run, Pallas kernels for 0% -> 0%
where the time goes in v7:
time: 189 us
  blocking collectives  74.2 us (39%)
  waiting for transfers between devices  51.3 us (27%)
  matrix products  26.8 us (14%)
  between operations  14.3 us (8%)
  local copies, waits for them, and re-layouts  11.5 us (6%)
  starting transfers between devices  7.68 us (4%)
  other arithmetic  3.03 us (2%)
    all_to_all x1, blocking collectives, on_device(): lax.all_to_all(sent_a.reshape(owners, capacity, 2 * model_width), 'dp', s...  54.2 us
    reduce_scatter x1, waiting for transfers between devices, on_device(): lax.psum_scatter(partial_value, 'expert', scatter_dimension=0, tiled=True)  45.9 us
    all_to_all x1, blocking collectives, on_device(): lax.all_to_all(sent_b.reshape(owners, capacity, band), 'dp', split_axis=0...  20.1 us
    all_to_all x1, starting transfers between devices, on_device(): lax.all_to_all(summed.reshape(1, cols, local_count, owners, capacity), 'd...  7.6 us
    dot_general x2, matrix products, expert_math(): lax.dot_general(routed_in, pre_grad, (((0,), (0,)), ((), ())), preferred_...  6.15 us
    all_to_all x1, waiting for transfers between devices, on_device(): lax.all_to_all(summed.reshape(1, cols, local_count, owners, capacity), 'd...  5.43 us
    unnamed x34, local copies, waits for them, and re-layouts  4.93 us
    dot_general x2, matrix products, expert_math(): pre_act = jnp.dot(routed_in, w_in, preferred_element_type=jnp.float32)  4.49 us
  transfers between devices with their start and end apart: 3, of which 2 were waited for; matrix products, arithmetic and copies ran while one was open for 12% of the time, Pallas kernels for 0%

profile of v7, /device:TPU:1, one launch (start us, length us, event | category | flops | bytes accessed | tf_op | source)
XLA Modules:
  0.0 188.9 jit_solution(14371149161331755247)
XLA Ops:
  7.3 2.1 %fusion.46 = bf16[1024,256]{1,0:T(8,128)(2,1)S(1)} fusion(s32[512]{0:T(512)} %param.9, s32[512]{0:T(512)} %param.8, s32[1024]{0:T(1024)S(1)} %broadcast_add_fusion, s32[1024]{0:T(1024)S(1)} %get-tuple-element.3, bf16[512,1024]{1,0:T(8,128)(2,1)} %param.7, s32[]{:T(128)S(6)} %select_n.52, bf16[512,1024]{1,0:T(8,128)(2,1)} %param.6, pred[]{:T(512)S(6)} %lt.28), kind=kOutput, calls=%fused_computation.44 | convolution fusion | flops 270401536 | bytes 1060869 | tf_op jit(solution)/shard_map/dot_general | solution.py:56
  9.4 20.1 %all_to_all.33 = bf16[32,32,256]{2,1,0:T(8,128)(2,1)} all-to-all(bf16[32,32,256]{2,1,0:T(8,128)(2,1)S(1)} %bitcast.58), channel_id=1, replica_groups=mesh['dp'=32,'expert'=8] {'dp'}, dimensions={0} | all-to-all | bytes 1048576 | tf_op jit(solution)/shard_map/all_to_all | solution.py:59
  29.6 2.9 %convolution_convert_fusion = bf16[1024,2048]{1,0:T(8,128)(2,1)S(1)} fusion(bf16[512,1024]{1,0:T(8,128)(2,1)S(1)} %copy-done.10, bf16[512,1024]{1,0:T(8,128)(2,1)S(1)} %copy-done.11, s32[512]{0:T(512)S(1)} %copy-done.3, s32[512]{0:T(512)S(1)} %copy-done.4, s32[1024]{0:T(1024)S(1)} %get-tuple-element.3, s32[1024]{0:T(1024)S(1)} %get-tuple-element.4), kind=kOutput, calls=%fused_computation.1 | convolution fusion | flops 2155347968 | bytes 6303744 | tf_op jit(solution)/shard_map/dot_general | solution.py:63
  32.5 54.2 %all_to_all.34 = bf16[32,32,2048]{2,1,0:T(8,128)(2,1)S(1)} all-to-all(bf16[32,32,2048]{2,1,0:T(8,128)(2,1)S(1)} %bitcast.55), channel_id=1, replica_groups=mesh['dp'=32,'expert'=8] {'dp'}, dimensions={0} | all-to-all | bytes 8388608 | tf_op jit(solution)/shard_map/all_to_all | solution.py:64
  86.7 1.2 fusion.16
  88.8 1.0 copy-done.7
  89.8 1.8 multiply_convert_fusion.3
  91.6 1.3 convert_bitcast_fusion
  92.9 2.5 %concatenate.7 = bf16[1024,2048]{1,0:T(8,128)(2,1)} pad(bf16[1024,1024]{1,0:T(8,128)(2,1)S(1)} %convert_bitcast_fusion, bf16[]{:T(256)} %constant.59.clone.1), padding=0_0x0_1024 | pad | bytes 6291458 | tf_op jit(solution)/shard_map/concatenate | solution.py:81
  95.4 3.2 %fusion.8 = f32[1024,512]{1,0:T(8,128)S(1)} fusion(bf16[1024,2048]{1,0:T(8,128)(2,1)} %all-gather.2.cloned.1.call-done, bf16[2,1024,512]{2,1,0:T(8,128)(2,1)} %param.10), kind=kOutput, calls=%fused_computation.22 | convolution fusion | flops 1073741824 | bytes 5242880 | tf_op jit(solution)/shard_map/dot_general | solution.py:9
  98.7 1.8 multiply_convert_fusion.2
  100.5 1.0 copy-done.16
  101.5 2.7 %bitcast_dynamic-update-slice_fusion = bf16[1024,2048]{1,0:T(8,128)(2,1)} fusion(bf16[1024,2048]{1,0:T(8,128)(2,1)} %concatenate.7, bf16[1024,512]{1,0:T(8,128)(2,1)S(1)} %multiply_convert_fusion.2, bf16[2,1024,512]{2,1,0:T(8,128)(2,1)S(1)} %copy-done.9), kind=kOutput, calls=%fused_computation.9 | convolution fusion | flops 1074790400 | bytes 4194304 | tf_op jit(solution)/shard_map/dot_general | solution.py:15
  104.3 3.0 %fusion.40 = bf16[1,1024,512]{2,1,0:T(8,128)(2,1)S(1)} fusion(bf16[1024,512]{1,0:T(8,128)(2,1)S(1)} %multiply_convert_fusion.3, bf16[1024,2048]{1,0:T(8,128)(2,1)} %bitcast.53), kind=kOutput, calls=%fused_computation.42 | convolution fusion | flops 1074266112 | bytes 4194304 | tf_op jit(solution)/shard_map/dot_general | solution.py:22
  107.7 1.3 fusion.43
  110.6 2.3 %fusion.37 = bf16[1,512,1024]{2,1,0:T(8,128)(2,1)} fusion(bf16[1024,2048]{1,0:T(8,128)(2,1)S(1)} %copy-done.6, f32[1024,512]{1,0:T(8,128)S(1)} %copy-done.15), kind=kOutput, calls=%fused_computation.41 | convolution fusion | flops 1076887552 | bytes 5242880 | tf_op jit(solution)/shard_map/dot_general | solution.py:19
  112.9 45.9 %reduce-scatter.2.cloned.1.call-done = bf16[128,2048]{1,0:T(8,128)(2,1)} async-done(((bf16[1024,2048]{1,0:T(8,128)(2,1)}), bf16[128,2048]{1,0:T(8,128)(2,1)}) %reduce-scatter.2.cloned.1.call-update) | async-done | bytes 524304 | tf_op jit(solution)/shard_map/reduce_scatter | solution.py:85
  158.7 1.3 copy.18
  160.9 7.6 %all-to-all-start.2 = ((bf16[1,128,2,32,32]{1,4,2,0,3:T(8,128)(2,1)}), bf16[1,128,2,32,32]{1,4,2,0,3:T(8,128)(2,1)S(1)}, u32[]{:S(2)}, u32[]{:S(2)}) async-start(bf16[1,128,2,32,32]{1,4,2,0,3:T(8,128)(2,1)} %copy.19), calls=%async_computation.3 | async-start | bytes 1048576 | tf_op jit(solution)/shard_map/all_to_all | solution.py:87
  168.6 3.1 %fusion.34 = bf16[1,1024,512]{2,1,0:T(8,128)(2,1)S(1)} fusion(bf16[1024,512]{1,0:T(8,128)(2,1)} %copy-done.16, bf16[1024,2048]{1,0:T(8,128)(2,1)} %all-gather.2.cloned.1.call-done), kind=kOutput, calls=%fused_computation.40 | convolution fusion | flops 1074266112 | bytes 4194304 | tf_op jit(solution)/shard_map/dot_general | solution.py:22
  171.7 1.5 pad_maximum_fusion
  173.2 1.5 pad_maximum_fusion.1
  174.7 5.4 %all-to-all-done.2 = bf16[1,128,2,32,32]{1,4,2,0,3:T(8,128)(2,1)S(1)} async-done(((bf16[1,128,2,32,32]{1,4,2,0,3:T(8,128)(2,1)}), bf16[1,128,2,32,32]{1,4,2,0,3:T(8,128)(2,1)S(1)}, u32[]{:S(2)}, u32[]{:S(2)}) %all-to-all-start.2) | async-done | bytes 524320 | tf_op jit(solution)/shard_map/all_to_all | solution.py:87
  180.2 1.9 %gather_fusion = bf16[512,128]{1,0:T(8,128)(2,1)} fusion(bf16[2048,128]{1,0:T(8,128)(2,1)S(1)} %bitcast.50, s32[1024]{0:T(1024)S(1)} %pad_clamp_fusion), kind=kCustom, calls=%fused_computation | custom fusion | bytes 264192 | tf_op jit(solution)/shard_map/gather | solution.py:95
  (42 shorter events, 3.9 us)
Async XLA Ops:
  7.2 88.2 %all-gather.2.cloned.1.call-start = ((), (), s32[]{:S(2)}) async-start(), calls=%async_computation.4 | async-start | bytes 4718592 | tf_op jit(solution)/shard_map/all_gather | solution.py:62
  7.3 22.3 %copy-start.3 = (s32[512]{0:T(512)S(1)}, s32[512]{0:T(512)}, u32[]{:S(2)}) copy-start(s32[512]{0:T(512)} %param.9) | copy-start | bytes 6148
  7.3 22.3 %copy-start.4 = (s32[512]{0:T(512)S(1)}, s32[512]{0:T(512)}, u32[]{:S(2)}) copy-start(s32[512]{0:T(512)} %param.8) | copy-start | bytes 6148
  7.3 22.3 %copy-start.10 = (bf16[512,1024]{1,0:T(8,128)(2,1)S(1)}, bf16[512,1024]{1,0:T(8,128)(2,1)}, u32[]{:S(2)}) copy-start(bf16[512,1024]{1,0:T(8,128)(2,1)} %param.7) | copy-start | bytes 3145732
  7.3 22.3 %copy-start.11 = (bf16[512,1024]{1,0:T(8,128)(2,1)S(1)}, bf16[512,1024]{1,0:T(8,128)(2,1)}, u32[]{:S(2)}) copy-start(bf16[512,1024]{1,0:T(8,128)(2,1)} %param.6) | copy-start | bytes 3145732
  29.5 129.2 %reduce-scatter.2.cloned.1.call-start = ((), (), s32[]{:S(2)}) async-start(), calls=%async_computation.5 | async-start | bytes 4718592 | tf_op jit(solution)/shard_map/reduce_scatter | solution.py:85
  32.5 54.2 %copy-start.8 = (bf16[2,1024,512]{2,1,0:T(8,128)(2,1)S(1)}, bf16[2,1024,512]{2,1,0:T(8,128)(2,1)}, u32[]{:S(2)}) copy-start(bf16[2,1024,512]{2,1,0:T(8,128)(2,1)} %param.10) | copy-start | bytes 6291460
  86.7 2.1 %copy-start = (bf16[32,32,2048]{2,1,0:T(8,128)(2,1)}, bf16[32,32,2048]{2,1,0:T(8,128)(2,1)S(1)}, u32[]{:S(2)}) copy-start(bf16[32,32,2048]{2,1,0:T(8,128)(2,1)S(1)} %all_to_all.34) | copy-start | bytes 12582916
  86.7 3.1 %copy-start.7 = (bf16[2,512,1024]{2,1,0:T(8,128)(2,1)S(1)}, bf16[2,512,1024]{2,1,0:T(8,128)(2,1)}, u32[]{:S(2)}) copy-start(bf16[2,512,1024]{2,1,0:T(8,128)(2,1)} %param.11) | copy-start | bytes 6291460
  89.8 1.8 copy-start.12
  95.4 3.3 %copy-start.5 = (bf16[1024,2048]{1,0:T(8,128)(2,1)S(1)}, bf16[1024,2048]{1,0:T(8,128)(2,1)}, u32[]{:S(2)}) copy-start(bf16[1024,2048]{1,0:T(8,128)(2,1)} %all-gather.2.cloned.1.call-done) | copy-start | bytes 12582916
  98.6 1.8 copy-start.14
  98.7 2.9 %copy-start.9 = (bf16[2,1024,512]{2,1,0:T(8,128)(2,1)S(1)}, bf16[2,1024,512]{2,1,0:T(8,128)(2,1)}, u32[]{:S(2)}) copy-start(bf16[2,1024,512]{2,1,0:T(8,128)(2,1)} %param.10) | copy-start | bytes 6291460
  100.5 1.0 copy-start.16
  104.2 3.1 %copy-start.1 = (bf16[32,32,2048]{2,1,0:T(8,128)(2,1)S(1)}, bf16[32,32,2048]{2,1,0:T(8,128)(2,1)}, u32[]{:S(2)}) copy-start(bf16[32,32,2048]{2,1,0:T(8,128)(2,1)} %copy-done) | copy-start | bytes 12582916
  104.2 3.5 %copy-start.13 = (f32[1024,512]{1,0:T(8,128)S(1)}, f32[1024,512]{1,0:T(8,128)}, u32[]{:S(2)}) copy-start(f32[1024,512]{1,0:T(8,128)} %copy-done.12) | copy-start | bytes 6291460
  107.7 2.2 %copy-start.6 = (bf16[1024,2048]{1,0:T(8,128)(2,1)S(1)}, bf16[1024,2048]{1,0:T(8,128)(2,1)}, u32[]{:S(2)}) copy-start(bf16[1024,2048]{1,0:T(8,128)(2,1)} %all-gather.2.cloned.1.call-done) | copy-start | bytes 12582916
  107.7 2.9 %copy-start.15 = (f32[1024,512]{1,0:T(8,128)S(1)}, f32[1024,512]{1,0:T(8,128)}, u32[]{:S(2)}) copy-start(f32[1024,512]{1,0:T(8,128)} %copy-done.14) | copy-start | bytes 6291460
  160.9 19.2 %all-to-all-start.2 = ((bf16[1,128,2,32,32]{1,4,2,0,3:T(8,128)(2,1)}), bf16[1,128,2,32,32]{1,4,2,0,3:T(8,128)(2,1)S(1)}, u32[]{:S(2)}, u32[]{:S(2)}) async-start(bf16[1,128,2,32,32]{1,4,2,0,3:T(8,128)(2,1)} %copy.19), calls=%async_computation.3 | async-start | bytes 1048576 | tf_op jit(solution)/shard_map/all_to_all | solution.py:87
  171.7 1.5 copy-start.2
Sparse Core Ops, SparseCore 0:
  29.7 57.1 all-gather.1
  104.3 54.3 reduce-scatter.1

commit v8 on v6

--- a/solution.py
+++ b/solution.py
@@ -87,8 +87,13 @@
         concat_axis=0,
         tiled=True,
     )
-    back_rows = jnp.transpose(back_rows[:, :, :, 0, :], (0, 2, 3, 1))
-    grad_tokens = back_rows.reshape(experts_all * capacity, cols)[where_to]
+    slots = jnp.arange(experts_all * capacity, dtype=jnp.int32)
+    take = (where_to[:, None] == slots[None, :]).astype(jnp.bfloat16)
+    take = take.reshape(tok_rows, owners, local_count, capacity)
+    grad_tokens = lax.dot_general(
+        take, back_rows[:, :, :, 0, :], (((1, 2, 3), (0, 2, 3)), ((), ())),
+        preferred_element_type=jnp.float32,
+    ).astype(jnp.bfloat16)
     grad_win = jnp.stack([o[1] for o in outs])
     grad_wout = jnp.stack([o[2] for o in outs])
     return (grad_tokens, grad_win, grad_wout)

time: 188 us -> 189 us (level)
  matrix products: 25.4 us -> 27.6 us
  local copies, waits for them, and re-layouts: 9.58 us -> 7.63 us
    dot_general x0 -> x1, matrix products: none -> 2.25 us  [on_device(): lax.dot_general(take, back_rows[:, :, :, 0, :], (((1, 2, 3), (0, 2, 3)),...]
    gather x1 -> x0, local copies, waits for them, and re-layouts: 1.91 us -> none  [on_device(): grad_tokens = back_rows.reshape(experts_all * capacity, cols)[where_to]]
where the time goes in v8:
time: 189 us; the launch traced here: 188 us
  blocking collectives  74.2 us (39%)
  waiting for transfers between devices  51.3 us (27%)
  matrix products  27.6 us (15%)
  between operations  14.3 us (8%)
  starting transfers between devices  7.7 us (4%)
  local copies, waits for them, and re-layouts  7.63 us (4%)
  other arithmetic  5.41 us (3%)
    all_to_all x1, blocking collectives, on_device(): lax.all_to_all(sent_a.reshape(owners, capacity, 2 * model_width), 'dp', s...  54.2 us
    reduce_scatter x1, waiting for transfers between devices, on_device(): lax.psum_scatter(partial_value, 'expert', scatter_dimension=0, tiled=True)  45.8 us
    all_to_all x1, blocking collectives, on_device(): lax.all_to_all(sent_b.reshape(owners, capacity, band), 'dp', split_axis=0...  20.1 us
    all_to_all x1, starting transfers between devices, on_device(): lax.all_to_all(summed.reshape(1, cols, local_count, owners, capacity), 'd...  7.62 us
    dot_general x2, matrix products, expert_math(): lax.dot_general(routed_in, pre_grad, (((0,), (0,)), ((), ())), preferred_...  6.17 us
    unnamed x36, local copies, waits for them, and re-layouts  5.46 us
    all_to_all x1, waiting for transfers between devices, on_device(): lax.all_to_all(summed.reshape(1, cols, local_count, owners, capacity), 'd...  5.43 us
    dot_general x2, matrix products, expert_math(): pre_act = jnp.dot(routed_in, w_in, preferred_element_type=jnp.float32)  4.49 us
  transfers between devices with their start and end apart: 3, of which 2 were waited for; matrix products, arithmetic and copies ran while one was open for 11% of the time, Pallas kernels for 0%

profile of v8, /device:TPU:1, one launch (start us, length us, event | category | flops | bytes accessed | tf_op | source)
XLA Modules:
  0.0 188.3 jit_solution(18002031475639223594)
XLA Ops:
  7.3 2.1 %fusion.50 = bf16[1024,256]{1,0:T(8,128)(2,1)S(1)} fusion(s32[512]{0:T(512)} %param.9, s32[512]{0:T(512)} %param.8, s32[1024]{0:T(1024)S(1)} %get-tuple-element.4, s32[1024]{0:T(1024)S(1)} %get-tuple-element.3, bf16[512,1024]{1,0:T(8,128)(2,1)} %param.7, s32[]{:T(128)S(6)} %select_n.49, bf16[512,1024]{1,0:T(8,128)(2,1)} %param.6, pred[]{:T(512)S(6)} %lt.22), kind=kOutput, calls=%fused_computation.48 | convolution fusion | flops 270401536 | bytes 1060869 | tf_op jit(solution)/shard_map/dot_general | solution.py:56
  9.4 20.1 %all_to_all.33 = bf16[32,32,256]{2,1,0:T(8,128)(2,1)} all-to-all(bf16[32,32,256]{2,1,0:T(8,128)(2,1)S(1)} %bitcast.61), channel_id=1, replica_groups=mesh['dp'=32,'expert'=8] {'dp'}, dimensions={0} | all-to-all | bytes 1048576 | tf_op jit(solution)/shard_map/all_to_all | solution.py:59
  29.6 2.8 %convolution_convert_fusion = bf16[1024,2048]{1,0:T(8,128)(2,1)S(1)} fusion(bf16[512,1024]{1,0:T(8,128)(2,1)S(1)} %copy-done.11, bf16[512,1024]{1,0:T(8,128)(2,1)S(1)} %copy-done.12, s32[512]{0:T(512)S(1)} %copy-done.3, s32[512]{0:T(512)S(1)} %copy-done.4, s32[1024]{0:T(1024)S(1)} %get-tuple-element.3, s32[1024]{0:T(1024)S(1)} %fusion.98), kind=kOutput, calls=%fused_computation.3 | convolution fusion | flops 2155347968 | bytes 6303744 | tf_op jit(solution)/shard_map/dot_general | solution.py:63
  32.5 54.2 %all_to_all.34 = bf16[32,32,2048]{2,1,0:T(8,128)(2,1)S(1)} all-to-all(bf16[32,32,2048]{2,1,0:T(8,128)(2,1)S(1)} %bitcast.58), channel_id=1, replica_groups=mesh['dp'=32,'expert'=8] {'dp'}, dimensions={0} | all-to-all | bytes 8388608 | tf_op jit(solution)/shard_map/all_to_all | solution.py:64
  86.6 1.2 fusion.20
  88.8 1.0 copy-done.7
  89.8 1.8 multiply_convert_fusion.3
  91.6 1.3 convert_bitcast_fusion.1
  92.9 3.2 %fusion.12 = f32[1024,512]{1,0:T(8,128)S(1)} fusion(bf16[1024,2048]{1,0:T(8,128)(2,1)} %all-gather.2.cloned.1.call-done, bf16[2,1024,512]{2,1,0:T(8,128)(2,1)} %param.10), kind=kOutput, calls=%fused_computation.26 | convolution fusion | flops 1073741824 | bytes 5242880 | tf_op jit(solution)/shard_map/dot_general | solution.py:9
  96.7 1.8 multiply_convert_fusion.2
  98.5 1.0 copy-done.17
  99.6 1.3 convert_bitcast_fusion
  100.9 2.4 %pad_maximum_fusion = bf16[1024,2048]{1,0:T(8,128)(2,1)} fusion(bf16[1024,1024]{1,0:T(8,128)(2,1)S(1)} %convert_bitcast_fusion, bf16[1024,1024]{1,0:T(8,128)(2,1)S(1)} %convert_bitcast_fusion.1), kind=kLoop, calls=%fused_computation | loop fusion | flops 8388608 | bytes 8388608 | tf_op jit(solution)/shard_map/concatenate | solution.py:79
  103.3 3.0 %fusion.44 = bf16[1,1024,512]{2,1,0:T(8,128)(2,1)S(1)} fusion(bf16[1024,512]{1,0:T(8,128)(2,1)S(1)} %multiply_convert_fusion.3, bf16[1024,2048]{1,0:T(8,128)(2,1)} %bitcast.56), kind=kOutput, calls=%fused_computation.46 | convolution fusion | flops 1074266112 | bytes 4194304 | tf_op jit(solution)/shard_map/dot_general | solution.py:22
  106.8 1.3 fusion.47
  109.7 2.3 %fusion.41 = bf16[1,512,1024]{2,1,0:T(8,128)(2,1)} fusion(bf16[1024,2048]{1,0:T(8,128)(2,1)S(1)} %copy-done.6, f32[1024,512]{1,0:T(8,128)S(1)} %copy-done.16), kind=kOutput, calls=%fused_computation.45 | convolution fusion | flops 1076887552 | bytes 5242880 | tf_op jit(solution)/shard_map/dot_general | solution.py:19
  111.9 45.8 %reduce-scatter.2.cloned.1.call-done = bf16[128,2048]{1,0:T(8,128)(2,1)} async-done(((bf16[1024,2048]{1,0:T(8,128)(2,1)}), bf16[128,2048]{1,0:T(8,128)(2,1)}) %reduce-scatter.2.cloned.1.call-update) | async-done | bytes 524304 | tf_op jit(solution)/shard_map/reduce_scatter | solution.py:81
  157.8 1.3 copy.18
  160.0 7.6 %all-to-all-start.2 = ((bf16[1,128,2,32,32]{1,4,2,0,3:T(8,128)(2,1)}), bf16[1,128,2,32,32]{1,4,2,0,3:T(8,128)(2,1)S(1)}, u32[]{:S(2)}, u32[]{:S(2)}) async-start(bf16[1,128,2,32,32]{1,4,2,0,3:T(8,128)(2,1)} %copy.19), calls=%async_computation.3 | async-start | bytes 1048576 | tf_op jit(solution)/shard_map/all_to_all | solution.py:83
  167.6 3.1 %fusion.38 = bf16[1,1024,512]{2,1,0:T(8,128)(2,1)S(1)} fusion(bf16[1024,512]{1,0:T(8,128)(2,1)} %copy-done.17, bf16[1024,2048]{1,0:T(8,128)(2,1)} %all-gather.2.cloned.1.call-done), kind=kOutput, calls=%fused_computation.44 | convolution fusion | flops 1074266112 | bytes 4194304 | tf_op jit(solution)/shard_map/dot_general | solution.py:22
  170.8 1.5 pad_maximum_fusion.1
  172.3 1.5 pad_maximum_fusion.2
  173.8 5.4 %all-to-all-done.2 = bf16[1,128,2,32,32]{1,4,2,0,3:T(8,128)(2,1)S(1)} async-done(((bf16[1,128,2,32,32]{1,4,2,0,3:T(8,128)(2,1)}), bf16[1,128,2,32,32]{1,4,2,0,3:T(8,128)(2,1)S(1)}, u32[]{:S(2)}, u32[]{:S(2)}) %all-to-all-start.2) | async-done | bytes 524320 | tf_op jit(solution)/shard_map/all_to_all | solution.py:83
  179.2 2.2 %fusion.54 = bf16[512,128]{1,0:T(8,128)(2,1)} fusion(s32[32,2,32]{2,1,0:T(2,128)S(1)} %multiply_add_fusion, s32[512]{0:T(512)S(1)} %multiply_add_fusion.1, bf16[1,128,2,32,32]{1,4,2,0,3:T(8,128)(2,1)S(1)} %all-to-all-done.2), kind=kOutput, calls=%fused_computation.50 | convolution fusion | flops 269549568 | bytes 665600 | tf_op jit(solution)/shard_map/dot_general | solution.py:93
  (44 shorter events, 4.5 us)
Async XLA Ops:
  7.2 85.7 %all-gather.2.cloned.1.call-start = ((), (), s32[]{:S(2)}) async-start(), calls=%async_computation.4 | async-start | bytes 4718592 | tf_op jit(solution)/shard_map/all_gather | solution.py:62
  7.2 22.4 %copy-start.3 = (s32[512]{0:T(512)S(1)}, s32[512]{0:T(512)}, u32[]{:S(2)}) copy-start(s32[512]{0:T(512)} %param.9) | copy-start | bytes 6148
  7.3 22.4 %copy-start.4 = (s32[512]{0:T(512)S(1)}, s32[512]{0:T(512)}, u32[]{:S(2)}) copy-start(s32[512]{0:T(512)} %param.8) | copy-start | bytes 6148
  7.3 22.4 %copy-start.11 = (bf16[512,1024]{1,0:T(8,128)(2,1)S(1)}, bf16[512,1024]{1,0:T(8,128)(2,1)}, u32[]{:S(2)}) copy-start(bf16[512,1024]{1,0:T(8,128)(2,1)} %param.7) | copy-start | bytes 3145732
  7.3 22.3 %copy-start.12 = (bf16[512,1024]{1,0:T(8,128)(2,1)S(1)}, bf16[512,1024]{1,0:T(8,128)(2,1)}, u32[]{:S(2)}) copy-start(bf16[512,1024]{1,0:T(8,128)(2,1)} %param.6) | copy-start | bytes 3145732
  29.5 128.3 %reduce-scatter.2.cloned.1.call-start = ((), (), s32[]{:S(2)}) async-start(), calls=%async_computation.5 | async-start | bytes 4718592 | tf_op jit(solution)/shard_map/reduce_scatter | solution.py:81
  32.5 54.2 %copy-start.9 = (bf16[2,1024,512]{2,1,0:T(8,128)(2,1)S(1)}, bf16[2,1024,512]{2,1,0:T(8,128)(2,1)}, u32[]{:S(2)}) copy-start(bf16[2,1024,512]{2,1,0:T(8,128)(2,1)} %param.10) | copy-start | bytes 6291460
  86.6 2.1 %copy-start = (bf16[32,32,2048]{2,1,0:T(8,128)(2,1)}, bf16[32,32,2048]{2,1,0:T(8,128)(2,1)S(1)}, u32[]{:S(2)}) copy-start(bf16[32,32,2048]{2,1,0:T(8,128)(2,1)S(1)} %all_to_all.34) | copy-start | bytes 12582916
  86.6 3.1 %copy-start.7 = (bf16[2,512,1024]{2,1,0:T(8,128)(2,1)S(1)}, bf16[2,512,1024]{2,1,0:T(8,128)(2,1)}, u32[]{:S(2)}) copy-start(bf16[2,512,1024]{2,1,0:T(8,128)(2,1)} %param.11) | copy-start | bytes 6291460
  89.8 1.8 copy-start.13
  92.9 3.3 %copy-start.5 = (bf16[1024,2048]{1,0:T(8,128)(2,1)S(1)}, bf16[1024,2048]{1,0:T(8,128)(2,1)}, u32[]{:S(2)}) copy-start(bf16[1024,2048]{1,0:T(8,128)(2,1)} %all-gather.2.cloned.1.call-done) | copy-start | bytes 12582916
  92.9 3.8 %copy-start.8 = (bf16[2,512,1024]{2,1,0:T(8,128)(2,1)S(1)}, bf16[2,512,1024]{2,1,0:T(8,128)(2,1)}, u32[]{:S(2)}) copy-start(bf16[2,512,1024]{2,1,0:T(8,128)(2,1)} %param.11) | copy-start | bytes 6291460
  96.7 1.8 copy-start.15
  96.7 2.9 %copy-start.10 = (bf16[2,1024,512]{2,1,0:T(8,128)(2,1)S(1)}, bf16[2,1024,512]{2,1,0:T(8,128)(2,1)}, u32[]{:S(2)}) copy-start(bf16[2,1024,512]{2,1,0:T(8,128)(2,1)} %param.10) | copy-start | bytes 6291460
  98.5 1.0 copy-start.17
  103.3 3.1 %copy-start.1 = (bf16[32,32,2048]{2,1,0:T(8,128)(2,1)S(1)}, bf16[32,32,2048]{2,1,0:T(8,128)(2,1)}, u32[]{:S(2)}) copy-start(bf16[32,32,2048]{2,1,0:T(8,128)(2,1)} %copy-done) | copy-start | bytes 12582916
  103.3 3.5 %copy-start.14 = (f32[1024,512]{1,0:T(8,128)S(1)}, f32[1024,512]{1,0:T(8,128)}, u32[]{:S(2)}) copy-start(f32[1024,512]{1,0:T(8,128)} %copy-done.13) | copy-start | bytes 6291460
  106.8 2.2 %copy-start.6 = (bf16[1024,2048]{1,0:T(8,128)(2,1)S(1)}, bf16[1024,2048]{1,0:T(8,128)(2,1)}, u32[]{:S(2)}) copy-start(bf16[1024,2048]{1,0:T(8,128)(2,1)} %all-gather.2.cloned.1.call-done) | copy-start | bytes 12582916
  106.8 2.9 %copy-start.16 = (f32[1024,512]{1,0:T(8,128)S(1)}, f32[1024,512]{1,0:T(8,128)}, u32[]{:S(2)}) copy-start(f32[1024,512]{1,0:T(8,128)} %copy-done.15) | copy-start | bytes 6291460
  160.0 19.2 %all-to-all-start.2 = ((bf16[1,128,2,32,32]{1,4,2,0,3:T(8,128)(2,1)}), bf16[1,128,2,32,32]{1,4,2,0,3:T(8,128)(2,1)S(1)}, u32[]{:S(2)}, u32[]{:S(2)}) async-start(bf16[1,128,2,32,32]{1,4,2,0,3:T(8,128)(2,1)} %copy.19), calls=%async_computation.3 | async-start | bytes 1048576 | tf_op jit(solution)/shard_map/all_to_all | solution.py:83
  170.7 1.5 copy-start.2
Sparse Core Ops, SparseCore 0:
  29.7 57.1 all-gather.1
  103.4 54.3 reduce-scatter.1

commit v9 on v4

--- a/solution.py
+++ b/solution.py
@@ -36,7 +36,9 @@
     where_to = region_ids * capacity + slot_ids
     both = jnp.concatenate([tokens, grad_out], axis=1)
     band = 2 * model_width // splits
-    my_band = lax.dynamic_slice_in_dim(both, lax.axis_index("expert") * band, band, axis=1)
+    band_at = lax.axis_index("expert") * band
+    band_tok = lax.dynamic_slice_in_dim(tokens, band_at % model_width, band, axis=1)
+    band_grad = lax.dynamic_slice_in_dim(grad_out, band_at % model_width, band, axis=1)
 
     rows = jnp.arange(owners * capacity, dtype=jnp.int32)
     owner_of = rows // capacity
@@ -48,9 +50,12 @@
             (region_ids[None, :] == expert_of[:, None]) & (slot_ids[None, :] == slot_of[:, None])
         ).astype(jnp.bfloat16)
 
-    sent_b = jnp.dot(pick_for(1), my_band, preferred_element_type=jnp.float32).astype(
-        jnp.bfloat16
-    )
+    pick_b = pick_for(1)
+    sent_b = jnp.where(
+        band_at < model_width,
+        jnp.dot(pick_b, band_tok, preferred_element_type=jnp.float32),
+        jnp.dot(pick_b, band_grad, preferred_element_type=jnp.float32),
+    ).astype(jnp.bfloat16)
     got_b = lax.all_to_all(
         sent_b.reshape(owners, capacity, band), "dp", split_axis=0, concat_axis=1, tiled=True
     )[0]

time: 189 us -> 189 us (level)
  matrix products: 24.2 us -> 26.1 us
    dot_general x1 -> x2, matrix products: 0.95 us -> 2.96 us  [the longest x1 1.98 us: on_device(): jnp.dot(pick_b, band_grad, preferred_element_type=jnp.float32)]
    unnamed x35 -> x36, local copies, waits for them, and re-layouts: 6.88 us -> 5.46 us
where the time goes in v9:
time: 189 us
  blocking collectives  74.2 us (39%)
  waiting for transfers between devices  51.3 us (27%)
  matrix products  26.1 us (14%)
  between operations  14.4 us (8%)
  local copies, waits for them, and re-layouts  9.55 us (5%)
  starting transfers between devices  7.69 us (4%)
  other arithmetic  5.46 us (3%)
    all_to_all x1, blocking collectives, on_device(): lax.all_to_all(sent_a.reshape(owners, capacity, 2 * model_width), 'dp', s...  54.2 us
    reduce_scatter x1, waiting for transfers between devices, on_device(): lax.psum_scatter(partial_value, 'expert', scatter_dimension=0, tiled=True)  45.9 us
    all_to_all x1, blocking collectives, on_device(): lax.all_to_all(sent_b.reshape(owners, capacity, band), 'dp', split_axis=0...  20.1 us
    all_to_all x1, starting transfers between devices, on_device(): lax.all_to_all(summed.reshape(1, cols, local_count, owners, capacity), 'd...  7.61 us
    dot_general x2, matrix products, expert_math(): lax.dot_general(routed_in, pre_grad, (((0,), (0,)), ((), ())), preferred_...  6.15 us
    unnamed x36, local copies, waits for them, and re-layouts  5.46 us
    all_to_all x1, waiting for transfers between devices, on_device(): lax.all_to_all(summed.reshape(1, cols, local_count, owners, capacity), 'd...  5.43 us
    dot_general x2, matrix products, expert_math(): pre_act = jnp.dot(routed_in, w_in, preferred_element_type=jnp.float32)  4.52 us
  transfers between devices with their start and end apart: 3, of which 2 were waited for; matrix products, arithmetic and copies ran while one was open for 11% of the time, Pallas kernels for 0%

profile of v9, /device:TPU:1, one launch (start us, length us, event | category | flops | bytes accessed | tf_op | source)
XLA Modules:
  0.0 188.8 jit_solution(5162744475214912904)
XLA Ops:
  7.3 2.0 %fusion.20 = bf16[1024,256]{1,0:T(8,128)(2,1)S(1)} fusion(s32[512]{0:T(512)} %param.9, s32[512]{0:T(512)} %param.8, s32[1024]{0:T(1024)S(1)} %get-tuple-element.4, s32[1024]{0:T(1024)S(1)} %get-tuple-element.3, bf16[512,1024]{1,0:T(8,128)(2,1)} %param.7, s32[]{:T(128)S(6)} %select_n.52), kind=kOutput, calls=%fused_computation.35 | convolution fusion | flops 270008320 | bytes 798724 | tf_op jit(solution)/shard_map/dot_general | solution.py:57
  9.3 1.0 fusion.47
  10.3 20.1 %all_to_all.33 = bf16[32,32,256]{2,1,0:T(8,128)(2,1)} all-to-all(bf16[32,32,256]{2,1,0:T(8,128)(2,1)S(1)} %bitcast.58), channel_id=1, replica_groups=mesh['dp'=32,'expert'=8] {'dp'}, dimensions={0} | all-to-all | bytes 1048576 | tf_op jit(solution)/shard_map/all_to_all | solution.py:59
  30.5 2.8 %convolution_convert_fusion = bf16[1024,2048]{1,0:T(8,128)(2,1)S(1)} fusion(bf16[512,1024]{1,0:T(8,128)(2,1)S(1)} %copy-done.11, bf16[512,1024]{1,0:T(8,128)(2,1)S(1)} %copy-done.12, s32[512]{0:T(512)S(1)} %copy-done.3, s32[512]{0:T(512)S(1)} %copy-done.4, s32[1024]{0:T(1024)S(1)} %get-tuple-element.3, s32[1024]{0:T(1024)S(1)} %fusion.90), kind=kOutput, calls=%fused_computation.2 | convolution fusion | flops 2155347968 | bytes 6303744 | tf_op jit(solution)/shard_map/dot_general | solution.py:63
  33.3 54.2 %all_to_all.34 = bf16[32,32,2048]{2,1,0:T(8,128)(2,1)S(1)} all-to-all(bf16[32,32,2048]{2,1,0:T(8,128)(2,1)S(1)} %bitcast.55), channel_id=1, replica_groups=mesh['dp'=32,'expert'=8] {'dp'}, dimensions={0} | all-to-all | bytes 8388608 | tf_op jit(solution)/shard_map/all_to_all | solution.py:64
  87.5 1.3 fusion.14
  90.6 1.8 multiply_convert_fusion.3
  92.4 1.3 convert_bitcast_fusion.1
  93.7 3.3 %fusion.6 = f32[1024,512]{1,0:T(8,128)S(1)} fusion(bf16[1024,2048]{1,0:T(8,128)(2,1)} %all-gather.2.cloned.1.call-done, bf16[2,1024,512]{2,1,0:T(8,128)(2,1)} %param.10), kind=kOutput, calls=%fused_computation.21 | convolution fusion | flops 1073741824 | bytes 5242880 | tf_op jit(solution)/shard_map/dot_general | solution.py:9
  97.5 1.8 multiply_convert_fusion.2
  99.3 1.0 copy-done.17
  100.3 1.3 convert_bitcast_fusion
  101.6 2.4 %pad_maximum_fusion = bf16[1024,2048]{1,0:T(8,128)(2,1)} fusion(bf16[1024,1024]{1,0:T(8,128)(2,1)S(1)} %convert_bitcast_fusion, bf16[1024,1024]{1,0:T(8,128)(2,1)S(1)} %convert_bitcast_fusion.1), kind=kLoop, calls=%fused_computation.1 | loop fusion | flops 8388608 | bytes 8388608 | tf_op jit(solution)/shard_map/concatenate | solution.py:79
  104.1 3.0 %fusion.40 = bf16[1,1024,512]{2,1,0:T(8,128)(2,1)S(1)} fusion(bf16[1024,512]{1,0:T(8,128)(2,1)S(1)} %multiply_convert_fusion.3, bf16[1024,2048]{1,0:T(8,128)(2,1)} %bitcast.53), kind=kOutput, calls=%fused_computation.43 | convolution fusion | flops 1074266112 | bytes 4194304 | tf_op jit(solution)/shard_map/dot_general | solution.py:22
  107.6 1.3 fusion.43
  110.5 2.3 %fusion.37 = bf16[1,512,1024]{2,1,0:T(8,128)(2,1)} fusion(bf16[1024,2048]{1,0:T(8,128)(2,1)S(1)} %copy-done.6, f32[1024,512]{1,0:T(8,128)S(1)} %copy-done.16), kind=kOutput, calls=%fused_computation.42 | convolution fusion | flops 1076887552 | bytes 5242880 | tf_op jit(solution)/shard_map/dot_general | solution.py:19
  112.8 45.9 %reduce-scatter.2.cloned.1.call-done = bf16[128,2048]{1,0:T(8,128)(2,1)} async-done(((bf16[1024,2048]{1,0:T(8,128)(2,1)}), bf16[128,2048]{1,0:T(8,128)(2,1)}) %reduce-scatter.2.cloned.1.call-update) | async-done | bytes 524304 | tf_op jit(solution)/shard_map/reduce_scatter | solution.py:81
  158.6 1.3 copy.18
  160.8 7.6 %all-to-all-start.2 = ((bf16[1,128,2,32,32]{1,4,2,0,3:T(8,128)(2,1)}), bf16[1,128,2,32,32]{1,4,2,0,3:T(8,128)(2,1)S(1)}, u32[]{:S(2)}, u32[]{:S(2)}) async-start(bf16[1,128,2,32,32]{1,4,2,0,3:T(8,128)(2,1)} %copy.19), calls=%async_computation.3 | async-start | bytes 1048576 | tf_op jit(solution)/shard_map/all_to_all | solution.py:83
  168.4 3.1 %fusion.34 = bf16[1,1024,512]{2,1,0:T(8,128)(2,1)S(1)} fusion(bf16[1024,512]{1,0:T(8,128)(2,1)} %copy-done.17, bf16[1024,2048]{1,0:T(8,128)(2,1)} %all-gather.2.cloned.1.call-done), kind=kOutput, calls=%fused_computation.41 | convolution fusion | flops 1074266112 | bytes 4194304 | tf_op jit(solution)/shard_map/dot_general | solution.py:22
  171.6 1.5 pad_maximum_fusion.1
  173.1 1.5 pad_maximum_fusion.2
  174.6 5.4 %all-to-all-done.2 = bf16[1,128,2,32,32]{1,4,2,0,3:T(8,128)(2,1)S(1)} async-done(((bf16[1,128,2,32,32]{1,4,2,0,3:T(8,128)(2,1)}), bf16[1,128,2,32,32]{1,4,2,0,3:T(8,128)(2,1)S(1)}, u32[]{:S(2)}, u32[]{:S(2)}) %all-to-all-start.2) | async-done | bytes 524320 | tf_op jit(solution)/shard_map/all_to_all | solution.py:83
  180.0 1.9 %gather_fusion = bf16[512,128]{1,0:T(8,128)(2,1)} fusion(bf16[2048,128]{1,0:T(8,128)(2,1)S(1)} %bitcast.50, s32[1024]{0:T(1024)S(1)} %pad_clamp_fusion), kind=kCustom, calls=%fused_computation | custom fusion | bytes 264192 | tf_op jit(solution)/shard_map/gather | solution.py:91
  (45 shorter events, 5.5 us)
Async XLA Ops:
  7.2 2.1 %copy-start.3 = (s32[512]{0:T(512)S(1)}, s32[512]{0:T(512)}, u32[]{:S(2)}) copy-start(s32[512]{0:T(512)} %param.9) | copy-start | bytes 6148
  7.2 2.1 %copy-start.4 = (s32[512]{0:T(512)S(1)}, s32[512]{0:T(512)}, u32[]{:S(2)}) copy-start(s32[512]{0:T(512)} %param.8) | copy-start | bytes 6148
  7.2 2.1 %copy-start.12 = (bf16[512,1024]{1,0:T(8,128)(2,1)S(1)}, bf16[512,1024]{1,0:T(8,128)(2,1)}, u32[]{:S(2)}) copy-start(bf16[512,1024]{1,0:T(8,128)(2,1)} %param.6) | copy-start | bytes 3145732
  7.2 86.5 %all-gather.2.cloned.1.call-start = ((), (), s32[]{:S(2)}) async-start(), calls=%async_computation.4 | async-start | bytes 4718592 | tf_op jit(solution)/shard_map/all_gather | solution.py:62
  9.3 21.2 %copy-start.11 = (bf16[512,1024]{1,0:T(8,128)(2,1)S(1)}, bf16[512,1024]{1,0:T(8,128)(2,1)}, u32[]{:S(2)}) copy-start(bf16[512,1024]{1,0:T(8,128)(2,1)} %param.7) | copy-start | bytes 3145732
  30.4 128.2 %reduce-scatter.2.cloned.1.call-start = ((), (), s32[]{:S(2)}) async-start(), calls=%async_computation.5 | async-start | bytes 4718592 | tf_op jit(solution)/shard_map/reduce_scatter | solution.py:81
  33.3 54.2 %copy-start.9 = (bf16[2,1024,512]{2,1,0:T(8,128)(2,1)S(1)}, bf16[2,1024,512]{2,1,0:T(8,128)(2,1)}, u32[]{:S(2)}) copy-start(bf16[2,1024,512]{2,1,0:T(8,128)(2,1)} %param.10) | copy-start | bytes 6291460
  87.5 2.1 %copy-start = (bf16[32,32,2048]{2,1,0:T(8,128)(2,1)}, bf16[32,32,2048]{2,1,0:T(8,128)(2,1)S(1)}, u32[]{:S(2)}) copy-start(bf16[32,32,2048]{2,1,0:T(8,128)(2,1)S(1)} %all_to_all.34) | copy-start | bytes 12582916
  87.5 3.1 %copy-start.7 = (bf16[2,512,1024]{2,1,0:T(8,128)(2,1)S(1)}, bf16[2,512,1024]{2,1,0:T(8,128)(2,1)}, u32[]{:S(2)}) copy-start(bf16[2,512,1024]{2,1,0:T(8,128)(2,1)} %param.11) | copy-start | bytes 6291460
  90.6 1.8 copy-start.13
  93.7 3.3 %copy-start.5 = (bf16[1024,2048]{1,0:T(8,128)(2,1)S(1)}, bf16[1024,2048]{1,0:T(8,128)(2,1)}, u32[]{:S(2)}) copy-start(bf16[1024,2048]{1,0:T(8,128)(2,1)} %all-gather.2.cloned.1.call-done) | copy-start | bytes 12582916
  93.7 3.8 %copy-start.8 = (bf16[2,512,1024]{2,1,0:T(8,128)(2,1)S(1)}, bf16[2,512,1024]{2,1,0:T(8,128)(2,1)}, u32[]{:S(2)}) copy-start(bf16[2,512,1024]{2,1,0:T(8,128)(2,1)} %param.11) | copy-start | bytes 6291460
  97.5 1.8 copy-start.15
  97.5 2.8 %copy-start.10 = (bf16[2,1024,512]{2,1,0:T(8,128)(2,1)S(1)}, bf16[2,1024,512]{2,1,0:T(8,128)(2,1)}, u32[]{:S(2)}) copy-start(bf16[2,1024,512]{2,1,0:T(8,128)(2,1)} %param.10) | copy-start | bytes 6291460
  99.3 1.0 copy-start.17
  104.1 3.1 %copy-start.1 = (bf16[32,32,2048]{2,1,0:T(8,128)(2,1)S(1)}, bf16[32,32,2048]{2,1,0:T(8,128)(2,1)}, u32[]{:S(2)}) copy-start(bf16[32,32,2048]{2,1,0:T(8,128)(2,1)} %copy-done) | copy-start | bytes 12582916
  104.1 3.5 %copy-start.14 = (f32[1024,512]{1,0:T(8,128)S(1)}, f32[1024,512]{1,0:T(8,128)}, u32[]{:S(2)}) copy-start(f32[1024,512]{1,0:T(8,128)} %copy-done.13) | copy-start | bytes 6291460
  107.6 2.2 %copy-start.6 = (bf16[1024,2048]{1,0:T(8,128)(2,1)S(1)}, bf16[1024,2048]{1,0:T(8,128)(2,1)}, u32[]{:S(2)}) copy-start(bf16[1024,2048]{1,0:T(8,128)(2,1)} %all-gather.2.cloned.1.call-done) | copy-start | bytes 12582916
  107.6 2.9 %copy-start.16 = (f32[1024,512]{1,0:T(8,128)S(1)}, f32[1024,512]{1,0:T(8,128)}, u32[]{:S(2)}) copy-start(f32[1024,512]{1,0:T(8,128)} %copy-done.15) | copy-start | bytes 6291460
  160.8 19.2 %all-to-all-start.2 = ((bf16[1,128,2,32,32]{1,4,2,0,3:T(8,128)(2,1)}), bf16[1,128,2,32,32]{1,4,2,0,3:T(8,128)(2,1)S(1)}, u32[]{:S(2)}, u32[]{:S(2)}) async-start(bf16[1,128,2,32,32]{1,4,2,0,3:T(8,128)(2,1)} %copy.19), calls=%async_computation.3 | async-start | bytes 1048576 | tf_op jit(solution)/shard_map/all_to_all | solution.py:83
  171.6 1.5 copy-start.2
Sparse Core Ops, SparseCore 0:
  30.5 57.1 all-gather.1
  104.2 54.3 reduce-scatter.1
